TPU v7x, 32 devices: a whole 2x2x4 slice. The times are simulated.
32 devices in a mesh: dp: 8 (over z, x), vocab: 4 (over y, core).
Axes of the slice: x: 2, y: 2, z: 4, core: 2. Of those that a mesh axis runs over, the one named last changes fastest.
Arguments:
- hidden: bfloat16 [4096, 4096], P(('dp', 'vocab')), may hold values from -6 to 6
- positions: int32 [32, 6], P(('dp', 'vocab')), may hold values from 0 to 127, as said below
- counts: int32 [32], P(('dp', 'vocab')), may hold values from 0 to 6, as said below
- targets: int32 [32, 6], P(('dp', 'vocab')), may hold values from 0 to 131071
- dense_weight: bfloat16 [4096, 4096], P('dp', 'vocab'), may hold values from -0.09375 to 0.09375
- dense_bias: float32 [4096], P('vocab'), may hold values from -3 to 3
- norm_gain: float32 [4096], P('vocab'), may hold values from 0.5 to 1.5
- norm_shift: float32 [4096], P('vocab'), may hold values from -3 to 3
- embedding: bfloat16 [131072, 4096], P(('dp', 'vocab')), as said below
- decoder_bias: float32 [131072], P(('dp', 'vocab')), may hold values from -6 to 6
Outputs:
- emb_grad: bfloat16 [131072, 4096], P(('dp', 'vocab'))
- bias_grad: float32 [131072], P(('dp', 'vocab'))
- row_loss: float32 [64], replicated
Inputs may be any that keep to these rules, and one draw needn't show every extreme that they name: Each micro-batch's counts sum to exactly 8; in every micro-batch one device has exactly 6. `positions`: A device's list holds distinct rows of its own block. `embedding`: entries lie within 302 / sqrt(4096) in magnitude.
All inputs are finite; a program needn't handle non-finite values.
Results may differ from a plain program's by a relative error of at most 0.0085.
Values may be sent and summed in bfloat16 or wider, within the bound.
No kernel may reach another device: no remote copies, remote signals or barrier semaphores. Data moves between devices by JAX's collectives and lax.ppermute only.
A program may use at most 128 MiB of HBM per device.

v0:
```python
import jax
import jax.numpy as jnp
from jax import lax
from jax.sharding import PartitionSpec as P

MEAN = 2


EPS = 1e-05


def body(
    hidden,
    positions,
    counts,
    targets,
    dense_weight,
    dense_bias,
    norm_gain,
    norm_shift,
    embedding,
    decoder_bias,
):
    ways = lax.axis_size("vocab")
    groups = lax.axis_size("dp")
    model = hidden.shape[1]
    slots = positions.shape[1]
    group_rows = MEAN * ways
    total_rows = groups * group_rows
    picked = jnp.take(hidden, positions[0], axis=0)
    listed_rows, listed_tgt, listed_counts = (
        lax.all_gather(picked, "vocab", axis=0, tiled=True),
        lax.all_gather(targets[0], "vocab", axis=0, tiled=True),
        lax.all_gather(counts, "vocab", axis=0, tiled=True),
    )
    slot_ids = jnp.tile(jnp.arange(slots, dtype=jnp.int32), ways)
    count_of = jnp.repeat(listed_counts, slots)
    start_of = jnp.repeat(jnp.cumsum(listed_counts) - listed_counts, slots)
    valid = slot_ids < count_of
    dest = start_of + slot_ids
    chooser = (dest[None, :] == jnp.arange(group_rows, dtype=jnp.int32)[:, None]) & valid[None, :]
    rows = jnp.dot(
        chooser.astype(jnp.bfloat16), listed_rows, preferred_element_type=jnp.float32
    ).astype(jnp.bfloat16)
    tgt = jnp.sum(jnp.where(chooser, listed_tgt[None, :], 0), axis=1).astype(jnp.int32)
    act = jnp.dot(
        rows,
        lax.all_gather(dense_weight, "dp", axis=0, tiled=True),
        preferred_element_type=jnp.float32,
    )
    act = jax.nn.gelu(act + dense_bias, approximate=False)
    sums, squares = lax.psum((jnp.sum(act, axis=1), jnp.sum(act * act, axis=1)), "vocab")
    mean = sums / model
    var = squares / model - mean * mean
    head_cols = (
        (act - mean[:, None]) * lax.rsqrt(var + EPS)[:, None] * norm_gain + norm_shift
    ).astype(jnp.bfloat16)
    head_group = lax.all_gather(head_cols, "vocab", axis=1, tiled=True)
    head_all, tgt_all = (
        lax.all_gather(head_group, "dp", axis=0, tiled=True),
        lax.all_gather(tgt, "dp", axis=0, tiled=True),
    )
    vocab_rows = embedding.shape[0]
    first_id = (lax.axis_index("dp") * ways + lax.axis_index("vocab")) * vocab_rows
    ids = first_id + jnp.arange(vocab_rows, dtype=jnp.int32)
    logits = (
        jnp.einsum("rd,vd->rv", head_all, embedding, preferred_element_type=jnp.float32)
        + decoder_bias[None, :]
    )
    hit = tgt_all[:, None] == ids[None, :]
    row_max = jnp.max(logits, axis=1)
    row_tgt = jnp.sum(jnp.where(hit, logits, 0.0), axis=1)
    peak = lax.pmax(row_max, ("dp", "vocab"))
    denom, target_logit = lax.psum(
        (jnp.sum(jnp.exp(logits - peak[:, None]), axis=1), row_tgt), ("dp", "vocab")
    )
    lse = peak + jnp.log(denom)
    row_loss = lse - target_logit
    diff = jnp.exp(logits - lse[:, None]) - hit.astype(jnp.float32)
    grad = (diff / total_rows).astype(jnp.bfloat16)
    emb_grad = jnp.einsum("rv,rd->vd", grad, head_all, preferred_element_type=jnp.float32).astype(
        jnp.bfloat16
    )
    bias_grad = jnp.sum(diff, axis=0) / total_rows
    return (emb_grad, bias_grad, row_loss)


def solution(mesh):
    return jax.shard_map(
        body,
        mesh=mesh,
        in_specs=(
            P(("dp", "vocab"), None),
            P(("dp", "vocab"), None),
            P(("dp", "vocab")),
            P(("dp", "vocab"), None),
            P("dp", "vocab"),
            P("vocab"),
            P("vocab"),
            P("vocab"),
            P(("dp", "vocab"), None),
            P(("dp", "vocab")),
        ),
        out_specs=(P(("dp", "vocab"), None), P(("dp", "vocab")), P()),
        check_vma=False,
    )
```

profile of v0, /device:TPU:0, one launch (start us, length us, event | category | flops | bytes accessed | tf_op | source)
XLA Modules:
  0.0 342.2 jit_solution(2646844981046583333)
XLA Ops:
  7.2 0.0 copy-start
  7.2 0.0 all-gather.4.cloned.1.call-start
  7.2 0.7 all-gather.4.cloned.1.call-update
  8.6 1.2 dynamic-slice
  10.5 0.8 bitcast_dynamic-update-slice_fusion
  11.2 0.8 dynamic-update-slice
  12.0 6.4 %all-reduce.3 = (s32[4]{0:T(128)S(1)}, s32[24]{0:T(128)S(1)}) all-reduce(s32[4]{0:T(128)S(1)} %dynamic-update-slice, s32[24]{0:T(128)S(1)} %bitcast_dynamic-update-slice_fusion), channel_id=1, replica_groups=mesh['dp'=8,'vocab'=4] {'vocab'}, use_global_device_ids=true, to_apply=%add | all-reduce | flops 28 | bytes 224
  18.4 0.2 reduce-window.9
  18.6 0.1 iota_add_fusion.1
  18.7 0.1 add.77
  18.7 0.1 iota_compare_fusion.1
  18.8 0.1 lt.26
  18.9 0.7 fusion.25
  19.6 0.0 copy-done
  19.6 0.6 gather_fusion
  20.2 0.7 compare_and_fusion
  20.8 0.1 select_bitcast_fusion
  20.9 5.8 %all-gather.1 = bf16[4,6,4096]{2,1,0:T(8,128)(2,1)S(1)} all-gather(bf16[1,6,4096]{2,1,0:T(8,128)(2,1)S(1)} %select_bitcast_fusion), channel_id=1, replica_groups=mesh['dp'=8,'vocab'=4] {'vocab'}, dimensions={0}, use_global_device_ids=true | all-gather | bytes 245760 | tf_op jit(solution)/shard_map/all_gather | solution.py:32
  26.7 0.1 reshape.123
  26.7 1.2 dynamic-slice.2
  28.6 0.1 select_reduce_fusion
  28.8 0.2 dynamic-update-slice.2
  29.0 13.1 %all-reduce.2 = s32[64]{0:T(128)S(1)} all-reduce(s32[64]{0:T(128)S(1)} %dynamic-update-slice.2), channel_id=1, replica_groups=mesh['dp'=8,'vocab'=4] {'dp'}, use_global_device_ids=true, to_apply=%add.2 | all-reduce | flops 64 | bytes 512
  42.2 95.4 %all-gather.4.cloned.1.call-done = bf16[4096,1024]{1,0:T(8,128)(2,1)} async-done(((bf16[512,1024]{1,0:T(8,128)(2,1)}), bf16[4096,1024]{1,0:T(8,128)(2,1)}) %all-gather.4.cloned.1.call-update) | async-done | bytes 8388624 | tf_op jit(solution)/shard_map/all_gather | solution.py:48
  137.6 4.9 %fusion.27 = (f32[8]{0:T(128)S(1)}, f32[8]{0:T(128)S(1)}, f32[8,1024]{1,0:T(8,128)S(1)}) fusion(f32[1024]{0:T(1024)} %param.15, bf16[4096,1024]{1,0:T(8,128)(2,1)} %all-gather.4.cloned.1.call-done, bf16[24,4096]{1,0:T(8,128)(2,1)S(1)} %reshape.123, s32[24]{0:T(128)S(1)} %add.77, pred[24]{0:T(512)(128)(4,1)S(1)} %lt.26), kind=kOutput, calls=%fused_computation.58 | convolution fusion | flops 69271920 | bytes 8622264 | tf_op jit(solution)/shard_map/dot_general | solution.py:46
  142.4 5.9 %all-reduce.4 = (f32[8]{0:T(128)S(1)}, f32[8]{0:T(128)S(1)}) all-reduce(f32[8]{0:T(128)S(1)} %get-tuple-element.6, f32[8]{0:T(128)S(1)} %get-tuple-element.5), channel_id=1, replica_groups=mesh['dp'=8,'vocab'=4] {'vocab'}, use_global_device_ids=true, to_apply=%region_4.5 | all-reduce | flops 16 | bytes 128 | tf_op jit(solution)/shard_map/psum | solution.py:52
  148.3 0.8 add_convert_fusion
  149.1 5.2 %all_gather.24 = bf16[8,4096]{1,0:T(8,128)(2,1)S(1)} all-gather(bf16[8,1024]{1,0:T(8,128)(2,1)S(1)} %add_convert_fusion), channel_id=1, replica_groups=mesh['dp'=8,'vocab'=4] {'vocab'}, dimensions={1}, use_global_device_ids=true | all-gather | bytes 81920 | tf_op jit(solution)/shard_map/all_gather | solution.py:58
  154.3 31.5 %all_gather.25 = bf16[64,4096]{1,0:T(8,128)(2,1)S(1)} all-gather(bf16[8,4096]{1,0:T(8,128)(2,1)S(1)} %all_gather.24), channel_id=1, replica_groups=mesh['dp'=8,'vocab'=4] {'dp'}, dimensions={0}, use_global_device_ids=true | all-gather | bytes 589824 | tf_op jit(solution)/shard_map/all_gather | solution.py:60
  185.8 15.7 %fusion.30 = (f32[64]{0:T(128)S(1)}, f32[64,4096]{1,0:T(8,128)S(1)}) fusion(f32[4096]{0:T(1024)} %param.19, bf16[64,4096]{1,0:T(8,128)(2,1)S(1)} %all_gather.25, bf16[4096,4096]{1,0:T(8,128)(2,1)} %param.18), kind=kOutput, calls=%fused_computation.59 | convolution fusion | flops 2148007936 | bytes 35143936 | tf_op jit(solution)/shard_map/rd,vd->rv/dot_general | solution.py:67
  201.5 36.8 %pmax.7 = f32[64]{0:T(128)S(1)} all-reduce(f32[64]{0:T(128)S(1)} %get-tuple-element.14), channel_id=1, replica_groups=mesh['dp'=8,'vocab'=4] {'dp','vocab'}, use_global_device_ids=true, to_apply=%region_6.7 | all-reduce | flops 64 | bytes 512 | tf_op jit(solution)/shard_map/pmax | solution.py:73
  238.3 0.3 exponential_reduce_fusion
  238.6 42.3 %psum.30 = f32[64]{0:T(128)S(1)} all-reduce(f32[64]{0:T(128)S(1)} %exponential_reduce_fusion), channel_id=1, replica_groups=mesh['dp'=8,'vocab'=4] {'dp','vocab'}, use_global_device_ids=true, to_apply=%region_8.9 | all-reduce | flops 64 | bytes 512 | tf_op jit(solution)/shard_map/psum | solution.py:74
  281.0 14.5 %convolution_convert_fusion = bf16[4096,4096]{1,0:T(8,128)(2,1)} fusion(bf16[64,4096]{1,0:T(8,128)(2,1)S(1)} %all_gather.25, f32[64,4096]{1,0:T(8,128)S(1)} %get-tuple-element.15, s32[4096]{0:T(1024)S(1)} %iota_add_fusion, f32[64]{0:T(128)S(1)} %log_add_fusion, s32[64]{0:T(128)S(1)} %all-reduce.2), kind=kOutput, calls=%fused_computation.1 | convolution fusion | flops 2165833728 | bytes 35144192 | tf_op jit(solution)/shard_map/rv,rd->vd/dot_general | solution.py:81
  295.4 0.5 fusion.3
  295.9 38.4 %psum.31 = f32[64]{0:T(128)S(1)} all-reduce(f32[64]{0:T(128)S(1)} %get-tuple-element.3), channel_id=1, replica_groups=mesh['dp'=8,'vocab'=4] {'dp','vocab'}, use_global_device_ids=true, to_apply=%region_12.13 | all-reduce | flops 64 | bytes 512 | tf_op jit(solution)/shard_map/psum | solution.py:74
  334.3 0.5 sub.45
  334.8 0.6 broadcast_multiply_fusion
  (8 shorter events, 0.0 us)
Async XLA Ops:
  7.2 12.4 %copy-start = (bf16[128,4096]{1,0:T(8,128)(2,1)S(1)}, bf16[128,4096]{1,0:T(8,128)(2,1)}, u32[]{:S(2)}) copy-start(bf16[128,4096]{1,0:T(8,128)(2,1)} %param.10) | copy-start | bytes 3145732
  7.2 130.4 %all-gather.4.cloned.1.call-start = ((), (), s32[]{:S(2)}) async-start(), calls=%async_computation | async-start | bytes 9437184 | tf_op jit(solution)/shard_map/all_gather | solution.py:48
Sparse Core Ops, SparseCore 0:
  10.1 127.4 all-gather.3
where the time goes:
time: 343 us; the launch traced here: 342 us
  blocking collectives  185 us (54%)
  waiting for transfers between devices  96.1 us (28%)
  matrix products  35 us (10%)
  between operations  16 us (5%)
  local copies, waits for them, and re-layouts  5.07 us (1%)
  other arithmetic  4.6 us (1%)
    all_gather x1, waiting for transfers between devices, body(): lax.all_gather(dense_weight, 'dp', axis=0, tiled=True)  95.4 us
    psum x2, blocking collectives, body(): lax.psum((jnp.sum(jnp.exp(logits - peak[:, None]), axis=1), row_tgt), ('d...  80.7 us
    pmax x1, blocking collectives, body(): peak = lax.pmax(row_max, ('dp', 'vocab'))  36.8 us
    all_gather x1, blocking collectives, body(): lax.all_gather(head_group, 'dp', axis=0, tiled=True)  31.5 us
    unnamed x2, blocking collectives  19.6 us
    dot_general x1, matrix products, body(): jnp.einsum('rd,vd->rv', head_all, embedding, preferred_element_type=jnp.f...  15.7 us
    dot_general x1, matrix products, body(): jnp.einsum('rv,rd->vd', grad, head_all, preferred_element_type=jnp.float32)  14.5 us
  transfers between devices with their start and end apart: 1, of which 1 were waited for; matrix products, arithmetic and copies ran while one was open for 2% of the time, Pallas kernels for 0%

commit v1 on v0

--- a/solution.py
+++ b/solution.py
@@ -7,6 +7,58 @@
 
 
 EPS = 1e-05
+
+
+def _pow2(n):
+    return n & (n - 1) == 0
+
+
+def _canon(axis, step, mine, theirs):
+    upper = (lax.axis_index(axis) & step) != 0
+    return jnp.where(upper, theirs, mine), jnp.where(upper, mine, theirs)
+
+
+def _allreduce(x, axis, n, merge):
+    step = 1
+    while step < n:
+        theirs = lax.ppermute(x, axis, [(a, a ^ step) for a in range(n)])
+        lo, hi = _canon(axis, step, x, theirs)
+        x = merge(lo, hi)
+        step *= 2
+    return x
+
+
+def _allgather(x, axis, n):
+    buf = x[None]
+    step = 1
+    while step < n:
+        theirs = lax.ppermute(buf, axis, [(a, a ^ step) for a in range(n)])
+        upper = (lax.axis_index(axis) & step) != 0
+        buf = jnp.where(upper, jnp.concatenate([theirs, buf]), jnp.concatenate([buf, theirs]))
+        step *= 2
+    return buf
+
+
+def _add(lo, hi):
+    return lo + hi
+
+
+def _psum(x, axis, n):
+    if _pow2(n):
+        return _allreduce(x, axis, n, _add)
+    return lax.psum(x, axis)
+
+
+def _gather(x, axis, n):
+    if _pow2(n):
+        return _allgather(x, axis, n)
+    return lax.all_gather(x, axis, axis=0, tiled=False)
+
+
+def _softmax_merge(lo, hi):
+    peak = jnp.maximum(lo[0], hi[0])
+    total = lo[1] * jnp.exp(lo[0] - peak) + hi[1] * jnp.exp(hi[0] - peak)
+    return jnp.stack([peak, total, lo[2] + hi[2]])
 
 
 def body(
@@ -27,12 +79,14 @@
     slots = positions.shape[1]
     group_rows = MEAN * ways
     total_rows = groups * group_rows
+    in_block = dense_weight.shape[0]
     picked = jnp.take(hidden, positions[0], axis=0)
-    listed_rows, listed_tgt, listed_counts = (
-        lax.all_gather(picked, "vocab", axis=0, tiled=True),
-        lax.all_gather(targets[0], "vocab", axis=0, tiled=True),
-        lax.all_gather(counts, "vocab", axis=0, tiled=True),
+    listed_rows = lax.all_gather(picked, "vocab", axis=0, tiled=True)
+    listed_ints = lax.all_gather(
+        jnp.concatenate([counts, targets[0]]), "vocab", axis=0, tiled=False
     )
+    listed_counts = listed_ints[:, 0]
+    listed_tgt = listed_ints[:, 1:].reshape(-1)
     slot_ids = jnp.tile(jnp.arange(slots, dtype=jnp.int32), ways)
     count_of = jnp.repeat(listed_counts, slots)
     start_of = jnp.repeat(jnp.cumsum(listed_counts) - listed_counts, slots)
@@ -43,23 +97,19 @@
         chooser.astype(jnp.bfloat16), listed_rows, preferred_element_type=jnp.float32
     ).astype(jnp.bfloat16)
     tgt = jnp.sum(jnp.where(chooser, listed_tgt[None, :], 0), axis=1).astype(jnp.int32)
-    act = jnp.dot(
-        rows,
-        lax.all_gather(dense_weight, "dp", axis=0, tiled=True),
-        preferred_element_type=jnp.float32,
-    )
+    blocks = rows.reshape(group_rows, groups, in_block).transpose(1, 0, 2)
+    rows_in = lax.all_to_all(blocks, "dp", 0, 0, tiled=True).reshape(total_rows, in_block)
+    tgt_all = _gather(tgt, "dp", groups).reshape(total_rows)
+    part = jnp.dot(rows_in, dense_weight, preferred_element_type=jnp.float32)
+    act = _psum(part, "dp", groups)
     act = jax.nn.gelu(act + dense_bias, approximate=False)
-    sums, squares = lax.psum((jnp.sum(act, axis=1), jnp.sum(act * act, axis=1)), "vocab")
-    mean = sums / model
-    var = squares / model - mean * mean
+    stats = _psum(jnp.stack([jnp.sum(act, axis=1), jnp.sum(act * act, axis=1)]), "vocab", ways)
+    mean = stats[0] / model
+    var = stats[1] / model - mean * mean
     head_cols = (
         (act - mean[:, None]) * lax.rsqrt(var + EPS)[:, None] * norm_gain + norm_shift
     ).astype(jnp.bfloat16)
-    head_group = lax.all_gather(head_cols, "vocab", axis=1, tiled=True)
-    head_all, tgt_all = (
-        lax.all_gather(head_group, "dp", axis=0, tiled=True),
-        lax.all_gather(tgt, "dp", axis=0, tiled=True),
-    )
+    head_all = _gather(head_cols, "vocab", ways).transpose(1, 0, 2).reshape(total_rows, model)
     vocab_rows = embedding.shape[0]
     first_id = (lax.axis_index("dp") * ways + lax.axis_index("vocab")) * vocab_rows
     ids = first_id + jnp.arange(vocab_rows, dtype=jnp.int32)
@@ -69,11 +119,21 @@
     )
     hit = tgt_all[:, None] == ids[None, :]
     row_max = jnp.max(logits, axis=1)
-    row_tgt = jnp.sum(jnp.where(hit, logits, 0.0), axis=1)
-    peak = lax.pmax(row_max, ("dp", "vocab"))
-    denom, target_logit = lax.psum(
-        (jnp.sum(jnp.exp(logits - peak[:, None]), axis=1), row_tgt), ("dp", "vocab")
+    local = jnp.stack(
+        [
+            row_max,
+            jnp.sum(jnp.exp(logits - row_max[:, None]), axis=1),
+            jnp.sum(jnp.where(hit, logits, 0.0), axis=1),
+        ]
     )
+    if _pow2(ways) and _pow2(groups):
+        merged = _allreduce(_allreduce(local, "vocab", ways, _softmax_merge), "dp", groups, _softmax_merge)
+        peak, denom, target_logit = merged[0], merged[1], merged[2]
+    else:
+        peak = lax.pmax(row_max, ("dp", "vocab"))
+        denom, target_logit = lax.psum(
+            (jnp.sum(jnp.exp(logits - peak[:, None]), axis=1), local[2]), ("dp", "vocab")
+        )
     lse = peak + jnp.log(denom)
     row_loss = lse - target_logit
     diff = jnp.exp(logits - lse[:, None]) - hit.astype(jnp.float32)

time: 343 us -> 127 us (0.37)
  blocking collectives: 185 us -> 24.7 us
  waiting for transfers between devices: 96.1 us -> 49.8 us
  between operations: 16 us -> 2.21 us
  starting transfers between devices: 0.04 us -> 8.51 us
  matrix products: 35 us -> 30.6 us
    all_gather x1 -> x0, waiting for transfers between devices: 95.4 us -> none  [body(): lax.all_gather(dense_weight, 'dp', axis=0, tiled=True)]
    psum x3 -> x0, blocking collectives: 86.5 us -> none  [the longest x2 80.7 us: body(): lax.psum((jnp.sum(jnp.exp(logits - peak[:, None]), axis=1), row_tgt), ('d...]
    ppermute x0 -> x15, waiting for transfers between devices: none -> 49.8 us  [the longest x10 40.1 us: _allreduce(): theirs = lax.ppermute(x, axis, [(a, a ^ step) for a in range(n)])]
    pmax x1 -> x0, blocking collectives: 36.8 us -> none  [body(): peak = lax.pmax(row_max, ('dp', 'vocab'))]
    all_gather x3 -> x1, blocking collectives: 42.5 us -> 5.76 us  [body(): listed_rows = lax.all_gather(picked, 'vocab', axis=0, tiled=True)]
    unnamed x2 -> x1, blocking collectives: 19.6 us -> 6.41 us
    all_to_all x0 -> x1, blocking collectives: none -> 12.5 us  [body(): lax.all_to_all(blocks, 'dp', 0, 0, tiled=True).reshape(total_rows, in_block)]
    ppermute x0 -> x15, starting transfers between devices: none -> 8.51 us  [the longest x10 6.34 us: _allreduce(): theirs = lax.ppermute(x, axis, [(a, a ^ step) for a in range(n)])]
  transfers between devices with their start and end apart: 1 -> 15, of which waited for: 1 -> 13; matrix products, arithmetic and copies ran while one was open for 2% -> 0% of each run, Pallas kernels for 0% -> 0%
where the time goes in v1:
time: 127 us
  waiting for transfers between devices  49.8 us (39%)
  matrix products  30.6 us (24%)
  blocking collectives  24.7 us (19%)
  starting transfers between devices  8.51 us (7%)
  other arithmetic  7.29 us (6%)
  local copies, waits for them, and re-layouts  3.96 us (3%)
  between operations  2.21 us (2%)
    ppermute x10, waiting for transfers between devices, _allreduce(): theirs = lax.ppermute(x, axis, [(a, a ^ step) for a in range(n)])  40.1 us
    dot_general x1, matrix products, body(): jnp.einsum('rd,vd->rv', head_all, embedding, preferred_element_type=jnp.f...  15.7 us
    dot_general x1, matrix products, body(): jnp.einsum('rv,rd->vd', grad, head_all, preferred_element_type=jnp.float32)  14.5 us
    all_to_all x1, blocking collectives, body(): lax.all_to_all(blocks, 'dp', 0, 0, tiled=True).reshape(total_rows, in_block)  12.5 us
    ppermute x5, waiting for transfers between devices, _allgather(): theirs = lax.ppermute(buf, axis, [(a, a ^ step) for a in range(n)])  9.64 us
    unnamed x1, blocking collectives  6.41 us
    ppermute x10, starting transfers between devices, _allreduce(): theirs = lax.ppermute(x, axis, [(a, a ^ step) for a in range(n)])  6.34 us
    all_gather x1, blocking collectives, body(): listed_rows = lax.all_gather(picked, 'vocab', axis=0, tiled=True)  5.76 us
  transfers between devices with their start and end apart: 15, of which 13 were waited for; matrix products, arithmetic and copies ran while one was open for 0% of the time, Pallas kernels for 0%

profile of v1, /device:TPU:0, one launch (start us, length us, event | category | flops | bytes accessed | tf_op | source)
XLA Modules:
  0.0 127.0 jit_solution(10257022733557772699)
XLA Ops:
  0.6 0.0 copy-start
  0.7 0.7 fusion.24
  1.4 0.7 compare_and_fusion
  2.7 1.2 dynamic-slice
  4.6 0.8 add_dynamic-update-slice_fusion
  5.5 6.4 %all-reduce = s32[28]{0:T(128)S(1)} all-reduce(s32[28]{0:T(128)S(1)} %add_dynamic-update-slice_fusion), channel_id=2, replica_groups=mesh['dp'=8,'vocab'=4] {'vocab'}, use_global_device_ids=true, to_apply=%add | all-reduce | flops 28 | bytes 224
  11.9 0.1 reshape.179
  11.9 0.1 slice_reduce_fusion
  12.1 0.1 reduce
  12.2 0.1 iota_compare_fusion.1
  12.3 0.1 iota_add_fusion.1
  12.4 0.1 add.140
  12.5 0.1 lt.26
  12.6 2.0 %gather_fusion = bf16[6,4096]{1,0:T(8,128)(2,1)S(1)} fusion(bf16[128,4096]{1,0:T(8,128)(2,1)} %param.10, s32[1024]{0:T(1024)S(1)} %pad_clamp_fusion), kind=kCustom, calls=%fused_computation | custom fusion | bytes 98328 | tf_op jit(solution)/shard_map/jit(_take)/gather | solution.py:83
  14.5 0.1 select_bitcast_fusion
  14.6 5.8 %all-gather.1 = bf16[4,6,4096]{2,1,0:T(8,128)(2,1)S(1)} all-gather(bf16[1,6,4096]{2,1,0:T(8,128)(2,1)S(1)} %select_bitcast_fusion), channel_id=1, replica_groups=mesh['dp'=8,'vocab'=4] {'vocab'}, dimensions={0}, use_global_device_ids=true | all-gather | bytes 245760 | tf_op jit(solution)/shard_map/all_gather | solution.py:84
  20.4 0.1 reshape.184
  20.5 0.2 convolution_convert_fusion.1
  20.6 12.5 %all_to_all.5 = bf16[8,8,512]{2,1,0:T(8,128)(2,1)S(1)} all-to-all(bf16[8,8,512]{2,1,0:T(8,128)(2,1)S(1)} %bitcast.80), channel_id=1, replica_groups=mesh['dp'=8,'vocab'=4] {'dp'}, dimensions={0} | all-to-all | bytes 131072 | tf_op jit(solution)/shard_map/all_to_all | solution.py:101
  33.1 0.0 copy-done
  33.1 0.3 fusion.18
  33.4 0.5 collective-permute-start
  33.9 6.7 %collective-permute-done = f32[64,1024]{1,0:T(8,128)S(1)} collective-permute-done((f32[64,1024]{1,0:T(8,128)S(1)}, f32[64,1024]{1,0:T(8,128)S(1)}, u32[]{:S(2)}, u32[]{:S(2)}) %collective-permute-start) | collective-permute-done | bytes 262176 | tf_op jit(solution)/shard_map/ppermute | solution.py:24
  40.7 0.3 collective-permute-start.1
  41.0 6.2 %collective-permute-done.1 = f32[64,1024]{1,0:T(8,128)S(1)} collective-permute-done((f32[64,1024]{1,0:T(8,128)S(1)}, f32[64,1024]{1,0:T(8,128)S(1)}, u32[]{:S(2)}, u32[]{:S(2)}) %collective-permute-start.1) | collective-permute-done | bytes 262176 | tf_op jit(solution)/shard_map/ppermute | solution.py:24
  47.1 0.6 collective-permute-start.2
  47.7 10.8 %collective-permute-done.2 = f32[64,1024]{1,0:T(8,128)S(1)} collective-permute-done((f32[64,1024]{1,0:T(8,128)S(1)}, f32[64,1024]{1,0:T(8,128)S(1)}, u32[]{:S(2)}, u32[]{:S(2)}) %collective-permute-start.2) | collective-permute-done | bytes 262176 | tf_op jit(solution)/shard_map/ppermute | solution.py:24
  58.6 1.4 %fusion.34 = (f32[64]{0:T(128)S(1)}, f32[64]{0:T(128)S(1)}, f32[64,1024]{1,0:T(8,128)S(1)}) fusion(f32[1024]{0:T(1024)} %param.15, f32[64,1024]{1,0:T(8,128)S(1)} %select_add_fusion, f32[64,1024]{1,0:T(8,128)S(1)} %collective-permute-done.2, pred[]{:T(512)S(6)} %ne.12), kind=kLoop, calls=%fused_computation.110 | loop fusion | flops 4652928 | bytes 791041 | tf_op jit(solution)/shard_map/reduce_sum | solution.py:106
  60.0 0.1 collective-permute-start.3
  60.1 1.1 collective-permute-done.3
  61.2 0.9 collective-permute-start.4
  62.2 0.1 slice.115
  62.2 0.1 broadcast_in_dim.57
  62.3 2.6 %collective-permute-done.4 = f32[2,64]{1,0:T(2,128)S(1)} collective-permute-done((f32[2,64]{1,0:T(2,128)S(1)}, f32[2,64]{1,0:T(2,128)S(1)}, u32[]{:S(2)}, u32[]{:S(2)}) %collective-permute-start.4) | collective-permute-done | bytes 544 | tf_op jit(solution)/shard_map/ppermute | solution.py:24
  64.9 0.8 fusion.17
  65.7 0.1 collective-permute-start.5
  65.8 0.1 select_reduce_fusion
  65.9 1.0 collective-permute-start.7
  67.0 2.6 %collective-permute-done.7 = s32[1,8]{1,0:T(1,128)S(1)} collective-permute-done((s32[1,8]{1,0:T(1,128)S(1)}, s32[1,8]{1,0:T(1,128)S(1)}, u32[]{:S(2)}, u32[]{:S(2)}) %collective-permute-start.7) | collective-permute-done | bytes 64 | tf_op jit(solution)/shard_map/ppermute | solution.py:35
  69.6 0.1 collective-permute-start.8
  69.6 0.0 collective-permute-done.5
  69.7 0.9 collective-permute-start.6
  70.6 2.6 %collective-permute-done.8 = s32[2,8]{1,0:T(2,128)S(1)} collective-permute-done((s32[2,8]{1,0:T(2,128)S(1)}, s32[2,8]{1,0:T(2,128)S(1)}, u32[]{:S(2)}, u32[]{:S(2)}) %collective-permute-start.8) | collective-permute-done | bytes 96 | tf_op jit(solution)/shard_map/ppermute | solution.py:35
  73.2 0.1 collective-permute-start.9
  73.3 4.5 %collective-permute-done.9 = s32[4,8]{1,0:T(4,128)S(1)} collective-permute-done((s32[4,8]{1,0:T(4,128)S(1)}, s32[4,8]{1,0:T(4,128)S(1)}, u32[]{:S(2)}, u32[]{:S(2)}) %collective-permute-start.9) | collective-permute-done | bytes 160 | tf_op jit(solution)/shard_map/ppermute | solution.py:35
  77.8 0.1 select_n.215
  77.9 0.0 collective-permute-done.6
  77.9 0.1 fusion.3
  78.0 15.7 %fusion.37 = (f32[64]{0:T(128)S(1)}, f32[64,4096]{1,0:T(8,128)S(1)}) fusion(f32[4096]{0:T(1024)} %param.19, bf16[64,4096]{1,0:T(8,128)(2,1)S(1)} %bitcast.78, bf16[4096,4096]{1,0:T(8,128)(2,1)} %param.18), kind=kOutput, calls=%fused_computation.111 | convolution fusion | flops 2148007936 | bytes 35143936 | tf_op jit(solution)/shard_map/rd,vd->rv/dot_general | solution.py:117
  93.7 0.4 exponential_reduce_fusion
  94.2 0.1 collective-permute-start.10
  94.2 1.1 collective-permute-done.10
  95.4 0.9 collective-permute-start.11
  96.3 2.7 %collective-permute-done.11 = f32[3,64]{1,0:T(4,128)S(1)} collective-permute-done((f32[3,64]{1,0:T(4,128)S(1)}, f32[3,64]{1,0:T(4,128)S(1)}, u32[]{:S(2)}, u32[]{:S(2)}) %collective-permute-start.11) | collective-permute-done | bytes 800 | tf_op jit(solution)/shard_map/ppermute | solution.py:24
  99.1 1.0 collective-permute-start.12
  100.2 2.6 %collective-permute-done.12 = f32[3,64]{1,0:T(4,128)S(1)} collective-permute-done((f32[3,64]{1,0:T(4,128)S(1)}, f32[3,64]{1,0:T(4,128)S(1)}, u32[]{:S(2)}, u32[]{:S(2)}) %collective-permute-start.12) | collective-permute-done | bytes 800 | tf_op jit(solution)/shard_map/ppermute | solution.py:24
  102.8 1.2 collective-permute-start.13
  104.1 2.4 %collective-permute-done.13 = f32[3,64]{1,0:T(4,128)S(1)} collective-permute-done((f32[3,64]{1,0:T(4,128)S(1)}, f32[3,64]{1,0:T(4,128)S(1)}, u32[]{:S(2)}, u32[]{:S(2)}) %collective-permute-start.13) | collective-permute-done | bytes 800 | tf_op jit(solution)/shard_map/ppermute | solution.py:24
  106.5 0.8 collective-permute-start.14
  107.3 3.8 %collective-permute-done.14 = f32[3,64]{1,0:T(4,128)S(1)} collective-permute-done((f32[3,64]{1,0:T(4,128)S(1)}, f32[3,64]{1,0:T(4,128)S(1)}, u32[]{:S(2)}, u32[]{:S(2)}) %collective-permute-start.14) | collective-permute-done | bytes 800 | tf_op jit(solution)/shard_map/ppermute | solution.py:24
  111.1 0.5 bitcast_subtract_fusion
  111.6 14.5 %convolution_convert_fusion = bf16[4096,4096]{1,0:T(8,128)(2,1)} fusion(bf16[64,4096]{1,0:T(8,128)(2,1)S(1)} %bitcast.79, f32[64,4096]{1,0:T(8,128)S(1)} %get-tuple-element.35, f32[64]{0:T(128)S(1)} %get-tuple-element.8, s32[4096]{0:T(1024)S(1)} %iota_add_fusion, s32[64]{0:T(128)S(1)} %select_n.215), kind=kOutput, calls=%fused_computation.1 | convolution fusion | flops 2165833728 | bytes 35144192 | tf_op jit(solution)/shard_map/rv,rd->vd/dot_general | solution.py:141
  126.1 0.3 fusion.2
  126.4 0.6 broadcast_multiply_fusion
  (31 shorter events, 0.4 us)
Async XLA Ops:
  0.6 32.5 %copy-start = (bf16[512,1024]{1,0:T(8,128)(2,1)S(1)}, bf16[512,1024]{1,0:T(8,128)(2,1)}, u32[]{:S(2)}) copy-start(bf16[512,1024]{1,0:T(8,128)(2,1)} %param.14) | copy-start | bytes 3145732
  33.4 7.2 %collective-permute-start = (f32[64,1024]{1,0:T(8,128)S(1)}, f32[64,1024]{1,0:T(8,128)S(1)}, u32[]{:S(2)}, u32[]{:S(2)}) collective-permute-start(f32[64,1024]{1,0:T(8,128)S(1)} %fusion.18), channel_id=1, source_target_pairs={{0,4},{4,0},{8,12},{12,8},{16,20},{20,16},{24,28},{28,24},{1,5},{5... | collective-permute-start | bytes 786440 | tf_op jit(solution)/shard_map/ppermute | solution.py:24
  40.7 6.4 %collective-permute-start.1 = (f32[64,1024]{1,0:T(8,128)S(1)}, f32[64,1024]{1,0:T(8,128)S(1)}, u32[]{:S(2)}, u32[]{:S(2)}) collective-permute-start(f32[64,1024]{1,0:T(8,128)S(1)} %select_add_fusion.1), channel_id=1, source_target_pairs={{0,8},{4,12},{8,0},{12,4},{16,24},{20,28},{24,16},{28,20},{1,9},{5... | collective-permute-start | bytes 786440 | tf_op jit(solution)/shard_map/ppermute | solution.py:24
  47.1 11.4 %collective-permute-start.2 = (f32[64,1024]{1,0:T(8,128)S(1)}, f32[64,1024]{1,0:T(8,128)S(1)}, u32[]{:S(2)}, u32[]{:S(2)}) collective-permute-start(f32[64,1024]{1,0:T(8,128)S(1)} %select_add_fusion), channel_id=1, source_target_pairs={{0,16},{4,20},{8,24},{12,28},{16,0},{20,4},{24,8},{28,12},{1,17},{... | collective-permute-start | bytes 786440 | tf_op jit(solution)/shard_map/ppermute | solution.py:24
  60.0 1.2 collective-permute-start.3
  61.2 3.6 %collective-permute-start.4 = (f32[2,64]{1,0:T(2,128)S(1)}, f32[2,64]{1,0:T(2,128)S(1)}, u32[]{:S(2)}, u32[]{:S(2)}) collective-permute-start(f32[2,64]{1,0:T(2,128)S(1)} %select_add_fusion.3), channel_id=1, source_target_pairs={{0,2},{1,3},{2,0},{3,1},{4,6},{5,7},{6,4},{7,5},{8,10},{9,11},{10,... | collective-permute-start | bytes 1544 | tf_op jit(solution)/shard_map/ppermute | solution.py:24
  65.7 3.9 %collective-permute-start.5 = (bf16[1,64,1024]{2,1,0:T(8,128)(2,1)S(1)}, bf16[1,64,1024]{2,1,0:T(8,128)(2,1)S(1)}, u32[]{:S(2)}, u32[]{:S(2)}) collective-permute-start(bf16[1,64,1024]{2,1,0:T(8,128)(2,1)S(1)} %fusion.17), channel_id=1, source_target_pairs={{0,1},{1,0},{2,3},{3,2},{4,5},{5,4},{6,7},{7,6},{8,9},{9,8},{10,11... | collective-permute-start | bytes 393224 | tf_op jit(solution)/shard_map/ppermute | solution.py:35
  65.9 3.6 %collective-permute-start.7 = (s32[1,8]{1,0:T(1,128)S(1)}, s32[1,8]{1,0:T(1,128)S(1)}, u32[]{:S(2)}, u32[]{:S(2)}) collective-permute-start(s32[1,8]{1,0:T(1,128)S(1)} %bitcast.93), channel_id=1, source_target_pairs={{0,4},{4,0},{8,12},{12,8},{16,20},{20,16},{24,28},{28,24},{1,5},{5... | collective-permute-start | bytes 104 | tf_op jit(solution)/shard_map/ppermute | solution.py:35
  69.6 3.6 %collective-permute-start.8 = (s32[2,8]{1,0:T(2,128)S(1)}, s32[2,8]{1,0:T(2,128)S(1)}, u32[]{:S(2)}, u32[]{:S(2)}) collective-permute-start(s32[2,8]{1,0:T(2,128)S(1)} %add_select_fusion.2), channel_id=1, source_target_pairs={{0,8},{4,12},{8,0},{12,4},{16,24},{20,28},{24,16},{28,20},{1,9},{5... | collective-permute-start | bytes 200 | tf_op jit(solution)/shard_map/ppermute | solution.py:35
  69.7 8.2 %collective-permute-start.6 = (bf16[2,64,1024]{2,1,0:T(8,128)(2,1)S(1)}, bf16[2,64,1024]{2,1,0:T(8,128)(2,1)S(1)}, u32[]{:S(2)}, u32[]{:S(2)}) collective-permute-start(bf16[2,64,1024]{2,1,0:T(8,128)(2,1)S(1)} %maximum_select_fusion.1), channel_id=1, source_target_pairs={{0,2},{1,3},{2,0},{3,1},{4,6},{5,7},{6,4},{7,5},{8,10},{9,11},{10,... | collective-permute-start | bytes 786440 | tf_op jit(solution)/shard_map/ppermute | solution.py:35
  73.2 4.5 %collective-permute-start.9 = (s32[4,8]{1,0:T(4,128)S(1)}, s32[4,8]{1,0:T(4,128)S(1)}, u32[]{:S(2)}, u32[]{:S(2)}) collective-permute-start(s32[4,8]{1,0:T(4,128)S(1)} %add_select_fusion.1), channel_id=1, source_target_pairs={{0,16},{4,20},{8,24},{12,28},{16,0},{20,4},{24,8},{28,12},{1,17},{... | collective-permute-start | bytes 392 | tf_op jit(solution)/shard_map/ppermute | solution.py:35
  94.2 1.2 collective-permute-start.10
  95.4 3.7 %collective-permute-start.11 = (f32[3,64]{1,0:T(4,128)S(1)}, f32[3,64]{1,0:T(4,128)S(1)}, u32[]{:S(2)}, u32[]{:S(2)}) collective-permute-start(f32[3,64]{1,0:T(4,128)S(1)} %pad_maximum_fusion.1), channel_id=1, source_target_pairs={{0,2},{1,3},{2,0},{3,1},{4,6},{5,7},{6,4},{7,5},{8,10},{9,11},{10,... | collective-permute-start | bytes 2312 | tf_op jit(solution)/shard_map/ppermute | solution.py:24
  99.1 3.7 %collective-permute-start.12 = (f32[3,64]{1,0:T(4,128)S(1)}, f32[3,64]{1,0:T(4,128)S(1)}, u32[]{:S(2)}, u32[]{:S(2)}) collective-permute-start(f32[3,64]{1,0:T(4,128)S(1)} %pad_maximum_fusion.2), channel_id=1, source_target_pairs={{0,4},{4,0},{8,12},{12,8},{16,20},{20,16},{24,28},{28,24},{1,5},{5... | collective-permute-start | bytes 2312 | tf_op jit(solution)/shard_map/ppermute | solution.py:24
  102.8 3.7 %collective-permute-start.13 = (f32[3,64]{1,0:T(4,128)S(1)}, f32[3,64]{1,0:T(4,128)S(1)}, u32[]{:S(2)}, u32[]{:S(2)}) collective-permute-start(f32[3,64]{1,0:T(4,128)S(1)} %pad_maximum_fusion.3), channel_id=1, source_target_pairs={{0,8},{4,12},{8,0},{12,4},{16,24},{20,28},{24,16},{28,20},{1,9},{5... | collective-permute-start | bytes 2312 | tf_op jit(solution)/shard_map/ppermute | solution.py:24
  106.5 4.5 %collective-permute-start.14 = (f32[3,64]{1,0:T(4,128)S(1)}, f32[3,64]{1,0:T(4,128)S(1)}, u32[]{:S(2)}, u32[]{:S(2)}) collective-permute-start(f32[3,64]{1,0:T(4,128)S(1)} %pad_maximum_fusion.4), channel_id=1, source_target_pairs={{0,16},{4,20},{8,24},{12,28},{16,0},{20,4},{24,8},{28,12},{1,17},{... | collective-permute-start | bytes 2312 | tf_op jit(solution)/shard_map/ppermute | solution.py:24

commit v2 on v1

--- a/solution.py
+++ b/solution.py
@@ -37,6 +37,21 @@
         buf = jnp.where(upper, jnp.concatenate([theirs, buf]), jnp.concatenate([buf, theirs]))
         step *= 2
     return buf
+
+
+def _reduce_scatter(x, axis, n):
+    idx = lax.axis_index(axis)
+    step = n // 2
+    while step >= 1:
+        halves = x.reshape((2, x.shape[0] // 2) + x.shape[1:])
+        upper = (idx & step) != 0
+        kept = jnp.where(upper, halves[1], halves[0])
+        sent = jnp.where(upper, halves[0], halves[1])
+        theirs = lax.ppermute(sent, axis, [(a, a ^ step) for a in range(n)])
+        lo, hi = _canon(axis, step, kept, theirs)
+        x = lo + hi
+        step //= 2
+    return x[0]
 
 
 def _add(lo, hi):
@@ -80,35 +95,48 @@
     group_rows = MEAN * ways
     total_rows = groups * group_rows
     in_block = dense_weight.shape[0]
-    picked = jnp.take(hidden, positions[0], axis=0)
-    listed_rows = lax.all_gather(picked, "vocab", axis=0, tiled=True)
-    listed_ints = lax.all_gather(
-        jnp.concatenate([counts, targets[0]]), "vocab", axis=0, tiled=False
-    )
-    listed_counts = listed_ints[:, 0]
-    listed_tgt = listed_ints[:, 1:].reshape(-1)
+    tokens = hidden.shape[0]
+    onehot = (positions[0][:, None] == jnp.arange(tokens, dtype=jnp.int32)[None, :]).astype(hidden.dtype)
+    picked = jnp.dot(onehot, hidden, preferred_element_type=jnp.float32).astype(hidden.dtype)
+    count_row = jnp.broadcast_to(counts.astype(hidden.dtype)[:, None], (1, model))
+    listed = lax.all_gather(jnp.concatenate([picked, count_row]), "vocab", axis=0, tiled=False)
+    listed_rows = listed[:, :slots].reshape(ways * slots, model)
+    listed_counts = listed[:, slots, 0].astype(jnp.int32)
     slot_ids = jnp.tile(jnp.arange(slots, dtype=jnp.int32), ways)
-    count_of = jnp.repeat(listed_counts, slots)
-    start_of = jnp.repeat(jnp.cumsum(listed_counts) - listed_counts, slots)
-    valid = slot_ids < count_of
-    dest = start_of + slot_ids
-    chooser = (dest[None, :] == jnp.arange(group_rows, dtype=jnp.int32)[:, None]) & valid[None, :]
+    row_ids = jnp.arange(group_rows, dtype=jnp.int32)
+
+    def choose(group_counts):
+        count_of = jnp.repeat(group_counts, slots)
+        start_of = jnp.repeat(jnp.cumsum(group_counts) - group_counts, slots)
+        valid = slot_ids < count_of
+        dest = start_of + slot_ids
+        return (dest[None, :] == row_ids[:, None]) & valid[None, :]
+
+    chooser = choose(listed_counts)
     rows = jnp.dot(
         chooser.astype(jnp.bfloat16), listed_rows, preferred_element_type=jnp.float32
     ).astype(jnp.bfloat16)
-    tgt = jnp.sum(jnp.where(chooser, listed_tgt[None, :], 0), axis=1).astype(jnp.int32)
+    ints = jnp.concatenate([counts, targets[0]])
+    all_ints = _gather(_gather(ints, "vocab", ways), "dp", groups).reshape(groups, ways, slots + 1)
+    all_choosers = jax.vmap(choose)(all_ints[:, :, 0])
+    tgt_all = jnp.sum(
+        jnp.where(all_choosers, all_ints[:, None, :, 1:].reshape(groups, 1, ways * slots), 0), axis=2
+    ).reshape(total_rows).astype(jnp.int32)
     blocks = rows.reshape(group_rows, groups, in_block).transpose(1, 0, 2)
     rows_in = lax.all_to_all(blocks, "dp", 0, 0, tiled=True).reshape(total_rows, in_block)
-    tgt_all = _gather(tgt, "dp", groups).reshape(total_rows)
     part = jnp.dot(rows_in, dense_weight, preferred_element_type=jnp.float32)
-    act = _psum(part, "dp", groups)
+    if _pow2(groups):
+        act = _reduce_scatter(part.reshape(groups, group_rows, -1), "dp", groups)
+    else:
+        act = lax.psum_scatter(part.reshape(groups, group_rows, -1), "dp", scatter_dimension=0, tiled=True)[0]
     act = jax.nn.gelu(act + dense_bias, approximate=False)
     stats = _psum(jnp.stack([jnp.sum(act, axis=1), jnp.sum(act * act, axis=1)]), "vocab", ways)
     mean = stats[0] / model
     var = stats[1] / model - mean * mean
-    head_cols = (
+    head_rows = (
         (act - mean[:, None]) * lax.rsqrt(var + EPS)[:, None] * norm_gain + norm_shift
     ).astype(jnp.bfloat16)
+    head_cols = _gather(head_rows, "dp", groups).reshape(total_rows, -1)
     head_all = _gather(head_cols, "vocab", ways).transpose(1, 0, 2).reshape(total_rows, model)
     vocab_rows = embedding.shape[0]
     first_id = (lax.axis_index("dp") * ways + lax.axis_index("vocab")) * vocab_rows

time: 127 us -> 120 us (0.945)
  blocking collectives: 24.7 us -> 7.25 us
  starting transfers between devices: 8.51 us -> 18.1 us
  waiting for transfers between devices: 49.8 us -> 53.2 us
  local copies, waits for them, and re-layouts: 3.96 us -> 1.36 us
  matrix products: 30.6 us -> 32.8 us
  other arithmetic: 7.29 us -> 5.47 us
    ppermute x10 -> x7, waiting for transfers between devices: 40.1 us -> 16.8 us  [_allreduce(): theirs = lax.ppermute(x, axis, [(a, a ^ step) for a in range(n)])]
    all_to_all x1 -> x0, blocking collectives: 12.5 us -> none  [body(): lax.all_to_all(blocks, 'dp', 0, 0, tiled=True).reshape(total_rows, in_block)]
    ppermute x0 -> x3, waiting for transfers between devices: none -> 11.6 us  [_reduce_scatter(): theirs = lax.ppermute(sent, axis, [(a, a ^ step) for a in range(n)])]
    ppermute x5 -> x10, waiting for transfers between devices: 9.64 us -> 18.7 us  [_allgather(): theirs = lax.ppermute(buf, axis, [(a, a ^ step) for a in range(n)])]
    unnamed x1 -> x0, blocking collectives: 6.41 us -> none
    all_to_all x0 -> x1, waiting for transfers between devices: none -> 6.11 us  [body(): lax.all_to_all(blocks, 'dp', 0, 0, tiled=True).reshape(total_rows, in_block)]
    all_to_all x0 -> x1, starting transfers between devices: none -> 5.81 us  [body(): lax.all_to_all(blocks, 'dp', 0, 0, tiled=True).reshape(total_rows, in_block)]
    ppermute x5 -> x10, starting transfers between devices: 2.17 us -> 5.94 us  [_allgather(): theirs = lax.ppermute(buf, axis, [(a, a ^ step) for a in range(n)])]
  transfers between devices with their start and end apart: 15 -> 21, of which waited for: 13 -> 17; matrix products, arithmetic and copies ran while one was open for 0% -> 3% of each run, Pallas kernels for 0% -> 0%
where the time goes in v2:
time: 120 us
  waiting for transfers between devices  53.2 us (44%)
  matrix products  32.8 us (27%)
  starting transfers between devices  18.1 us (15%)
  blocking collectives  7.25 us (6%)
  other arithmetic  5.47 us (5%)
  between operations  1.69 us (1%)
  local copies, waits for them, and re-layouts  1.36 us (1%)
    ppermute x10, waiting for transfers between devices, _allgather(): theirs = lax.ppermute(buf, axis, [(a, a ^ step) for a in range(n)])  18.7 us
    ppermute x7, waiting for transfers between devices, _allreduce(): theirs = lax.ppermute(x, axis, [(a, a ^ step) for a in range(n)])  16.8 us
    dot_general x1, matrix products, body(): jnp.einsum('rd,vd->rv', head_all, embedding, preferred_element_type=jnp.f...  15.7 us
    dot_general x1, matrix products, body(): jnp.einsum('rv,rd->vd', grad, head_all, preferred_element_type=jnp.float32)  14.5 us
    ppermute x3, waiting for transfers between devices, _reduce_scatter(): theirs = lax.ppermute(sent, axis, [(a, a ^ step) for a in range(n)])  11.6 us
    all_gather x1, blocking collectives, body(): lax.all_gather(jnp.concatenate([picked, count_row]), 'vocab', axis=0, til...  7.25 us
    all_to_all x1, waiting for transfers between devices, body(): lax.all_to_all(blocks, 'dp', 0, 0, tiled=True).reshape(total_rows, in_block)  6.11 us
    ppermute x10, starting transfers between devices, _allgather(): theirs = lax.ppermute(buf, axis, [(a, a ^ step) for a in range(n)])  5.94 us
  transfers between devices with their start and end apart: 21, of which 17 were waited for; matrix products, arithmetic and copies ran while one was open for 3% of the time, Pallas kernels for 0%

profile of v2, /device:TPU:0, one launch (start us, length us, event | category | flops | bytes accessed | tf_op | source)
XLA Modules:
  0.0 119.9 jit_solution(4158970002687474075)
XLA Ops:
  1.4 1.5 %convolution_convert_fusion.2 = bf16[6,4096]{1,0:T(8,128)(2,1)S(1)} fusion(bf16[128,4096]{1,0:T(8,128)(2,1)} %param.10, s32[6]{0:T(128)} %bitcast.118), kind=kOutput, calls=%fused_computation.3 | convolution fusion | flops 6316800 | bytes 1097752 | tf_op jit(solution)/shard_map/dot_general | solution.py:100
  3.0 7.3 %all-gather.1 = bf16[4,7,4096]{2,1,0:T(8,128)(2,1)S(1)} all-gather(bf16[1,7,4096]{2,1,0:T(8,128)(2,1)S(1)} %pad_bitcast_fusion), channel_id=2, replica_groups=mesh['dp'=8,'vocab'=4] {'vocab'}, dimensions={0}, use_global_device_ids=true | all-gather | bytes 286720 | tf_op jit(solution)/shard_map/all_gather | solution.py:102
  10.2 0.2 fusion.38
  10.4 0.2 reduce-window.9
  10.6 0.1 broadcast_in_dim.30
  10.6 0.1 reshape.367
  10.7 0.1 tile.22
  10.9 0.1 reshape.368
  11.1 0.8 convolution_convert_fusion.1
  11.8 5.8 %all-to-all-start = ((bf16[8,8,512]{2,1,0:T(8,128)(2,1)}), bf16[8,8,512]{2,1,0:T(8,128)(2,1)S(1)}, u32[]{:S(2)}, u32[]{:S(2)}) async-start(bf16[8,8,512]{2,1,0:T(8,128)(2,1)} %bitcast.5), calls=%async_computation | async-start | bytes 131072 | tf_op jit(solution)/shard_map/all_to_all | solution.py:126
  17.7 0.7 add_bitcast_fusion
  18.5 6.1 %all-to-all-done = bf16[8,8,512]{2,1,0:T(8,128)(2,1)S(1)} async-done(((bf16[8,8,512]{2,1,0:T(8,128)(2,1)}), bf16[8,8,512]{2,1,0:T(8,128)(2,1)S(1)}, u32[]{:S(2)}, u32[]{:S(2)}) %all-to-all-start) | async-done | bytes 65568 | tf_op jit(solution)/shard_map/all_to_all | solution.py:126
  24.6 0.3 fusion.10
  24.9 0.5 collective-permute-start
  25.5 1.6 %collective-permute-start.11 = (s32[2,7]{1,0:T(2,128)S(1)}, s32[2,7]{1,0:T(2,128)S(1)}, u32[]{:S(2)}, u32[]{:S(2)}) collective-permute-start(s32[2,7]{1,0:T(2,128)S(1)} %add_select_fusion.4), channel_id=1, source_target_pairs={{0,2},{1,3},{2,0},{3,1},{4,6},{5,7},{6,4},{7,5},{8,10},{9,11},{10,... | collective-permute-start | bytes 176 | tf_op jit(solution)/shard_map/ppermute | solution.py:35
  27.0 5.6 %collective-permute-done = f32[4,8,1024]{2,1,0:T(8,128)S(1)} collective-permute-done((f32[4,8,1024]{2,1,0:T(8,128)S(1)}, f32[4,8,1024]{2,1,0:T(8,128)S(1)}, u32[]{:S(2)}, u32[]{:S(2)}) %collective-permute-start) | collective-permute-done | bytes 131104 | tf_op jit(solution)/shard_map/ppermute | solution.py:50
  32.7 0.1 collective-permute-start.1
  32.8 4.2 %collective-permute-done.1 = f32[2,8,1024]{2,1,0:T(8,128)S(1)} collective-permute-done((f32[2,8,1024]{2,1,0:T(8,128)S(1)}, f32[2,8,1024]{2,1,0:T(8,128)S(1)}, u32[]{:S(2)}, u32[]{:S(2)}) %collective-permute-start.1) | collective-permute-done | bytes 65568 | tf_op jit(solution)/shard_map/ppermute | solution.py:50
  37.0 1.1 collective-permute-start.2
  38.1 1.1 collective-permute-start.12
  39.2 1.8 %collective-permute-done.2 = f32[1,8,1024]{2,1,0:T(8,128)S(1)} collective-permute-done((f32[1,8,1024]{2,1,0:T(8,128)S(1)}, f32[1,8,1024]{2,1,0:T(8,128)S(1)}, u32[]{:S(2)}, u32[]{:S(2)}) %collective-permute-start.2) | collective-permute-done | bytes 32800 | tf_op jit(solution)/shard_map/ppermute | solution.py:50
  41.0 0.8 fusion.20
  41.8 0.1 fusion.51
  42.0 0.1 collective-permute-start.3
  42.1 1.1 collective-permute-done.3
  43.2 1.6 %collective-permute-start.4 = (f32[2,8]{1,0:T(2,128)S(1)}, f32[2,8]{1,0:T(2,128)S(1)}, u32[]{:S(2)}, u32[]{:S(2)}) collective-permute-start(f32[2,8]{1,0:T(2,128)S(1)} %select_add_fusion.3), channel_id=1, source_target_pairs={{0,2},{1,3},{2,0},{3,1},{4,6},{5,7},{6,4},{7,5},{8,10},{9,11},{10,... | collective-permute-start | bytes 200 | tf_op jit(solution)/shard_map/ppermute | solution.py:24
  44.8 2.0 %collective-permute-done.4 = f32[2,8]{1,0:T(2,128)S(1)} collective-permute-done((f32[2,8]{1,0:T(2,128)S(1)}, f32[2,8]{1,0:T(2,128)S(1)}, u32[]{:S(2)}, u32[]{:S(2)}) %collective-permute-start.4) | collective-permute-done | bytes 96 | tf_op jit(solution)/shard_map/ppermute | solution.py:24
  46.9 0.8 fusion.18
  47.7 1.1 collective-permute-start.5
  48.8 0.1 collective-permute-start.14
  48.9 2.7 %collective-permute-done.5 = bf16[1,8,1024]{2,1,0:T(8,128)(2,1)S(1)} collective-permute-done((bf16[1,8,1024]{2,1,0:T(8,128)(2,1)S(1)}, bf16[1,8,1024]{2,1,0:T(8,128)(2,1)S(1)}, u32[]{:S(2)}, u32[]{:S(2)}) %collective-permute-start.5) | collective-permute-done | bytes 16416 | tf_op jit(solution)/shard_map/ppermute | solution.py:35
  51.6 1.8 %collective-permute-done.14 = s32[4,4,7]{2,1,0:T(4,128)S(1)} collective-permute-done((s32[4,4,7]{2,1,0:T(4,128)S(1)}, s32[4,4,7]{2,1,0:T(4,128)S(1)}, u32[]{:S(2)}, u32[]{:S(2)}) %collective-permute-start.14) | collective-permute-done | bytes 480 | tf_op jit(solution)/shard_map/ppermute | solution.py:35
  53.4 0.1 copy.28
  53.5 1.9 %collective-permute-done.6 = bf16[2,8,1024]{2,1,0:T(8,128)(2,1)S(1)} collective-permute-done((bf16[2,8,1024]{2,1,0:T(8,128)(2,1)S(1)}, bf16[2,8,1024]{2,1,0:T(8,128)(2,1)S(1)}, u32[]{:S(2)}, u32[]{:S(2)}) %collective-permute-start.6) | collective-permute-done | bytes 32800 | tf_op jit(solution)/shard_map/ppermute | solution.py:35
  55.5 0.3 collective-permute-start.7
  55.8 0.1 copy.30
  55.9 0.1 slice.199
  56.0 0.1 copy.29
  56.1 0.1 broadcast_in_dim.33
  56.2 0.1 reshape.373
  56.3 0.1 reshape.374
  56.4 0.1 broadcast_in_dim.36
  56.5 4.4 %collective-permute-done.7 = bf16[4,8,1024]{2,1,0:T(8,128)(2,1)S(1)} collective-permute-done((bf16[4,8,1024]{2,1,0:T(8,128)(2,1)S(1)}, bf16[4,8,1024]{2,1,0:T(8,128)(2,1)S(1)}, u32[]{:S(2)}, u32[]{:S(2)}) %collective-permute-start.7) | collective-permute-done | bytes 65568 | tf_op jit(solution)/shard_map/ppermute | solution.py:35
  60.9 0.1 collective-permute-start.8
  61.0 1.3 %collective-permute-done.8 = bf16[1,64,1024]{2,1,0:T(8,128)(2,1)S(1)} collective-permute-done((bf16[1,64,1024]{2,1,0:T(8,128)(2,1)S(1)}, bf16[1,64,1024]{2,1,0:T(8,128)(2,1)S(1)}, u32[]{:S(2)}, u32[]{:S(2)}) %collective-permute-start.8) | collective-permute-done | bytes 131104 | tf_op jit(solution)/shard_map/ppermute | solution.py:35
  62.3 1.6 %collective-permute-start.9 = (bf16[2,64,1024]{2,1,0:T(8,128)(2,1)S(1)}, bf16[2,64,1024]{2,1,0:T(8,128)(2,1)S(1)}, u32[]{:S(2)}, u32[]{:S(2)}) collective-permute-start(bf16[2,64,1024]{2,1,0:T(8,128)(2,1)S(1)} %maximum_select_fusion.1), channel_id=1, source_target_pairs={{0,2},{1,3},{2,0},{3,1},{4,6},{5,7},{6,4},{7,5},{8,10},{9,11},{10,... | collective-permute-start | bytes 786440 | tf_op jit(solution)/shard_map/ppermute | solution.py:35
  63.9 0.2 select_reduce_fusion
  64.1 0.1 eq.66
  64.2 6.5 %collective-permute-done.9 = bf16[2,64,1024]{2,1,0:T(8,128)(2,1)S(1)} collective-permute-done((bf16[2,64,1024]{2,1,0:T(8,128)(2,1)S(1)}, bf16[2,64,1024]{2,1,0:T(8,128)(2,1)S(1)}, u32[]{:S(2)}, u32[]{:S(2)}) %collective-permute-start.9) | collective-permute-done | bytes 262176 | tf_op jit(solution)/shard_map/ppermute | solution.py:35
  70.8 0.1 fusion.3
  70.9 15.7 %fusion.53 = (f32[64]{0:T(128)S(1)}, f32[64,4096]{1,0:T(8,128)S(1)}) fusion(f32[4096]{0:T(1024)} %param.19, bf16[64,4096]{1,0:T(8,128)(2,1)S(1)} %bitcast.98, bf16[4096,4096]{1,0:T(8,128)(2,1)} %param.18), kind=kOutput, calls=%fused_computation.146 | convolution fusion | flops 2148007936 | bytes 35143936 | tf_op jit(solution)/shard_map/rd,vd->rv/dot_general | solution.py:145
  86.6 0.4 exponential_reduce_fusion
  87.1 1.1 collective-permute-done.15
  88.3 1.6 %collective-permute-start.16 = (f32[3,64]{1,0:T(4,128)S(1)}, f32[3,64]{1,0:T(4,128)S(1)}, u32[]{:S(2)}, u32[]{:S(2)}) collective-permute-start(f32[3,64]{1,0:T(4,128)S(1)} %pad_maximum_fusion.1), channel_id=1, source_target_pairs={{0,2},{1,3},{2,0},{3,1},{4,6},{5,7},{6,4},{7,5},{8,10},{9,11},{10,... | collective-permute-start | bytes 2312 | tf_op jit(solution)/shard_map/ppermute | solution.py:24
  89.9 2.1 %collective-permute-done.16 = f32[3,64]{1,0:T(4,128)S(1)} collective-permute-done((f32[3,64]{1,0:T(4,128)S(1)}, f32[3,64]{1,0:T(4,128)S(1)}, u32[]{:S(2)}, u32[]{:S(2)}) %collective-permute-start.16) | collective-permute-done | bytes 800 | tf_op jit(solution)/shard_map/ppermute | solution.py:24
  92.0 1.1 collective-permute-start.17
  93.1 2.6 %collective-permute-done.17 = f32[3,64]{1,0:T(4,128)S(1)} collective-permute-done((f32[3,64]{1,0:T(4,128)S(1)}, f32[3,64]{1,0:T(4,128)S(1)}, u32[]{:S(2)}, u32[]{:S(2)}) %collective-permute-start.17) | collective-permute-done | bytes 800 | tf_op jit(solution)/shard_map/ppermute | solution.py:24
  95.8 3.6 %collective-permute-done.18 = f32[3,64]{1,0:T(4,128)S(1)} collective-permute-done((f32[3,64]{1,0:T(4,128)S(1)}, f32[3,64]{1,0:T(4,128)S(1)}, u32[]{:S(2)}, u32[]{:S(2)}) %collective-permute-start.18) | collective-permute-done | bytes 800 | tf_op jit(solution)/shard_map/ppermute | solution.py:24
  99.4 0.3 collective-permute-start.19
  99.7 4.3 %collective-permute-done.19 = f32[3,64]{1,0:T(4,128)S(1)} collective-permute-done((f32[3,64]{1,0:T(4,128)S(1)}, f32[3,64]{1,0:T(4,128)S(1)}, u32[]{:S(2)}, u32[]{:S(2)}) %collective-permute-start.19) | collective-permute-done | bytes 800 | tf_op jit(solution)/shard_map/ppermute | solution.py:24
  104.0 0.5 bitcast_subtract_fusion
  104.5 14.5 %convolution_convert_fusion = bf16[4096,4096]{1,0:T(8,128)(2,1)} fusion(bf16[64,4096]{1,0:T(8,128)(2,1)S(1)} %bitcast.99, f32[64,4096]{1,0:T(8,128)S(1)} %get-tuple-element.34, f32[64]{0:T(128)S(1)} %get-tuple-element.8, s32[4096]{0:T(1024)S(1)} %iota_add_fusion, s32[64]{0:T(128)S(1)} %eq.66), kind=kOutput, calls=%fused_computation | convolution fusion | flops 2165833728 | bytes 35144192 | tf_op jit(solution)/shard_map/rv,rd->vd/dot_general | solution.py:169
  119.0 0.3 fusion.2
  119.3 0.6 broadcast_multiply_fusion
  (59 shorter events, 1.0 us)
Async XLA Ops:
  0.6 23.9 %copy-start = (bf16[512,1024]{1,0:T(8,128)(2,1)S(1)}, bf16[512,1024]{1,0:T(8,128)(2,1)}, u32[]{:S(2)}) copy-start(bf16[512,1024]{1,0:T(8,128)(2,1)} %param.14) | copy-start | bytes 3145732
  11.8 12.7 %all-to-all-start = ((bf16[8,8,512]{2,1,0:T(8,128)(2,1)}), bf16[8,8,512]{2,1,0:T(8,128)(2,1)S(1)}, u32[]{:S(2)}, u32[]{:S(2)}) async-start(bf16[8,8,512]{2,1,0:T(8,128)(2,1)} %bitcast.5), calls=%async_computation | async-start | bytes 131072 | tf_op jit(solution)/shard_map/all_to_all | solution.py:126
  18.4 7.1 %collective-permute-start.10 = (s32[1,7]{1,0:T(1,128)S(1)}, s32[1,7]{1,0:T(1,128)S(1)}, u32[]{:S(2)}, u32[]{:S(2)}) collective-permute-start(s32[1,7]{1,0:T(1,128)S(1)} %add_bitcast_fusion), channel_id=1, source_target_pairs={{0,1},{1,0},{2,3},{3,2},{4,5},{5,4},{6,7},{7,6},{8,9},{9,8},{10,11... | collective-permute-start | bytes 92 | tf_op jit(solution)/shard_map/ppermute | solution.py:35
  24.9 7.7 %collective-permute-start = (f32[4,8,1024]{2,1,0:T(8,128)S(1)}, f32[4,8,1024]{2,1,0:T(8,128)S(1)}, u32[]{:S(2)}, u32[]{:S(2)}) collective-permute-start(f32[4,8,1024]{2,1,0:T(8,128)S(1)} %select_bitcast_fusion), channel_id=1, source_target_pairs={{0,16},{4,20},{8,24},{12,28},{16,0},{20,4},{24,8},{28,12},{1,17},{... | collective-permute-start | bytes 393224 | tf_op jit(solution)/shard_map/ppermute | solution.py:50
  25.5 12.7 %collective-permute-start.11 = (s32[2,7]{1,0:T(2,128)S(1)}, s32[2,7]{1,0:T(2,128)S(1)}, u32[]{:S(2)}, u32[]{:S(2)}) collective-permute-start(s32[2,7]{1,0:T(2,128)S(1)} %add_select_fusion.4), channel_id=1, source_target_pairs={{0,2},{1,3},{2,0},{3,1},{4,6},{5,7},{6,4},{7,5},{8,10},{9,11},{10,... | collective-permute-start | bytes 176 | tf_op jit(solution)/shard_map/ppermute | solution.py:35
  32.7 4.3 %collective-permute-start.1 = (f32[2,8,1024]{2,1,0:T(8,128)S(1)}, f32[2,8,1024]{2,1,0:T(8,128)S(1)}, u32[]{:S(2)}, u32[]{:S(2)}) collective-permute-start(f32[2,8,1024]{2,1,0:T(8,128)S(1)} %slice_select_fusion), channel_id=1, source_target_pairs={{0,8},{4,12},{8,0},{12,4},{16,24},{20,28},{24,16},{28,20},{1,9},{5... | collective-permute-start | bytes 196616 | tf_op jit(solution)/shard_map/ppermute | solution.py:50
  37.0 4.0 %collective-permute-start.2 = (f32[1,8,1024]{2,1,0:T(8,128)S(1)}, f32[1,8,1024]{2,1,0:T(8,128)S(1)}, u32[]{:S(2)}, u32[]{:S(2)}) collective-permute-start(f32[1,8,1024]{2,1,0:T(8,128)S(1)} %slice_select_fusion.1), channel_id=1, source_target_pairs={{0,4},{4,0},{8,12},{12,8},{16,20},{20,16},{24,28},{28,24},{1,5},{5... | collective-permute-start | bytes 98312 | tf_op jit(solution)/shard_map/ppermute | solution.py:50
  38.1 3.9 %collective-permute-start.12 = (s32[1,4,7]{2,1,0:T(4,128)S(1)}, s32[1,4,7]{2,1,0:T(4,128)S(1)}, u32[]{:S(2)}, u32[]{:S(2)}) collective-permute-start(s32[1,4,7]{2,1,0:T(4,128)S(1)} %add_select_fusion.3), channel_id=1, source_target_pairs={{0,4},{4,0},{8,12},{12,8},{16,20},{20,16},{24,28},{28,24},{1,5},{5... | collective-permute-start | bytes 344 | tf_op jit(solution)/shard_map/ppermute | solution.py:35
  42.0 1.2 %collective-permute-start.3 = (f32[2,8]{1,0:T(2,128)S(1)}, f32[2,8]{1,0:T(2,128)S(1)}, u32[]{:S(2)}, u32[]{:S(2)}) collective-permute-start(f32[2,8]{1,0:T(2,128)S(1)} %pad_maximum_fusion.5), channel_id=1, source_target_pairs={{0,1},{1,0},{2,3},{3,2},{4,5},{5,4},{6,7},{7,6},{8,9},{9,8},{10,11... | collective-permute-start | bytes 200 | tf_op jit(solution)/shard_map/ppermute | solution.py:24
  43.2 3.6 %collective-permute-start.4 = (f32[2,8]{1,0:T(2,128)S(1)}, f32[2,8]{1,0:T(2,128)S(1)}, u32[]{:S(2)}, u32[]{:S(2)}) collective-permute-start(f32[2,8]{1,0:T(2,128)S(1)} %select_add_fusion.3), channel_id=1, source_target_pairs={{0,2},{1,3},{2,0},{3,1},{4,6},{5,7},{6,4},{7,5},{8,10},{9,11},{10,... | collective-permute-start | bytes 200 | tf_op jit(solution)/shard_map/ppermute | solution.py:24
  44.8 4.0 %collective-permute-start.13 = (s32[2,4,7]{2,1,0:T(4,128)S(1)}, s32[2,4,7]{2,1,0:T(4,128)S(1)}, u32[]{:S(2)}, u32[]{:S(2)}) collective-permute-start(s32[2,4,7]{2,1,0:T(4,128)S(1)} %add_select_fusion.2), channel_id=1, source_target_pairs={{0,8},{4,12},{8,0},{12,4},{16,24},{20,28},{24,16},{28,20},{1,9},{5... | collective-permute-start | bytes 680 | tf_op jit(solution)/shard_map/ppermute | solution.py:35
  47.7 3.8 %collective-permute-start.5 = (bf16[1,8,1024]{2,1,0:T(8,128)(2,1)S(1)}, bf16[1,8,1024]{2,1,0:T(8,128)(2,1)S(1)}, u32[]{:S(2)}, u32[]{:S(2)}) collective-permute-start(bf16[1,8,1024]{2,1,0:T(8,128)(2,1)S(1)} %fusion.18), channel_id=1, source_target_pairs={{0,4},{4,0},{8,12},{12,8},{16,20},{20,16},{24,28},{28,24},{1,5},{5... | collective-permute-start | bytes 49160 | tf_op jit(solution)/shard_map/ppermute | solution.py:35
  48.8 4.6 %collective-permute-start.14 = (s32[4,4,7]{2,1,0:T(4,128)S(1)}, s32[4,4,7]{2,1,0:T(4,128)S(1)}, u32[]{:S(2)}, u32[]{:S(2)}) collective-permute-start(s32[4,4,7]{2,1,0:T(4,128)S(1)} %add_select_fusion.1), channel_id=1, source_target_pairs={{0,16},{4,20},{8,24},{12,28},{16,0},{20,4},{24,8},{28,12},{1,17},{... | collective-permute-start | bytes 1352 | tf_op jit(solution)/shard_map/ppermute | solution.py:35
  51.5 4.0 %collective-permute-start.6 = (bf16[2,8,1024]{2,1,0:T(8,128)(2,1)S(1)}, bf16[2,8,1024]{2,1,0:T(8,128)(2,1)S(1)}, u32[]{:S(2)}, u32[]{:S(2)}) collective-permute-start(bf16[2,8,1024]{2,1,0:T(8,128)(2,1)S(1)} %maximum_select_fusion.4), channel_id=1, source_target_pairs={{0,8},{4,12},{8,0},{12,4},{16,24},{20,28},{24,16},{28,20},{1,9},{5... | collective-permute-start | bytes 98312 | tf_op jit(solution)/shard_map/ppermute | solution.py:35
  55.5 5.4 %collective-permute-start.7 = (bf16[4,8,1024]{2,1,0:T(8,128)(2,1)S(1)}, bf16[4,8,1024]{2,1,0:T(8,128)(2,1)S(1)}, u32[]{:S(2)}, u32[]{:S(2)}) collective-permute-start(bf16[4,8,1024]{2,1,0:T(8,128)(2,1)S(1)} %maximum_select_fusion.3), channel_id=1, source_target_pairs={{0,16},{4,20},{8,24},{12,28},{16,0},{20,4},{24,8},{28,12},{1,17},{... | collective-permute-start | bytes 196616 | tf_op jit(solution)/shard_map/ppermute | solution.py:35
  60.9 1.4 %collective-permute-start.8 = (bf16[1,64,1024]{2,1,0:T(8,128)(2,1)S(1)}, bf16[1,64,1024]{2,1,0:T(8,128)(2,1)S(1)}, u32[]{:S(2)}, u32[]{:S(2)}) collective-permute-start(bf16[1,64,1024]{2,1,0:T(8,128)(2,1)S(1)} %fusion.8), channel_id=1, source_target_pairs={{0,1},{1,0},{2,3},{3,2},{4,5},{5,4},{6,7},{7,6},{8,9},{9,8},{10,11... | collective-permute-start | bytes 393224 | tf_op jit(solution)/shard_map/ppermute | solution.py:35
  62.3 8.4 %collective-permute-start.9 = (bf16[2,64,1024]{2,1,0:T(8,128)(2,1)S(1)}, bf16[2,64,1024]{2,1,0:T(8,128)(2,1)S(1)}, u32[]{:S(2)}, u32[]{:S(2)}) collective-permute-start(bf16[2,64,1024]{2,1,0:T(8,128)(2,1)S(1)} %maximum_select_fusion.1), channel_id=1, source_target_pairs={{0,2},{1,3},{2,0},{3,1},{4,6},{5,7},{6,4},{7,5},{8,10},{9,11},{10,... | collective-permute-start | bytes 786440 | tf_op jit(solution)/shard_map/ppermute | solution.py:35
  87.0 1.2 %collective-permute-start.15 = (f32[3,64]{1,0:T(4,128)S(1)}, f32[3,64]{1,0:T(4,128)S(1)}, u32[]{:S(2)}, u32[]{:S(2)}) collective-permute-start(f32[3,64]{1,0:T(4,128)S(1)} %pad_maximum_fusion), channel_id=1, source_target_pairs={{0,1},{1,0},{2,3},{3,2},{4,5},{5,4},{6,7},{7,6},{8,9},{9,8},{10,11... | collective-permute-start | bytes 2312 | tf_op jit(solution)/shard_map/ppermute | solution.py:24
  88.3 3.7 %collective-permute-start.16 = (f32[3,64]{1,0:T(4,128)S(1)}, f32[3,64]{1,0:T(4,128)S(1)}, u32[]{:S(2)}, u32[]{:S(2)}) collective-permute-start(f32[3,64]{1,0:T(4,128)S(1)} %pad_maximum_fusion.1), channel_id=1, source_target_pairs={{0,2},{1,3},{2,0},{3,1},{4,6},{5,7},{6,4},{7,5},{8,10},{9,11},{10,... | collective-permute-start | bytes 2312 | tf_op jit(solution)/shard_map/ppermute | solution.py:24
  92.0 3.7 %collective-permute-start.17 = (f32[3,64]{1,0:T(4,128)S(1)}, f32[3,64]{1,0:T(4,128)S(1)}, u32[]{:S(2)}, u32[]{:S(2)}) collective-permute-start(f32[3,64]{1,0:T(4,128)S(1)} %pad_maximum_fusion.2), channel_id=1, source_target_pairs={{0,4},{4,0},{8,12},{12,8},{16,20},{20,16},{24,28},{28,24},{1,5},{5... | collective-permute-start | bytes 2312 | tf_op jit(solution)/shard_map/ppermute | solution.py:24
  95.7 3.7 %collective-permute-start.18 = (f32[3,64]{1,0:T(4,128)S(1)}, f32[3,64]{1,0:T(4,128)S(1)}, u32[]{:S(2)}, u32[]{:S(2)}) collective-permute-start(f32[3,64]{1,0:T(4,128)S(1)} %pad_maximum_fusion.3), channel_id=1, source_target_pairs={{0,8},{4,12},{8,0},{12,4},{16,24},{20,28},{24,16},{28,20},{1,9},{5... | collective-permute-start | bytes 2312 | tf_op jit(solution)/shard_map/ppermute | solution.py:24
  99.4 4.5 %collective-permute-start.19 = (f32[3,64]{1,0:T(4,128)S(1)}, f32[3,64]{1,0:T(4,128)S(1)}, u32[]{:S(2)}, u32[]{:S(2)}) collective-permute-start(f32[3,64]{1,0:T(4,128)S(1)} %pad_maximum_fusion.4), channel_id=1, source_target_pairs={{0,16},{4,20},{8,24},{12,28},{16,0},{20,4},{24,8},{28,12},{1,17},{... | collective-permute-start | bytes 2312 | tf_op jit(solution)/shard_map/ppermute | solution.py:24

commit v3 on v2

--- a/solution.py
+++ b/solution.py
@@ -28,30 +28,53 @@
     return x
 
 
-def _allgather(x, axis, n):
+def _allgather(x, axis, n, order=None):
+    order = order or _steps(n)
     buf = x[None]
-    step = 1
-    while step < n:
+    for step in order:
         theirs = lax.ppermute(buf, axis, [(a, a ^ step) for a in range(n)])
         upper = (lax.axis_index(axis) & step) != 0
         buf = jnp.where(upper, jnp.concatenate([theirs, buf]), jnp.concatenate([buf, theirs]))
+    block_of = [sum(((p >> t) & 1) * step for t, step in enumerate(order)) for p in range(n)]
+    if block_of != list(range(n)):
+        place = [block_of.index(k) for k in range(n)]
+        buf = buf[jnp.array(place, dtype=jnp.int32)]
+    return buf
+
+
+def _steps(n):
+    out, step = [], 1
+    while step < n:
+        out.append(step)
         step *= 2
-    return buf
-
-
-def _reduce_scatter(x, axis, n):
+    return out
+
+
+def _reduce_scatter(x, axis, n, order=None):
+    order = order or _steps(n)[::-1]
     idx = lax.axis_index(axis)
-    step = n // 2
-    while step >= 1:
-        halves = x.reshape((2, x.shape[0] // 2) + x.shape[1:])
+    bits = _steps(n)[::-1]
+    rest = x.shape[1:]
+    x = x.reshape((2,) * len(bits) + rest)
+    for step in order:
+        at = bits.index(step)
         upper = (idx & step) != 0
-        kept = jnp.where(upper, halves[1], halves[0])
-        sent = jnp.where(upper, halves[0], halves[1])
+        low, high = jnp.take(x, 0, axis=at), jnp.take(x, 1, axis=at)
+        kept = jnp.where(upper, high, low)
+        sent = jnp.where(upper, low, high)
         theirs = lax.ppermute(sent, axis, [(a, a ^ step) for a in range(n)])
         lo, hi = _canon(axis, step, kept, theirs)
         x = lo + hi
-        step //= 2
-    return x[0]
+        bits.pop(at)
+    return x
+
+
+def _pieces(t):
+    return jnp.concatenate([t >> 16, (t >> 8) & 255, t & 255])
+
+
+def _unpieces(p):
+    return p[..., 0, :] * 65536 + p[..., 1, :] * 256 + p[..., 2, :]
 
 
 def _add(lo, hi):
@@ -64,9 +87,9 @@
     return lax.psum(x, axis)
 
 
-def _gather(x, axis, n):
+def _gather(x, axis, n, order=None):
     if _pow2(n):
-        return _allgather(x, axis, n)
+        return _allgather(x, axis, n, order)
     return lax.all_gather(x, axis, axis=0, tiled=False)
 
 
@@ -98,10 +121,16 @@
     tokens = hidden.shape[0]
     onehot = (positions[0][:, None] == jnp.arange(tokens, dtype=jnp.int32)[None, :]).astype(hidden.dtype)
     picked = jnp.dot(onehot, hidden, preferred_element_type=jnp.float32).astype(hidden.dtype)
-    count_row = jnp.broadcast_to(counts.astype(hidden.dtype)[:, None], (1, model))
-    listed = lax.all_gather(jnp.concatenate([picked, count_row]), "vocab", axis=0, tiled=False)
+    meta = jnp.zeros((1, model), jnp.int32)
+    meta = meta.at[0, 0].set(counts[0])
+    meta = lax.dynamic_update_slice(meta, _pieces(targets[0])[None], (0, 1))
+    listed = lax.all_gather(
+        jnp.concatenate([picked, meta.astype(hidden.dtype)]), "vocab", axis=0, tiled=False
+    )
     listed_rows = listed[:, :slots].reshape(ways * slots, model)
-    listed_counts = listed[:, slots, 0].astype(jnp.int32)
+    listed_meta = listed[:, slots, : 1 + 3 * slots].astype(jnp.int32)
+    listed_counts = listed_meta[:, 0]
+    listed_tgt = _unpieces(listed_meta[:, 1:].reshape(ways, 3, slots)).reshape(ways * slots)
     slot_ids = jnp.tile(jnp.arange(slots, dtype=jnp.int32), ways)
     row_ids = jnp.arange(group_rows, dtype=jnp.int32)
 
@@ -116,17 +145,18 @@
     rows = jnp.dot(
         chooser.astype(jnp.bfloat16), listed_rows, preferred_element_type=jnp.float32
     ).astype(jnp.bfloat16)
-    ints = jnp.concatenate([counts, targets[0]])
-    all_ints = _gather(_gather(ints, "vocab", ways), "dp", groups).reshape(groups, ways, slots + 1)
-    all_choosers = jax.vmap(choose)(all_ints[:, :, 0])
-    tgt_all = jnp.sum(
-        jnp.where(all_choosers, all_ints[:, None, :, 1:].reshape(groups, 1, ways * slots), 0), axis=2
-    ).reshape(total_rows).astype(jnp.int32)
+    tgt = jnp.sum(jnp.where(chooser, listed_tgt[None, :], 0), axis=1).astype(jnp.int32)
     blocks = rows.reshape(group_rows, groups, in_block).transpose(1, 0, 2)
-    rows_in = lax.all_to_all(blocks, "dp", 0, 0, tiled=True).reshape(total_rows, in_block)
+    tgt_row = jnp.zeros((in_block,), jnp.int32).at[: 3 * group_rows].set(_pieces(tgt))
+    tgt_rows = jnp.broadcast_to(tgt_row.astype(jnp.bfloat16), (groups, 1, in_block))
+    got = lax.all_to_all(jnp.concatenate([blocks, tgt_rows], axis=1), "dp", 0, 0, tiled=True)
+    rows_in = got[:, :group_rows].reshape(total_rows, in_block)
+    tgt_all = _unpieces(
+        got[:, group_rows, : 3 * group_rows].astype(jnp.int32).reshape(groups, 3, group_rows)
+    ).reshape(total_rows)
     part = jnp.dot(rows_in, dense_weight, preferred_element_type=jnp.float32)
     if _pow2(groups):
-        act = _reduce_scatter(part.reshape(groups, group_rows, -1), "dp", groups)
+        act = _reduce_scatter(part.reshape(groups, group_rows, -1), "dp", groups, _steps(groups))
     else:
         act = lax.psum_scatter(part.reshape(groups, group_rows, -1), "dp", scatter_dimension=0, tiled=True)[0]
     act = jax.nn.gelu(act + dense_bias, approximate=False)
@@ -136,8 +166,8 @@
     head_rows = (
         (act - mean[:, None]) * lax.rsqrt(var + EPS)[:, None] * norm_gain + norm_shift
     ).astype(jnp.bfloat16)
-    head_cols = _gather(head_rows, "dp", groups).reshape(total_rows, -1)
-    head_all = _gather(head_cols, "vocab", ways).transpose(1, 0, 2).reshape(total_rows, model)
+    head_cols = _gather(head_rows, "dp", groups, _steps(groups)[::-1]).reshape(total_rows, -1)
+    head_all = _gather(head_cols, "vocab", ways, _steps(ways)[::-1]).transpose(1, 0, 2).reshape(total_rows, model)
     vocab_rows = embedding.shape[0]
     first_id = (lax.axis_index("dp") * ways + lax.axis_index("vocab")) * vocab_rows
     ids = first_id + jnp.arange(vocab_rows, dtype=jnp.int32)

time: 120 us -> 119 us (level)
  starting transfers between devices: 18.1 us -> 15.3 us
  other arithmetic: 5.47 us -> 8.07 us
  waiting for transfers between devices: 53.2 us -> 51.9 us
    ppermute x10 -> x5, waiting for transfers between devices: 18.7 us -> 14.9 us  [_allgather(): theirs = lax.ppermute(buf, axis, [(a, a ^ step) for a in range(n)])]
    ppermute x10 -> x5, starting transfers between devices: 5.94 us -> 3.15 us  [_allgather(): theirs = lax.ppermute(buf, axis, [(a, a ^ step) for a in range(n)])]
    all_to_all x1, waiting for transfers between devices: 6.11 us -> 7.49 us  [body(): lax.all_to_all(jnp.concatenate([blocks, tgt_rows], axis=1), 'dp', 0, 0, t...]
    gather x0 -> x2, other arithmetic: none -> 1.32 us  [_allgather(): buf = buf[jnp.array(place, dtype=jnp.int32)]]
    ppermute x3, waiting for transfers between devices: 11.6 us -> 12.9 us  [_reduce_scatter(): theirs = lax.ppermute(sent, axis, [(a, a ^ step) for a in range(n)])]
  transfers between devices with their start and end apart: 21 -> 16, of which waited for: 17 -> 16; matrix products, arithmetic and copies ran while one was open for 3% -> 1% of each run, Pallas kernels for 0% -> 0%
where the time goes in v3:
time: 119 us
  waiting for transfers between devices  51.9 us (44%)
  matrix products  32.1 us (27%)
  starting transfers between devices  15.3 us (13%)
  other arithmetic  8.07 us (7%)
  blocking collectives  7.25 us (6%)
  between operations  2.22 us (2%)
  local copies, waits for them, and re-layouts  2.17 us (2%)
    ppermute x7, waiting for transfers between devices, _allreduce(): theirs = lax.ppermute(x, axis, [(a, a ^ step) for a in range(n)])  16.6 us
    dot_general x1, matrix products, body(): jnp.einsum('rd,vd->rv', head_all, embedding, preferred_element_type=jnp.f...  15.7 us
    ppermute x5, waiting for transfers between devices, _allgather(): theirs = lax.ppermute(buf, axis, [(a, a ^ step) for a in range(n)])  14.9 us
    dot_general x1, matrix products, body(): jnp.einsum('rv,rd->vd', grad, head_all, preferred_element_type=jnp.float32)  14.5 us
    ppermute x3, waiting for transfers between devices, _reduce_scatter(): theirs = lax.ppermute(sent, axis, [(a, a ^ step) for a in range(n)])  12.9 us
    all_to_all x1, waiting for transfers between devices, body(): lax.all_to_all(jnp.concatenate([blocks, tgt_rows], axis=1), 'dp', 0, 0, t...  7.49 us
    all_gather x1, blocking collectives, body(): lax.all_gather(jnp.concatenate([picked, meta.astype(hidden.dtype)]), 'voc...  7.25 us
    all_to_all x1, starting transfers between devices, body(): lax.all_to_all(jnp.concatenate([blocks, tgt_rows], axis=1), 'dp', 0, 0, t...  5.81 us
  transfers between devices with their start and end apart: 16, of which 16 were waited for; matrix products, arithmetic and copies ran while one was open for 1% of the time, Pallas kernels for 0%

profile of v3, /device:TPU:0, one launch (start us, length us, event | category | flops | bytes accessed | tf_op | source)
XLA Modules:
  0.0 119.0 jit_solution(15006500445603578713)
XLA Ops:
  0.6 0.6 compare_reduce_fusion
  1.3 0.7 shift-right-arithmetic_bitcast_fusion
  3.3 0.1 add_bitcast_fusion
  3.3 0.2 dynamic_update_slice.3
  3.6 1.5 %convolution_convert_fusion.2 = bf16[6,4096]{1,0:T(8,128)(2,1)S(1)} fusion(bf16[128,4096]{1,0:T(8,128)(2,1)} %param.28, s32[6]{0:T(128)} %bitcast.151), kind=kOutput, calls=%fused_computation.5 | convolution fusion | flops 6316800 | bytes 1097752 | tf_op jit(solution)/shard_map/dot_general | solution.py:123
  5.2 7.3 %all-gather.1 = bf16[4,7,4096]{2,1,0:T(8,128)(2,1)S(1)} all-gather(bf16[1,7,4096]{2,1,0:T(8,128)(2,1)S(1)} %maximum_bitcast_fusion), channel_id=2, replica_groups=mesh['dp'=8,'vocab'=4] {'vocab'}, dimensions={0}, use_global_device_ids=true | all-gather | bytes 286720 | tf_op jit(solution)/shard_map/all_gather | solution.py:127
  12.4 0.1 slice_reduce_fusion
  12.6 0.1 reduce.9
  12.8 0.1 iota_compare_fusion.4
  12.8 0.1 iota_add_fusion.1
  12.9 0.1 add.178
  13.0 0.1 lt.23
  13.1 0.1 reshape.251
  13.2 0.1 add.181
  13.3 0.1 select_reduce_fusion
  13.5 0.2 convolution_convert_fusion.1
  13.7 0.1 fusion.36
  13.8 0.7 pad_maximum_fusion
  14.4 5.8 %all-to-all-start = ((bf16[8,9,512]{2,1,0:T(8,128)(2,1)}), bf16[8,9,512]{2,1,0:T(8,128)(2,1)S(1)}, u32[]{:S(2)}, u32[]{:S(2)}) async-start(bf16[8,9,512]{2,1,0:T(8,128)(2,1)} %pad_maximum_fusion), calls=%async_computation | async-start | bytes 262144 | tf_op jit(solution)/shard_map/all_to_all | solution.py:152
  20.2 7.5 %all-to-all-done = bf16[8,9,512]{2,1,0:T(8,128)(2,1)S(1)} async-done(((bf16[8,9,512]{2,1,0:T(8,128)(2,1)}), bf16[8,9,512]{2,1,0:T(8,128)(2,1)S(1)}, u32[]{:S(2)}, u32[]{:S(2)}) %all-to-all-start) | async-done | bytes 73760 | tf_op jit(solution)/shard_map/all_to_all | solution.py:152
  27.7 0.3 fusion.2
  28.1 0.5 collective-permute-start
  28.5 4.6 %collective-permute-done = f32[2,2,8,1024]{3,2,1,0:T(8,128)S(1)} collective-permute-done((f32[2,2,8,1024]{3,2,1,0:T(8,128)S(1)}, f32[2,2,8,1024]{3,2,1,0:T(8,128)S(1)}, u32[]{:S(2)}, u32[]{:S(2)}) %collective-permute-start) | collective-permute-done | bytes 131104 | tf_op jit(solution)/shard_map/ppermute | solution.py:65
  33.2 0.1 collective-permute-start.1
  33.3 4.2 %collective-permute-done.1 = f32[2,8,1024]{2,1,0:T(8,128)S(1)} collective-permute-done((f32[2,8,1024]{2,1,0:T(8,128)S(1)}, f32[2,8,1024]{2,1,0:T(8,128)S(1)}, u32[]{:S(2)}, u32[]{:S(2)}) %collective-permute-start.1) | collective-permute-done | bytes 65568 | tf_op jit(solution)/shard_map/ppermute | solution.py:65
  37.5 0.8 collective-permute-start.2
  38.3 4.1 %collective-permute-done.2 = f32[8,1024]{1,0:T(8,128)S(1)} collective-permute-done((f32[8,1024]{1,0:T(8,128)S(1)}, f32[8,1024]{1,0:T(8,128)S(1)}, u32[]{:S(2)}, u32[]{:S(2)}) %collective-permute-start.2) | collective-permute-done | bytes 32800 | tf_op jit(solution)/shard_map/ppermute | solution.py:65
  42.4 0.9 fusion.46
  43.4 1.1 collective-permute-done.3
  44.6 1.6 %collective-permute-start.4 = (f32[2,8]{1,0:T(2,128)S(1)}, f32[2,8]{1,0:T(2,128)S(1)}, u32[]{:S(2)}, u32[]{:S(2)}) collective-permute-start(f32[2,8]{1,0:T(2,128)S(1)} %select_add_fusion.3), channel_id=1, source_target_pairs={{0,2},{1,3},{2,0},{3,1},{4,6},{5,7},{6,4},{7,5},{8,10},{9,11},{10,... | collective-permute-start | bytes 200 | tf_op jit(solution)/shard_map/ppermute | solution.py:24
  46.2 2.1 %collective-permute-done.4 = f32[2,8]{1,0:T(2,128)S(1)} collective-permute-done((f32[2,8]{1,0:T(2,128)S(1)}, f32[2,8]{1,0:T(2,128)S(1)}, u32[]{:S(2)}, u32[]{:S(2)}) %collective-permute-start.4) | collective-permute-done | bytes 96 | tf_op jit(solution)/shard_map/ppermute | solution.py:24
  48.2 0.8 fusion.21
  49.0 0.8 collective-permute-start.5
  49.8 3.9 %collective-permute-done.5 = bf16[1,8,1024]{2,1,0:T(8,128)(2,1)S(1)} collective-permute-done((bf16[1,8,1024]{2,1,0:T(8,128)(2,1)S(1)}, bf16[1,8,1024]{2,1,0:T(8,128)(2,1)S(1)}, u32[]{:S(2)}, u32[]{:S(2)}) %collective-permute-start.5) | collective-permute-done | bytes 16416 | tf_op jit(solution)/shard_map/ppermute | solution.py:35
  53.7 0.3 collective-permute-start.6
  54.0 3.7 %collective-permute-done.6 = bf16[2,8,1024]{2,1,0:T(8,128)(2,1)S(1)} collective-permute-done((bf16[2,8,1024]{2,1,0:T(8,128)(2,1)S(1)}, bf16[2,8,1024]{2,1,0:T(8,128)(2,1)S(1)}, u32[]{:S(2)}, u32[]{:S(2)}) %collective-permute-start.6) | collective-permute-done | bytes 32800 | tf_op jit(solution)/shard_map/ppermute | solution.py:35
  57.7 0.5 collective-permute-start.7
  58.2 0.7 pad_clamp_fusion.1
  58.8 3.2 %collective-permute-done.7 = bf16[4,8,1024]{2,1,0:T(8,128)(2,1)S(1)} collective-permute-done((bf16[4,8,1024]{2,1,0:T(8,128)(2,1)S(1)}, bf16[4,8,1024]{2,1,0:T(8,128)(2,1)S(1)}, u32[]{:S(2)}, u32[]{:S(2)}) %collective-permute-start.7) | collective-permute-done | bytes 65568 | tf_op jit(solution)/shard_map/ppermute | solution.py:35
  62.0 0.6 gather_fusion
  62.6 1.6 %collective-permute-start.8 = (bf16[1,64,1024]{2,1,0:T(8,128)(2,1)S(1)}, bf16[1,64,1024]{2,1,0:T(8,128)(2,1)S(1)}, u32[]{:S(2)}, u32[]{:S(2)}) collective-permute-start(bf16[1,64,1024]{2,1,0:T(8,128)(2,1)S(1)} %bitcast.133), channel_id=1, source_target_pairs={{0,2},{1,3},{2,0},{3,1},{4,6},{5,7},{6,4},{7,5},{8,10},{9,11},{10,... | collective-permute-start | bytes 393224 | tf_op jit(solution)/shard_map/ppermute | solution.py:35
  64.2 3.4 %collective-permute-done.8 = bf16[1,64,1024]{2,1,0:T(8,128)(2,1)S(1)} collective-permute-done((bf16[1,64,1024]{2,1,0:T(8,128)(2,1)S(1)}, bf16[1,64,1024]{2,1,0:T(8,128)(2,1)S(1)}, u32[]{:S(2)}, u32[]{:S(2)}) %collective-permute-start.8) | collective-permute-done | bytes 131104 | tf_op jit(solution)/shard_map/ppermute | solution.py:35
  67.8 0.7 pad_clamp_fusion
  68.4 0.1 reshape.396
  68.6 0.1 add.198
  68.6 0.6 collective-permute-done.9
  69.3 0.1 maximum_select_fusion
  69.4 0.6 gather_fusion.1
  70.0 15.7 %fusion.49 = (f32[64]{0:T(128)S(1)}, f32[64,4096]{1,0:T(8,128)S(1)}) fusion(f32[4096]{0:T(1024)} %param.37, bf16[64,4096]{1,0:T(8,128)(2,1)S(1)} %bitcast.129, bf16[4096,4096]{1,0:T(8,128)(2,1)} %param.36), kind=kOutput, calls=%fused_computation.147 | convolution fusion | flops 2148007936 | bytes 35143936 | tf_op jit(solution)/shard_map/rd,vd->rv/dot_general | solution.py:175
  85.7 0.4 exponential_reduce_fusion
  86.1 0.2 collective-permute-start.10
  86.4 1.0 collective-permute-done.10
  87.4 1.6 %collective-permute-start.11 = (f32[3,64]{1,0:T(4,128)S(1)}, f32[3,64]{1,0:T(4,128)S(1)}, u32[]{:S(2)}, u32[]{:S(2)}) collective-permute-start(f32[3,64]{1,0:T(4,128)S(1)} %pad_maximum_fusion.2), channel_id=1, source_target_pairs={{0,2},{1,3},{2,0},{3,1},{4,6},{5,7},{6,4},{7,5},{8,10},{9,11},{10,... | collective-permute-start | bytes 2312 | tf_op jit(solution)/shard_map/ppermute | solution.py:24
  89.0 2.1 %collective-permute-done.11 = f32[3,64]{1,0:T(4,128)S(1)} collective-permute-done((f32[3,64]{1,0:T(4,128)S(1)}, f32[3,64]{1,0:T(4,128)S(1)}, u32[]{:S(2)}, u32[]{:S(2)}) %collective-permute-start.11) | collective-permute-done | bytes 800 | tf_op jit(solution)/shard_map/ppermute | solution.py:24
  91.1 0.5 collective-permute-start.12
  91.6 3.2 %collective-permute-done.12 = f32[3,64]{1,0:T(4,128)S(1)} collective-permute-done((f32[3,64]{1,0:T(4,128)S(1)}, f32[3,64]{1,0:T(4,128)S(1)}, u32[]{:S(2)}, u32[]{:S(2)}) %collective-permute-start.12) | collective-permute-done | bytes 800 | tf_op jit(solution)/shard_map/ppermute | solution.py:24
  94.8 0.3 collective-permute-start.13
  95.1 3.4 %collective-permute-done.13 = f32[3,64]{1,0:T(4,128)S(1)} collective-permute-done((f32[3,64]{1,0:T(4,128)S(1)}, f32[3,64]{1,0:T(4,128)S(1)}, u32[]{:S(2)}, u32[]{:S(2)}) %collective-permute-start.13) | collective-permute-done | bytes 800 | tf_op jit(solution)/shard_map/ppermute | solution.py:24
  98.5 0.8 collective-permute-start.14
  99.3 3.8 %collective-permute-done.14 = f32[3,64]{1,0:T(4,128)S(1)} collective-permute-done((f32[3,64]{1,0:T(4,128)S(1)}, f32[3,64]{1,0:T(4,128)S(1)}, u32[]{:S(2)}, u32[]{:S(2)}) %collective-permute-start.14) | collective-permute-done | bytes 800 | tf_op jit(solution)/shard_map/ppermute | solution.py:24
  103.1 0.5 bitcast_subtract_fusion
  103.6 14.5 %convolution_convert_fusion = bf16[4096,4096]{1,0:T(8,128)(2,1)} fusion(bf16[64,4096]{1,0:T(8,128)(2,1)S(1)} %bitcast.130, f32[64,4096]{1,0:T(8,128)S(1)} %get-tuple-element.137, f32[64]{0:T(128)S(1)} %get-tuple-element.104, s32[4096]{0:T(1024)S(1)} %iota_add_fusion, s32[64]{0:T(128)S(1)} %add.198), kind=kOutput, calls=%fused_computation.2 | convolution fusion | flops 2165833728 | bytes 35144192 | tf_op jit(solution)/shard_map/rv,rd->vd/dot_general | solution.py:199
  118.1 0.3 fusion.4
  118.4 0.6 broadcast_multiply_fusion
  (48 shorter events, 0.9 us)
Async XLA Ops:
  0.6 27.1 %copy-start = (bf16[512,1024]{1,0:T(8,128)(2,1)S(1)}, bf16[512,1024]{1,0:T(8,128)(2,1)}, u32[]{:S(2)}) copy-start(bf16[512,1024]{1,0:T(8,128)(2,1)} %param.32) | copy-start | bytes 3145732
  14.4 13.3 %all-to-all-start = ((bf16[8,9,512]{2,1,0:T(8,128)(2,1)}), bf16[8,9,512]{2,1,0:T(8,128)(2,1)S(1)}, u32[]{:S(2)}, u32[]{:S(2)}) async-start(bf16[8,9,512]{2,1,0:T(8,128)(2,1)} %pad_maximum_fusion), calls=%async_computation | async-start | bytes 262144 | tf_op jit(solution)/shard_map/all_to_all | solution.py:152
  28.1 5.0 %collective-permute-start = (f32[2,2,8,1024]{3,2,1,0:T(8,128)S(1)}, f32[2,2,8,1024]{3,2,1,0:T(8,128)S(1)}, u32[]{:S(2)}, u32[]{:S(2)}) collective-permute-start(f32[2,2,8,1024]{3,2,1,0:T(8,128)S(1)} %fusion.9), channel_id=1, source_target_pairs={{0,4},{4,0},{8,12},{12,8},{16,20},{20,16},{24,28},{28,24},{1,5},{5... | collective-permute-start | bytes 393224 | tf_op jit(solution)/shard_map/ppermute | solution.py:65
  33.2 4.3 %collective-permute-start.1 = (f32[2,8,1024]{2,1,0:T(8,128)S(1)}, f32[2,8,1024]{2,1,0:T(8,128)S(1)}, u32[]{:S(2)}, u32[]{:S(2)}) collective-permute-start(f32[2,8,1024]{2,1,0:T(8,128)S(1)} %fusion.10), channel_id=1, source_target_pairs={{0,8},{4,12},{8,0},{12,4},{16,24},{20,28},{24,16},{28,20},{1,9},{5... | collective-permute-start | bytes 196616 | tf_op jit(solution)/shard_map/ppermute | solution.py:65
  37.5 4.9 %collective-permute-start.2 = (f32[8,1024]{1,0:T(8,128)S(1)}, f32[8,1024]{1,0:T(8,128)S(1)}, u32[]{:S(2)}, u32[]{:S(2)}) collective-permute-start(f32[8,1024]{1,0:T(8,128)S(1)} %fusion.20), channel_id=1, source_target_pairs={{0,16},{4,20},{8,24},{12,28},{16,0},{20,4},{24,8},{28,12},{1,17},{... | collective-permute-start | bytes 98312 | tf_op jit(solution)/shard_map/ppermute | solution.py:65
  43.3 1.2 %collective-permute-start.3 = (f32[2,8]{1,0:T(2,128)S(1)}, f32[2,8]{1,0:T(2,128)S(1)}, u32[]{:S(2)}, u32[]{:S(2)}) collective-permute-start(f32[2,8]{1,0:T(2,128)S(1)} %pad_maximum_fusion.6), channel_id=1, source_target_pairs={{0,1},{1,0},{2,3},{3,2},{4,5},{5,4},{6,7},{7,6},{8,9},{9,8},{10,11... | collective-permute-start | bytes 200 | tf_op jit(solution)/shard_map/ppermute | solution.py:24
  44.6 3.6 %collective-permute-start.4 = (f32[2,8]{1,0:T(2,128)S(1)}, f32[2,8]{1,0:T(2,128)S(1)}, u32[]{:S(2)}, u32[]{:S(2)}) collective-permute-start(f32[2,8]{1,0:T(2,128)S(1)} %select_add_fusion.3), channel_id=1, source_target_pairs={{0,2},{1,3},{2,0},{3,1},{4,6},{5,7},{6,4},{7,5},{8,10},{9,11},{10,... | collective-permute-start | bytes 200 | tf_op jit(solution)/shard_map/ppermute | solution.py:24
  49.0 4.7 %collective-permute-start.5 = (bf16[1,8,1024]{2,1,0:T(8,128)(2,1)S(1)}, bf16[1,8,1024]{2,1,0:T(8,128)(2,1)S(1)}, u32[]{:S(2)}, u32[]{:S(2)}) collective-permute-start(bf16[1,8,1024]{2,1,0:T(8,128)(2,1)S(1)} %fusion.21), channel_id=1, source_target_pairs={{0,16},{4,20},{8,24},{12,28},{16,0},{20,4},{24,8},{28,12},{1,17},{... | collective-permute-start | bytes 49160 | tf_op jit(solution)/shard_map/ppermute | solution.py:35
  53.7 4.0 %collective-permute-start.6 = (bf16[2,8,1024]{2,1,0:T(8,128)(2,1)S(1)}, bf16[2,8,1024]{2,1,0:T(8,128)(2,1)S(1)}, u32[]{:S(2)}, u32[]{:S(2)}) collective-permute-start(bf16[2,8,1024]{2,1,0:T(8,128)(2,1)S(1)} %maximum_select_fusion.4), channel_id=1, source_target_pairs={{0,8},{4,12},{8,0},{12,4},{16,24},{20,28},{24,16},{28,20},{1,9},{5... | collective-permute-start | bytes 98312 | tf_op jit(solution)/shard_map/ppermute | solution.py:35
  57.7 4.3 %collective-permute-start.7 = (bf16[4,8,1024]{2,1,0:T(8,128)(2,1)S(1)}, bf16[4,8,1024]{2,1,0:T(8,128)(2,1)S(1)}, u32[]{:S(2)}, u32[]{:S(2)}) collective-permute-start(bf16[4,8,1024]{2,1,0:T(8,128)(2,1)S(1)} %maximum_select_fusion.3), channel_id=1, source_target_pairs={{0,4},{4,0},{8,12},{12,8},{16,20},{20,16},{24,28},{28,24},{1,5},{5... | collective-permute-start | bytes 196616 | tf_op jit(solution)/shard_map/ppermute | solution.py:35
  62.6 5.0 %collective-permute-start.8 = (bf16[1,64,1024]{2,1,0:T(8,128)(2,1)S(1)}, bf16[1,64,1024]{2,1,0:T(8,128)(2,1)S(1)}, u32[]{:S(2)}, u32[]{:S(2)}) collective-permute-start(bf16[1,64,1024]{2,1,0:T(8,128)(2,1)S(1)} %bitcast.133), channel_id=1, source_target_pairs={{0,2},{1,3},{2,0},{3,1},{4,6},{5,7},{6,4},{7,5},{8,10},{9,11},{10,... | collective-permute-start | bytes 393224 | tf_op jit(solution)/shard_map/ppermute | solution.py:35
  67.7 1.6 %collective-permute-start.9 = (bf16[2,64,1024]{2,1,0:T(8,128)(2,1)S(1)}, bf16[2,64,1024]{2,1,0:T(8,128)(2,1)S(1)}, u32[]{:S(2)}, u32[]{:S(2)}) collective-permute-start(bf16[2,64,1024]{2,1,0:T(8,128)(2,1)S(1)} %maximum_select_fusion.1), channel_id=1, source_target_pairs={{0,1},{1,0},{2,3},{3,2},{4,5},{5,4},{6,7},{7,6},{8,9},{9,8},{10,11... | collective-permute-start | bytes 786440 | tf_op jit(solution)/shard_map/ppermute | solution.py:35
  86.1 1.2 %collective-permute-start.10 = (f32[3,64]{1,0:T(4,128)S(1)}, f32[3,64]{1,0:T(4,128)S(1)}, u32[]{:S(2)}, u32[]{:S(2)}) collective-permute-start(f32[3,64]{1,0:T(4,128)S(1)} %pad_maximum_fusion.1), channel_id=1, source_target_pairs={{0,1},{1,0},{2,3},{3,2},{4,5},{5,4},{6,7},{7,6},{8,9},{9,8},{10,11... | collective-permute-start | bytes 2312 | tf_op jit(solution)/shard_map/ppermute | solution.py:24
  87.4 3.7 %collective-permute-start.11 = (f32[3,64]{1,0:T(4,128)S(1)}, f32[3,64]{1,0:T(4,128)S(1)}, u32[]{:S(2)}, u32[]{:S(2)}) collective-permute-start(f32[3,64]{1,0:T(4,128)S(1)} %pad_maximum_fusion.2), channel_id=1, source_target_pairs={{0,2},{1,3},{2,0},{3,1},{4,6},{5,7},{6,4},{7,5},{8,10},{9,11},{10,... | collective-permute-start | bytes 2312 | tf_op jit(solution)/shard_map/ppermute | solution.py:24
  91.1 3.7 %collective-permute-start.12 = (f32[3,64]{1,0:T(4,128)S(1)}, f32[3,64]{1,0:T(4,128)S(1)}, u32[]{:S(2)}, u32[]{:S(2)}) collective-permute-start(f32[3,64]{1,0:T(4,128)S(1)} %pad_maximum_fusion.3), channel_id=1, source_target_pairs={{0,4},{4,0},{8,12},{12,8},{16,20},{20,16},{24,28},{28,24},{1,5},{5... | collective-permute-start | bytes 2312 | tf_op jit(solution)/shard_map/ppermute | solution.py:24
  94.8 3.7 %collective-permute-start.13 = (f32[3,64]{1,0:T(4,128)S(1)}, f32[3,64]{1,0:T(4,128)S(1)}, u32[]{:S(2)}, u32[]{:S(2)}) collective-permute-start(f32[3,64]{1,0:T(4,128)S(1)} %pad_maximum_fusion.4), channel_id=1, source_target_pairs={{0,8},{4,12},{8,0},{12,4},{16,24},{20,28},{24,16},{28,20},{1,9},{5... | collective-permute-start | bytes 2312 | tf_op jit(solution)/shard_map/ppermute | solution.py:24
  98.5 4.5 %collective-permute-start.14 = (f32[3,64]{1,0:T(4,128)S(1)}, f32[3,64]{1,0:T(4,128)S(1)}, u32[]{:S(2)}, u32[]{:S(2)}) collective-permute-start(f32[3,64]{1,0:T(4,128)S(1)} %pad_maximum_fusion.5), channel_id=1, source_target_pairs={{0,16},{4,20},{8,24},{12,28},{16,0},{20,4},{24,8},{28,12},{1,17},{... | collective-permute-start | bytes 2312 | tf_op jit(solution)/shard_map/ppermute | solution.py:24

commit v4 on v3

--- a/solution.py
+++ b/solution.py
@@ -121,16 +121,20 @@
     tokens = hidden.shape[0]
     onehot = (positions[0][:, None] == jnp.arange(tokens, dtype=jnp.int32)[None, :]).astype(hidden.dtype)
     picked = jnp.dot(onehot, hidden, preferred_element_type=jnp.float32).astype(hidden.dtype)
-    meta = jnp.zeros((1, model), jnp.int32)
-    meta = meta.at[0, 0].set(counts[0])
-    meta = lax.dynamic_update_slice(meta, _pieces(targets[0])[None], (0, 1))
-    listed = lax.all_gather(
-        jnp.concatenate([picked, meta.astype(hidden.dtype)]), "vocab", axis=0, tiled=False
-    )
-    listed_rows = listed[:, :slots].reshape(ways * slots, model)
-    listed_meta = listed[:, slots, : 1 + 3 * slots].astype(jnp.int32)
-    listed_counts = listed_meta[:, 0]
-    listed_tgt = _unpieces(listed_meta[:, 1:].reshape(ways, 3, slots)).reshape(ways * slots)
+    meta = jnp.zeros((in_block,), jnp.int32).at[0].set(counts[0])
+    meta = lax.dynamic_update_slice(meta, _pieces(targets[0]), (1,))
+    blocks = jnp.concatenate(
+        [
+            picked.reshape(slots, groups, in_block).transpose(1, 0, 2),
+            jnp.broadcast_to(meta.astype(hidden.dtype), (groups, 1, in_block)),
+        ],
+        axis=1,
+    )
+    got = lax.all_to_all(jnp.repeat(blocks, ways, axis=0), ("dp", "vocab"), 0, 0, tiled=True)
+    got = got.reshape(groups, ways, slots + 1, in_block)
+    slot_rows = got[:, :, :slots].reshape(groups, ways * slots, in_block)
+    got_meta = got[:, :, slots, : 1 + 3 * slots].astype(jnp.int32)
+    got_tgt = _unpieces(got_meta[:, :, 1:].reshape(groups, ways, 3, slots)).reshape(groups, ways * slots)
     slot_ids = jnp.tile(jnp.arange(slots, dtype=jnp.int32), ways)
     row_ids = jnp.arange(group_rows, dtype=jnp.int32)
 
@@ -141,19 +145,11 @@
         dest = start_of + slot_ids
         return (dest[None, :] == row_ids[:, None]) & valid[None, :]
 
-    chooser = choose(listed_counts)
-    rows = jnp.dot(
-        chooser.astype(jnp.bfloat16), listed_rows, preferred_element_type=jnp.float32
-    ).astype(jnp.bfloat16)
-    tgt = jnp.sum(jnp.where(chooser, listed_tgt[None, :], 0), axis=1).astype(jnp.int32)
-    blocks = rows.reshape(group_rows, groups, in_block).transpose(1, 0, 2)
-    tgt_row = jnp.zeros((in_block,), jnp.int32).at[: 3 * group_rows].set(_pieces(tgt))
-    tgt_rows = jnp.broadcast_to(tgt_row.astype(jnp.bfloat16), (groups, 1, in_block))
-    got = lax.all_to_all(jnp.concatenate([blocks, tgt_rows], axis=1), "dp", 0, 0, tiled=True)
-    rows_in = got[:, :group_rows].reshape(total_rows, in_block)
-    tgt_all = _unpieces(
-        got[:, group_rows, : 3 * group_rows].astype(jnp.int32).reshape(groups, 3, group_rows)
-    ).reshape(total_rows)
+    choosers = jax.vmap(choose)(got_meta[:, :, 0])
+    rows_in = jnp.einsum(
+        "grs,gsd->grd", choosers.astype(hidden.dtype), slot_rows, preferred_element_type=jnp.float32
+    ).astype(hidden.dtype).reshape(total_rows, in_block)
+    tgt_all = jnp.sum(jnp.where(choosers, got_tgt[:, None, :], 0), axis=2).reshape(total_rows)
     part = jnp.dot(rows_in, dense_weight, preferred_element_type=jnp.float32)
     if _pow2(groups):
         act = _reduce_scatter(part.reshape(groups, group_rows, -1), "dp", groups, _steps(groups))
@@ -184,14 +180,11 @@
             jnp.sum(jnp.where(hit, logits, 0.0), axis=1),
         ]
     )
-    if _pow2(ways) and _pow2(groups):
-        merged = _allreduce(_allreduce(local, "vocab", ways, _softmax_merge), "dp", groups, _softmax_merge)
-        peak, denom, target_logit = merged[0], merged[1], merged[2]
-    else:
-        peak = lax.pmax(row_max, ("dp", "vocab"))
-        denom, target_logit = lax.psum(
-            (jnp.sum(jnp.exp(logits - peak[:, None]), axis=1), local[2]), ("dp", "vocab")
-        )
+    devices = groups * ways
+    every = lax.all_to_all(jnp.broadcast_to(local[None], (devices,) + local.shape), ("dp", "vocab"), 0, 0, tiled=True)
+    peak = jnp.max(every[:, 0], axis=0)
+    denom = jnp.sum(every[:, 1] * jnp.exp(every[:, 0] - peak[None, :]), axis=0)
+    target_logit = jnp.sum(every[:, 2], axis=0)
     lse = peak + jnp.log(denom)
     row_loss = lse - target_logit
     diff = jnp.exp(logits - lse[:, None]) - hit.astype(jnp.float32)

time: 119 us -> 110 us (0.924)
  waiting for transfers between devices: 51.9 us -> 41.9 us
  starting transfers between devices: 15.3 us -> 13.3 us
  blocking collectives: 7.25 us -> 9.06 us
  local copies, waits for them, and re-layouts: 2.17 us -> 3.96 us
    ppermute x7 -> x2, waiting for transfers between devices: 16.6 us -> 3.81 us  [_allreduce(): theirs = lax.ppermute(x, axis, [(a, a ^ step) for a in range(n)])]
    all_to_all x0 -> x1, blocking collectives: none -> 9.06 us  [body(): lax.all_to_all(jnp.broadcast_to(local[None], (devices,) + local.shape), (...]
    all_gather x1 -> x0, blocking collectives: 7.25 us -> none  [body(): lax.all_gather(jnp.concatenate([picked, meta.astype(hidden.dtype)]), 'voc...]
    ppermute x7 -> x2, starting transfers between devices: 4.98 us -> 1.05 us  [_allreduce(): theirs = lax.ppermute(x, axis, [(a, a ^ step) for a in range(n)])]
    all_to_all x1, waiting for transfers between devices: 7.49 us -> 10.5 us  [body(): lax.all_to_all(jnp.repeat(blocks, ways, axis=0), ('dp', 'vocab'), 0, 0, t...]
    all_to_all x1, starting transfers between devices: 5.81 us -> 7.33 us  [body(): lax.all_to_all(jnp.repeat(blocks, ways, axis=0), ('dp', 'vocab'), 0, 0, t...]
    ppermute x3, starting transfers between devices: 1.35 us -> 2.61 us  [_reduce_scatter(): theirs = lax.ppermute(sent, axis, [(a, a ^ step) for a in range(n)])]
  transfers between devices with their start and end apart: 16 -> 11, of which waited for: 16 -> 11; matrix products, arithmetic and copies ran while one was open for 1% -> 2% of each run, Pallas kernels for 0% -> 0%
where the time goes in v4:
time: 110 us; the launch traced here: 109 us
  waiting for transfers between devices  41.9 us (38%)
  matrix products  32.2 us (29%)
  starting transfers between devices  13.3 us (12%)
  blocking collectives  9.06 us (8%)
  other arithmetic  7.2 us (7%)
  local copies, waits for them, and re-layouts  3.96 us (4%)
  between operations  1.57 us (1%)
    dot_general x1, matrix products, body(): jnp.einsum('rd,vd->rv', head_all, embedding, preferred_element_type=jnp.f...  15.7 us
    ppermute x5, waiting for transfers between devices, _allgather(): theirs = lax.ppermute(buf, axis, [(a, a ^ step) for a in range(n)])  15.3 us
    dot_general x1, matrix products, body(): jnp.einsum('rv,rd->vd', grad, head_all, preferred_element_type=jnp.float32)  14.5 us
    ppermute x3, waiting for transfers between devices, _reduce_scatter(): theirs = lax.ppermute(sent, axis, [(a, a ^ step) for a in range(n)])  12.3 us
    all_to_all x1, waiting for transfers between devices, body(): lax.all_to_all(jnp.repeat(blocks, ways, axis=0), ('dp', 'vocab'), 0, 0, t...  10.5 us
    all_to_all x1, blocking collectives, body(): lax.all_to_all(jnp.broadcast_to(local[None], (devices,) + local.shape), (...  9.06 us
    all_to_all x1, starting transfers between devices, body(): lax.all_to_all(jnp.repeat(blocks, ways, axis=0), ('dp', 'vocab'), 0, 0, t...  7.33 us
    ppermute x2, waiting for transfers between devices, _allreduce(): theirs = lax.ppermute(x, axis, [(a, a ^ step) for a in range(n)])  3.81 us
  transfers between devices with their start and end apart: 11, of which 11 were waited for; matrix products, arithmetic and copies ran while one was open for 2% of the time, Pallas kernels for 0%

profile of v4, /device:TPU:0, one launch (start us, length us, event | category | flops | bytes accessed | tf_op | source)
XLA Modules:
  0.0 109.2 jit_solution(7199905612260917449)
XLA Ops:
  0.6 0.0 copy-start
  0.6 0.7 shift-right-arithmetic_bitcast_fusion
  2.1 0.2 add_dynamic-update-slice_fusion
  2.2 1.5 %convolution_convert_fusion.1 = bf16[6,4096]{1,0:T(8,128)(2,1)S(1)} fusion(bf16[128,4096]{1,0:T(8,128)(2,1)} %param.26, s32[6]{0:T(128)} %bitcast.136), kind=kOutput, calls=%fused_computation.4 | convolution fusion | flops 6316800 | bytes 1097752 | tf_op jit(solution)/shard_map/dot_general | solution.py:123
  3.9 0.7 broadcast_in_dim.51
  4.6 7.3 %all-to-all-start = ((bf16[32,7,512]{2,1,0:T(8,128)(2,1)}), bf16[32,7,512]{2,1,0:T(8,128)(2,1)S(1)}, u32[]{:S(2)}, u32[]{:S(2)}) async-start(bf16[32,7,512]{2,1,0:T(8,128)(2,1)} %bitcast.5), calls=%async_computation | async-start | bytes 524288 | tf_op jit(solution)/shard_map/all_to_all | solution.py:133
  11.9 0.1 add.118
  12.0 10.5 %all-to-all-done = bf16[32,7,512]{2,1,0:T(8,128)(2,1)S(1)} async-done(((bf16[32,7,512]{2,1,0:T(8,128)(2,1)}), bf16[32,7,512]{2,1,0:T(8,128)(2,1)S(1)}, u32[]{:S(2)}, u32[]{:S(2)}) %all-to-all-start) | async-done | bytes 229408 | tf_op jit(solution)/shard_map/all_to_all | solution.py:133
  22.5 0.1 copy.71
  22.7 0.1 copy.73
  22.8 0.1 copy.72
  22.8 0.1 broadcast_in_dim.52
  22.9 0.1 reshape.175
  23.0 0.1 broadcast_in_dim.53
  23.1 0.1 reshape.176
  23.2 0.1 copy.74
  23.3 0.2 convolution_convert_fusion.2
  23.5 0.0 copy-done
  23.5 0.3 fusion.2
  23.8 1.0 collective-permute-start
  24.8 4.4 %collective-permute-done = f32[2,2,8,1024]{3,2,1,0:T(8,128)S(1)} collective-permute-done((f32[2,2,8,1024]{3,2,1,0:T(8,128)S(1)}, f32[2,2,8,1024]{3,2,1,0:T(8,128)S(1)}, u32[]{:S(2)}, u32[]{:S(2)}) %collective-permute-start) | collective-permute-done | bytes 131104 | tf_op jit(solution)/shard_map/ppermute | solution.py:65
  29.3 0.6 collective-permute-start.1
  29.9 3.7 %collective-permute-done.1 = f32[2,8,1024]{2,1,0:T(8,128)S(1)} collective-permute-done((f32[2,8,1024]{2,1,0:T(8,128)S(1)}, f32[2,8,1024]{2,1,0:T(8,128)S(1)}, u32[]{:S(2)}, u32[]{:S(2)}) %collective-permute-start.1) | collective-permute-done | bytes 65568 | tf_op jit(solution)/shard_map/ppermute | solution.py:65
  33.6 1.0 collective-permute-start.2
  34.6 4.2 %collective-permute-done.2 = f32[8,1024]{1,0:T(8,128)S(1)} collective-permute-done((f32[8,1024]{1,0:T(8,128)S(1)}, f32[8,1024]{1,0:T(8,128)S(1)}, u32[]{:S(2)}, u32[]{:S(2)}) %collective-permute-start.2) | collective-permute-done | bytes 32800 | tf_op jit(solution)/shard_map/ppermute | solution.py:65
  38.9 0.9 fusion.33
  39.8 0.1 collective-permute-start.3
  39.9 1.1 %collective-permute-done.3 = f32[2,8]{1,0:T(2,128)S(1)} collective-permute-done((f32[2,8]{1,0:T(2,128)S(1)}, f32[2,8]{1,0:T(2,128)S(1)}, u32[]{:S(2)}, u32[]{:S(2)}) %collective-permute-start.3) | collective-permute-done | bytes 96 | tf_op jit(solution)/shard_map/ppermute | solution.py:24
  41.0 1.0 collective-permute-start.4
  42.0 2.7 %collective-permute-done.4 = f32[2,8]{1,0:T(2,128)S(1)} collective-permute-done((f32[2,8]{1,0:T(2,128)S(1)}, f32[2,8]{1,0:T(2,128)S(1)}, u32[]{:S(2)}, u32[]{:S(2)}) %collective-permute-start.4) | collective-permute-done | bytes 96 | tf_op jit(solution)/shard_map/ppermute | solution.py:24
  44.7 0.8 fusion.24
  45.5 0.6 collective-permute-start.5
  46.1 4.0 %collective-permute-done.5 = bf16[1,8,1024]{2,1,0:T(8,128)(2,1)S(1)} collective-permute-done((bf16[1,8,1024]{2,1,0:T(8,128)(2,1)S(1)}, bf16[1,8,1024]{2,1,0:T(8,128)(2,1)S(1)}, u32[]{:S(2)}, u32[]{:S(2)}) %collective-permute-start.5) | collective-permute-done | bytes 16416 | tf_op jit(solution)/shard_map/ppermute | solution.py:35
  50.2 0.4 collective-permute-start.6
  50.5 3.6 %collective-permute-done.6 = bf16[2,8,1024]{2,1,0:T(8,128)(2,1)S(1)} collective-permute-done((bf16[2,8,1024]{2,1,0:T(8,128)(2,1)S(1)}, bf16[2,8,1024]{2,1,0:T(8,128)(2,1)S(1)}, u32[]{:S(2)}, u32[]{:S(2)}) %collective-permute-start.6) | collective-permute-done | bytes 32800 | tf_op jit(solution)/shard_map/ppermute | solution.py:35
  54.2 0.3 collective-permute-start.7
  54.4 0.7 pad_clamp_fusion.1
  55.1 3.4 %collective-permute-done.7 = bf16[4,8,1024]{2,1,0:T(8,128)(2,1)S(1)} collective-permute-done((bf16[4,8,1024]{2,1,0:T(8,128)(2,1)S(1)}, bf16[4,8,1024]{2,1,0:T(8,128)(2,1)S(1)}, u32[]{:S(2)}, u32[]{:S(2)}) %collective-permute-start.7) | collective-permute-done | bytes 65568 | tf_op jit(solution)/shard_map/ppermute | solution.py:35
  58.5 0.6 gather_fusion
  59.1 1.0 collective-permute-start.8
  60.1 0.7 pad_clamp_fusion
  60.7 0.1 slice.149
  60.8 0.1 copy.79
  60.9 3.2 %collective-permute-done.8 = bf16[1,64,1024]{2,1,0:T(8,128)(2,1)S(1)} collective-permute-done((bf16[1,64,1024]{2,1,0:T(8,128)(2,1)S(1)}, bf16[1,64,1024]{2,1,0:T(8,128)(2,1)S(1)}, u32[]{:S(2)}, u32[]{:S(2)}) %collective-permute-start.8) | collective-permute-done | bytes 131104 | tf_op jit(solution)/shard_map/ppermute | solution.py:35
  64.1 0.1 collective-permute-start.9
  64.2 0.1 copy.80
  64.3 0.1 add.137
  64.4 0.2 select_reduce_fusion
  64.6 0.1 eq.50
  64.7 1.0 collective-permute-done.9
  65.7 0.1 maximum_select_fusion
  65.8 0.6 gather_fusion.1
  66.5 15.7 %fusion.37 = (f32[64]{0:T(128)S(1)}, f32[64,4096]{1,0:T(8,128)S(1)}) fusion(f32[4096]{0:T(1024)} %param.35, bf16[64,4096]{1,0:T(8,128)(2,1)S(1)} %bitcast.108, bf16[4096,4096]{1,0:T(8,128)(2,1)} %param.34), kind=kOutput, calls=%fused_computation.98 | convolution fusion | flops 2148007936 | bytes 35143936 | tf_op jit(solution)/shard_map/rd,vd->rv/dot_general | solution.py:171
  82.1 0.4 exponential_reduce_fusion
  82.6 0.1 reshape.350
  82.7 9.1 %all_to_all.10 = f32[32,1,192]{2,1,0:T(1,128)S(1)} all-to-all(f32[32,1,192]{2,1,0:T(1,128)S(1)} %reshape.350), channel_id=1, replica_groups=mesh['dp'=8,'vocab'=4] {'dp','vocab'}, dimensions={0} | all-to-all | bytes 49152 | tf_op jit(solution)/shard_map/all_to_all | solution.py:184
  91.8 0.5 broadcast.241
  92.3 0.7 reduce.4
  93.0 0.1 reshape.351
  93.2 0.5 fusion.34
  93.8 14.5 %convolution_convert_fusion = bf16[4096,4096]{1,0:T(8,128)(2,1)} fusion(bf16[64,4096]{1,0:T(8,128)(2,1)S(1)} %bitcast.109, f32[64,4096]{1,0:T(8,128)S(1)} %get-tuple-element.101, f32[64]{0:T(128)S(1)} %get-tuple-element.92, s32[4096]{0:T(1024)S(1)} %iota_add_fusion, s32[64]{0:T(128)S(1)} %eq.50), kind=kOutput, calls=%fused_computation.2 | convolution fusion | flops 2165833728 | bytes 35144192 | tf_op jit(solution)/shard_map/rv,rd->vd/dot_general | solution.py:192
  108.2 0.3 fusion.4
  108.6 0.6 broadcast_multiply_fusion
  (36 shorter events, 0.5 us)
Async XLA Ops:
  0.6 22.9 %copy-start = (bf16[512,1024]{1,0:T(8,128)(2,1)S(1)}, bf16[512,1024]{1,0:T(8,128)(2,1)}, u32[]{:S(2)}) copy-start(bf16[512,1024]{1,0:T(8,128)(2,1)} %param.30) | copy-start | bytes 3145732
  4.6 17.9 %all-to-all-start = ((bf16[32,7,512]{2,1,0:T(8,128)(2,1)}), bf16[32,7,512]{2,1,0:T(8,128)(2,1)S(1)}, u32[]{:S(2)}, u32[]{:S(2)}) async-start(bf16[32,7,512]{2,1,0:T(8,128)(2,1)} %bitcast.5), calls=%async_computation | async-start | bytes 524288 | tf_op jit(solution)/shard_map/all_to_all | solution.py:133
  23.8 5.4 %collective-permute-start = (f32[2,2,8,1024]{3,2,1,0:T(8,128)S(1)}, f32[2,2,8,1024]{3,2,1,0:T(8,128)S(1)}, u32[]{:S(2)}, u32[]{:S(2)}) collective-permute-start(f32[2,2,8,1024]{3,2,1,0:T(8,128)S(1)} %fusion.10), channel_id=1, source_target_pairs={{0,4},{4,0},{8,12},{12,8},{16,20},{20,16},{24,28},{28,24},{1,5},{5... | collective-permute-start | bytes 393224 | tf_op jit(solution)/shard_map/ppermute | solution.py:65
  29.3 4.3 %collective-permute-start.1 = (f32[2,8,1024]{2,1,0:T(8,128)S(1)}, f32[2,8,1024]{2,1,0:T(8,128)S(1)}, u32[]{:S(2)}, u32[]{:S(2)}) collective-permute-start(f32[2,8,1024]{2,1,0:T(8,128)S(1)} %fusion.11), channel_id=1, source_target_pairs={{0,8},{4,12},{8,0},{12,4},{16,24},{20,28},{24,16},{28,20},{1,9},{5... | collective-permute-start | bytes 196616 | tf_op jit(solution)/shard_map/ppermute | solution.py:65
  33.6 5.2 %collective-permute-start.2 = (f32[8,1024]{1,0:T(8,128)S(1)}, f32[8,1024]{1,0:T(8,128)S(1)}, u32[]{:S(2)}, u32[]{:S(2)}) collective-permute-start(f32[8,1024]{1,0:T(8,128)S(1)} %fusion.23), channel_id=1, source_target_pairs={{0,16},{4,20},{8,24},{12,28},{16,0},{20,4},{24,8},{28,12},{1,17},{... | collective-permute-start | bytes 98312 | tf_op jit(solution)/shard_map/ppermute | solution.py:65
  39.8 1.2 %collective-permute-start.3 = (f32[2,8]{1,0:T(2,128)S(1)}, f32[2,8]{1,0:T(2,128)S(1)}, u32[]{:S(2)}, u32[]{:S(2)}) collective-permute-start(f32[2,8]{1,0:T(2,128)S(1)} %pad_maximum_fusion.2), channel_id=1, source_target_pairs={{0,1},{1,0},{2,3},{3,2},{4,5},{5,4},{6,7},{7,6},{8,9},{9,8},{10,11... | collective-permute-start | bytes 200 | tf_op jit(solution)/shard_map/ppermute | solution.py:24
  41.0 3.6 %collective-permute-start.4 = (f32[2,8]{1,0:T(2,128)S(1)}, f32[2,8]{1,0:T(2,128)S(1)}, u32[]{:S(2)}, u32[]{:S(2)}) collective-permute-start(f32[2,8]{1,0:T(2,128)S(1)} %select_add_fusion.3), channel_id=1, source_target_pairs={{0,2},{1,3},{2,0},{3,1},{4,6},{5,7},{6,4},{7,5},{8,10},{9,11},{10,... | collective-permute-start | bytes 200 | tf_op jit(solution)/shard_map/ppermute | solution.py:24
  45.5 4.7 %collective-permute-start.5 = (bf16[1,8,1024]{2,1,0:T(8,128)(2,1)S(1)}, bf16[1,8,1024]{2,1,0:T(8,128)(2,1)S(1)}, u32[]{:S(2)}, u32[]{:S(2)}) collective-permute-start(bf16[1,8,1024]{2,1,0:T(8,128)(2,1)S(1)} %fusion.24), channel_id=1, source_target_pairs={{0,16},{4,20},{8,24},{12,28},{16,0},{20,4},{24,8},{28,12},{1,17},{... | collective-permute-start | bytes 49160 | tf_op jit(solution)/shard_map/ppermute | solution.py:35
  50.2 4.0 %collective-permute-start.6 = (bf16[2,8,1024]{2,1,0:T(8,128)(2,1)S(1)}, bf16[2,8,1024]{2,1,0:T(8,128)(2,1)S(1)}, u32[]{:S(2)}, u32[]{:S(2)}) collective-permute-start(bf16[2,8,1024]{2,1,0:T(8,128)(2,1)S(1)} %maximum_select_fusion.4), channel_id=1, source_target_pairs={{0,8},{4,12},{8,0},{12,4},{16,24},{20,28},{24,16},{28,20},{1,9},{5... | collective-permute-start | bytes 98312 | tf_op jit(solution)/shard_map/ppermute | solution.py:35
  54.2 4.3 %collective-permute-start.7 = (bf16[4,8,1024]{2,1,0:T(8,128)(2,1)S(1)}, bf16[4,8,1024]{2,1,0:T(8,128)(2,1)S(1)}, u32[]{:S(2)}, u32[]{:S(2)}) collective-permute-start(bf16[4,8,1024]{2,1,0:T(8,128)(2,1)S(1)} %maximum_select_fusion.3), channel_id=1, source_target_pairs={{0,4},{4,0},{8,12},{12,8},{16,20},{20,16},{24,28},{28,24},{1,5},{5... | collective-permute-start | bytes 196616 | tf_op jit(solution)/shard_map/ppermute | solution.py:35
  59.1 5.0 %collective-permute-start.8 = (bf16[1,64,1024]{2,1,0:T(8,128)(2,1)S(1)}, bf16[1,64,1024]{2,1,0:T(8,128)(2,1)S(1)}, u32[]{:S(2)}, u32[]{:S(2)}) collective-permute-start(bf16[1,64,1024]{2,1,0:T(8,128)(2,1)S(1)} %bitcast.114), channel_id=1, source_target_pairs={{0,2},{1,3},{2,0},{3,1},{4,6},{5,7},{6,4},{7,5},{8,10},{9,11},{10,... | collective-permute-start | bytes 393224 | tf_op jit(solution)/shard_map/ppermute | solution.py:35
  64.1 1.6 %collective-permute-start.9 = (bf16[2,64,1024]{2,1,0:T(8,128)(2,1)S(1)}, bf16[2,64,1024]{2,1,0:T(8,128)(2,1)S(1)}, u32[]{:S(2)}, u32[]{:S(2)}) collective-permute-start(bf16[2,64,1024]{2,1,0:T(8,128)(2,1)S(1)} %maximum_select_fusion.1), channel_id=1, source_target_pairs={{0,1},{1,0},{2,3},{3,2},{4,5},{5,4},{6,7},{7,6},{8,9},{9,8},{10,11... | collective-permute-start | bytes 786440 | tf_op jit(solution)/shard_map/ppermute | solution.py:35

commit v5 on v4

--- a/solution.py
+++ b/solution.py
@@ -151,10 +151,7 @@
     ).astype(hidden.dtype).reshape(total_rows, in_block)
     tgt_all = jnp.sum(jnp.where(choosers, got_tgt[:, None, :], 0), axis=2).reshape(total_rows)
     part = jnp.dot(rows_in, dense_weight, preferred_element_type=jnp.float32)
-    if _pow2(groups):
-        act = _reduce_scatter(part.reshape(groups, group_rows, -1), "dp", groups, _steps(groups))
-    else:
-        act = lax.psum_scatter(part.reshape(groups, group_rows, -1), "dp", scatter_dimension=0, tiled=True)[0]
+    act = jnp.sum(lax.all_to_all(part.reshape(groups, group_rows, -1), "dp", 0, 0, tiled=True), axis=0)
     act = jax.nn.gelu(act + dense_bias, approximate=False)
     stats = _psum(jnp.stack([jnp.sum(act, axis=1), jnp.sum(act * act, axis=1)]), "vocab", ways)
     mean = stats[0] / model
@@ -162,8 +159,11 @@
     head_rows = (
         (act - mean[:, None]) * lax.rsqrt(var + EPS)[:, None] * norm_gain + norm_shift
     ).astype(jnp.bfloat16)
-    head_cols = _gather(head_rows, "dp", groups, _steps(groups)[::-1]).reshape(total_rows, -1)
-    head_all = _gather(head_cols, "vocab", ways, _steps(ways)[::-1]).transpose(1, 0, 2).reshape(total_rows, model)
+    devices = groups * ways
+    every_head = lax.all_to_all(
+        jnp.broadcast_to(head_rows[None], (devices,) + head_rows.shape), ("dp", "vocab"), 0, 0, tiled=True
+    )
+    head_all = every_head.reshape(groups, ways, group_rows, -1).transpose(0, 2, 1, 3).reshape(total_rows, model)
     vocab_rows = embedding.shape[0]
     first_id = (lax.axis_index("dp") * ways + lax.axis_index("vocab")) * vocab_rows
     ids = first_id + jnp.arange(vocab_rows, dtype=jnp.int32)
@@ -180,7 +180,6 @@
             jnp.sum(jnp.where(hit, logits, 0.0), axis=1),
         ]
     )
-    devices = groups * ways
     every = lax.all_to_all(jnp.broadcast_to(local[None], (devices,) + local.shape), ("dp", "vocab"), 0, 0, tiled=True)
     peak = jnp.max(every[:, 0], axis=0)
     denom = jnp.sum(every[:, 1] * jnp.exp(every[:, 0] - peak[None, :]), axis=0)

time: 110 us -> 107 us (0.973)
  waiting for transfers between devices: 41.9 us -> 38.4 us
  other arithmetic: 7.2 us -> 5.69 us
  starting transfers between devices: 13.3 us -> 14.8 us
    ppermute x8 -> x0, waiting for transfers between devices: 27.6 us -> none  [the longest x5 15.3 us: _allgather(): theirs = lax.ppermute(buf, axis, [(a, a ^ step) for a in range(n)])]
    all_to_all x0 -> x2, waiting for transfers between devices: none -> 24.1 us  [the longest x1 14.9 us: body(): lax.all_to_all(jnp.broadcast_to(head_rows[None], (devices,) + head_rows.s...]
    all_to_all x0 -> x2, starting transfers between devices: none -> 6.4 us  [the longest x1 3.41 us: body(): lax.all_to_all(part.reshape(groups, group_rows, -1), 'dp', 0, 0, tiled=True)]
    ppermute x8 -> x0, starting transfers between devices: 4.94 us -> none  [the longest x3 2.61 us: _reduce_scatter(): theirs = lax.ppermute(sent, axis, [(a, a ^ step) for a in range(n)])]
    gather x2 -> x0, other arithmetic: 1.32 us -> none  [_allgather(): buf = buf[jnp.array(place, dtype=jnp.int32)]]
    gather x2 -> x0, local copies, waits for them, and re-layouts: 1.14 us -> none  [_allgather(): buf = buf[jnp.array(place, dtype=jnp.int32)]]
  transfers between devices with their start and end apart: 11 -> 5, of which waited for: 11 -> 5; matrix products, arithmetic and copies ran while one was open for 2% -> 1% of each run, Pallas kernels for 0% -> 0%
where the time goes in v5:
time: 107 us
  waiting for transfers between devices  38.4 us (36%)
  matrix products  32.8 us (31%)
  starting transfers between devices  14.8 us (14%)
  blocking collectives  10 us (9%)
  other arithmetic  5.69 us (5%)
  local copies, waits for them, and re-layouts  3.64 us (3%)
  between operations  1.52 us (1%)
    dot_general x1, matrix products, body(): jnp.einsum('rd,vd->rv', head_all, embedding, preferred_element_type=jnp.f...  15.7 us
    all_to_all x1, waiting for transfers between devices, body(): lax.all_to_all(jnp.broadcast_to(head_rows[None], (devices,) + head_rows.s...  14.9 us
    dot_general x1, matrix products, body(): jnp.einsum('rv,rd->vd', grad, head_all, preferred_element_type=jnp.float32)  14.5 us
    all_to_all x1, waiting for transfers between devices, body(): lax.all_to_all(jnp.repeat(blocks, ways, axis=0), ('dp', 'vocab'), 0, 0, t...  10.5 us
    all_to_all x1, blocking collectives, body(): lax.all_to_all(jnp.broadcast_to(local[None], (devices,) + local.shape), (...  10 us
    all_to_all x1, waiting for transfers between devices, body(): lax.all_to_all(part.reshape(groups, group_rows, -1), 'dp', 0, 0, tiled=True)  9.21 us
    all_to_all x1, starting transfers between devices, body(): lax.all_to_all(jnp.repeat(blocks, ways, axis=0), ('dp', 'vocab'), 0, 0, t...  7.33 us
    ppermute x2, waiting for transfers between devices, _allreduce(): theirs = lax.ppermute(x, axis, [(a, a ^ step) for a in range(n)])  3.81 us
  transfers between devices with their start and end apart: 5, of which 5 were waited for; matrix products, arithmetic and copies ran while one was open for 1% of the time, Pallas kernels for 0%

profile of v5, /device:TPU:0, one launch (start us, length us, event | category | flops | bytes accessed | tf_op | source)
XLA Modules:
  0.0 106.8 jit_solution(3867139527195731906)
XLA Ops:
  0.6 0.0 copy-start
  0.6 0.7 shift-right-arithmetic_bitcast_fusion
  2.1 0.2 add_dynamic-update-slice_fusion
  2.2 1.5 %convolution_convert_fusion.1 = bf16[6,4096]{1,0:T(8,128)(2,1)S(1)} fusion(bf16[128,4096]{1,0:T(8,128)(2,1)} %param.12, s32[6]{0:T(128)} %bitcast.85), kind=kOutput, calls=%fused_computation.2 | convolution fusion | flops 6316800 | bytes 1097752 | tf_op jit(solution)/shard_map/dot_general | solution.py:123
  3.9 0.7 broadcast_in_dim.28
  4.6 7.3 %all-to-all-start = ((bf16[32,7,512]{2,1,0:T(8,128)(2,1)}), bf16[32,7,512]{2,1,0:T(8,128)(2,1)S(1)}, u32[]{:S(2)}, u32[]{:S(2)}) async-start(bf16[32,7,512]{2,1,0:T(8,128)(2,1)} %bitcast.5), calls=%async_computation | async-start | bytes 524288 | tf_op jit(solution)/shard_map/all_to_all | solution.py:133
  11.9 0.1 add.105
  12.0 10.5 %all-to-all-done = bf16[32,7,512]{2,1,0:T(8,128)(2,1)S(1)} async-done(((bf16[32,7,512]{2,1,0:T(8,128)(2,1)}), bf16[32,7,512]{2,1,0:T(8,128)(2,1)S(1)}, u32[]{:S(2)}, u32[]{:S(2)}) %all-to-all-start) | async-done | bytes 229408 | tf_op jit(solution)/shard_map/all_to_all | solution.py:133
  22.5 0.1 copy.54
  22.7 0.1 copy.56
  22.8 0.1 copy.55
  22.8 0.1 broadcast_in_dim.29
  22.9 0.1 reshape.312
  23.0 0.1 broadcast_in_dim.31
  23.1 0.1 reshape.313
  23.2 0.1 copy.57
  23.3 0.0 copy-done
  23.3 1.1 %fusion = f32[8,8,1024]{2,1,0:T(8,128)} fusion(bf16[512,1024]{1,0:T(8,128)(2,1)S(1)} %copy-done, bf16[8,24,512]{2,0,1:T(8,128)(2,1)S(1)} %bitcast.65, s32[8,24]{1,0:T(8,128)S(1)} %broadcast_add_fusion, pred[8,24]{1,0:T(8,128)(4,1)S(1)} %broadcast_compare_fusion), kind=kOutput, calls=%fused_computation.6 | convolution fusion | flops 68717568 | bytes 1508288 | tf_op jit(solution)/shard_map/dot_general | solution.py:153
  24.4 3.4 %all-to-all-start.1 = ((f32[8,8,1024]{2,1,0:T(8,128)}), f32[8,8,1024]{2,1,0:T(8,128)S(1)}, u32[]{:S(2)}, u32[]{:S(2)}) async-start(f32[8,8,1024]{2,1,0:T(8,128)} %fusion), calls=%async_computation.1 | async-start | bytes 524288 | tf_op jit(solution)/shard_map/all_to_all | solution.py:154
  27.8 9.2 %all-to-all-done.1 = f32[8,8,1024]{2,1,0:T(8,128)S(1)} async-done(((f32[8,8,1024]{2,1,0:T(8,128)}), f32[8,8,1024]{2,1,0:T(8,128)S(1)}, u32[]{:S(2)}, u32[]{:S(2)}) %all-to-all-start.1) | async-done | bytes 262176 | tf_op jit(solution)/shard_map/all_to_all | solution.py:154
  37.1 0.9 fusion.33
  38.0 0.1 collective-permute-start
  38.1 1.1 %collective-permute-done = f32[2,8]{1,0:T(2,128)S(1)} collective-permute-done((f32[2,8]{1,0:T(2,128)S(1)}, f32[2,8]{1,0:T(2,128)S(1)}, u32[]{:S(2)}, u32[]{:S(2)}) %collective-permute-start) | collective-permute-done | bytes 96 | tf_op jit(solution)/shard_map/ppermute | solution.py:24
  39.2 1.0 collective-permute-start.1
  40.2 2.7 %collective-permute-done.1 = f32[2,8]{1,0:T(2,128)S(1)} collective-permute-done((f32[2,8]{1,0:T(2,128)S(1)}, f32[2,8]{1,0:T(2,128)S(1)}, u32[]{:S(2)}, u32[]{:S(2)}) %collective-permute-start.1) | collective-permute-done | bytes 96 | tf_op jit(solution)/shard_map/ppermute | solution.py:24
  42.9 0.8 add_convert_fusion
  43.7 0.9 broadcast_in_dim.32
  44.5 3.0 %all-to-all-start.2 = ((bf16[32,8,1024]{2,1,0:T(8,128)(2,1)}), bf16[32,8,1024]{2,1,0:T(8,128)(2,1)S(1)}, u32[]{:S(2)}, u32[]{:S(2)}) async-start(bf16[32,8,1024]{2,1,0:T(8,128)(2,1)} %broadcast_in_dim.32), calls=%async_computation.2 | async-start | bytes 1048576 | tf_op jit(solution)/shard_map/all_to_all | solution.py:163
  47.6 0.1 slice.61
  47.6 0.1 copy.59
  47.8 0.1 copy.60
  47.9 0.1 add.119
  48.0 0.2 select_reduce_fusion
  48.2 0.1 eq.50
  48.2 14.9 %all-to-all-done.2 = bf16[32,8,1024]{2,1,0:T(8,128)(2,1)S(1)} async-done(((bf16[32,8,1024]{2,1,0:T(8,128)(2,1)}), bf16[32,8,1024]{2,1,0:T(8,128)(2,1)S(1)}, u32[]{:S(2)}, u32[]{:S(2)}) %all-to-all-start.2) | async-done | bytes 524320 | tf_op jit(solution)/shard_map/all_to_all | solution.py:163
  63.2 15.7 %fusion.37 = (f32[64]{0:T(128)S(1)}, f32[64,4096]{1,0:T(8,128)S(1)}) fusion(f32[4096]{0:T(1024)} %param.21, bf16[64,4096]{1,0:T(8,128)(2,1)S(1)} %bitcast.61, bf16[4096,4096]{1,0:T(8,128)(2,1)} %param.20), kind=kOutput, calls=%fused_computation.76 | convolution fusion | flops 2148007936 | bytes 35143936 | tf_op jit(solution)/shard_map/rd,vd->rv/dot_general | solution.py:171
  78.8 0.4 exponential_reduce_fusion
  79.3 0.1 reshape.320
  79.4 10.0 %all_to_all.20 = f32[32,1,192]{2,1,0:T(1,128)S(1)} all-to-all(f32[32,1,192]{2,1,0:T(1,128)S(1)} %reshape.320), channel_id=1, replica_groups=mesh['dp'=8,'vocab'=4] {'dp','vocab'}, dimensions={0} | all-to-all | bytes 49152 | tf_op jit(solution)/shard_map/all_to_all | solution.py:183
  89.4 0.5 broadcast.302
  89.9 0.7 reduce.4
  90.7 0.1 reshape.321
  90.9 0.5 fusion.34
  91.4 14.5 %convolution_convert_fusion = bf16[4096,4096]{1,0:T(8,128)(2,1)} fusion(bf16[64,4096]{1,0:T(8,128)(2,1)S(1)} %bitcast.62, f32[64,4096]{1,0:T(8,128)S(1)} %get-tuple-element.29, f32[64]{0:T(128)S(1)} %get-tuple-element.20, s32[4096]{0:T(1024)S(1)} %iota_add_fusion, s32[64]{0:T(128)S(1)} %eq.50), kind=kOutput, calls=%fused_computation | convolution fusion | flops 2165833728 | bytes 35144192 | tf_op jit(solution)/shard_map/rv,rd->vd/dot_general | solution.py:191
  105.9 0.3 fusion.4
  106.2 0.6 broadcast_multiply_fusion
  (27 shorter events, 0.4 us)
Async XLA Ops:
  0.6 22.7 %copy-start = (bf16[512,1024]{1,0:T(8,128)(2,1)S(1)}, bf16[512,1024]{1,0:T(8,128)(2,1)}, u32[]{:S(2)}) copy-start(bf16[512,1024]{1,0:T(8,128)(2,1)} %param.16) | copy-start | bytes 3145732
  4.6 17.9 %all-to-all-start = ((bf16[32,7,512]{2,1,0:T(8,128)(2,1)}), bf16[32,7,512]{2,1,0:T(8,128)(2,1)S(1)}, u32[]{:S(2)}, u32[]{:S(2)}) async-start(bf16[32,7,512]{2,1,0:T(8,128)(2,1)} %bitcast.5), calls=%async_computation | async-start | bytes 524288 | tf_op jit(solution)/shard_map/all_to_all | solution.py:133
  24.4 12.6 %all-to-all-start.1 = ((f32[8,8,1024]{2,1,0:T(8,128)}), f32[8,8,1024]{2,1,0:T(8,128)S(1)}, u32[]{:S(2)}, u32[]{:S(2)}) async-start(f32[8,8,1024]{2,1,0:T(8,128)} %fusion), calls=%async_computation.1 | async-start | bytes 524288 | tf_op jit(solution)/shard_map/all_to_all | solution.py:154
  38.0 1.2 %collective-permute-start = (f32[2,8]{1,0:T(2,128)S(1)}, f32[2,8]{1,0:T(2,128)S(1)}, u32[]{:S(2)}, u32[]{:S(2)}) collective-permute-start(f32[2,8]{1,0:T(2,128)S(1)} %pad_maximum_fusion.2), channel_id=1, source_target_pairs={{0,1},{1,0},{2,3},{3,2},{4,5},{5,4},{6,7},{7,6},{8,9},{9,8},{10,11... | collective-permute-start | bytes 200 | tf_op jit(solution)/shard_map/ppermute | solution.py:24
  39.2 3.6 %collective-permute-start.1 = (f32[2,8]{1,0:T(2,128)S(1)}, f32[2,8]{1,0:T(2,128)S(1)}, u32[]{:S(2)}, u32[]{:S(2)}) collective-permute-start(f32[2,8]{1,0:T(2,128)S(1)} %select_add_fusion.1), channel_id=1, source_target_pairs={{0,2},{1,3},{2,0},{3,1},{4,6},{5,7},{6,4},{7,5},{8,10},{9,11},{10,... | collective-permute-start | bytes 200 | tf_op jit(solution)/shard_map/ppermute | solution.py:24
  44.5 18.6 %all-to-all-start.2 = ((bf16[32,8,1024]{2,1,0:T(8,128)(2,1)}), bf16[32,8,1024]{2,1,0:T(8,128)(2,1)S(1)}, u32[]{:S(2)}, u32[]{:S(2)}) async-start(bf16[32,8,1024]{2,1,0:T(8,128)(2,1)} %broadcast_in_dim.32), calls=%async_computation.2 | async-start | bytes 1048576 | tf_op jit(solution)/shard_map/all_to_all | solution.py:163

commit v6 on v5

--- a/solution.py
+++ b/solution.py
@@ -153,17 +153,16 @@
     part = jnp.dot(rows_in, dense_weight, preferred_element_type=jnp.float32)
     act = jnp.sum(lax.all_to_all(part.reshape(groups, group_rows, -1), "dp", 0, 0, tiled=True), axis=0)
     act = jax.nn.gelu(act + dense_bias, approximate=False)
-    stats = _psum(jnp.stack([jnp.sum(act, axis=1), jnp.sum(act * act, axis=1)]), "vocab", ways)
-    mean = stats[0] / model
-    var = stats[1] / model - mean * mean
-    head_rows = (
-        (act - mean[:, None]) * lax.rsqrt(var + EPS)[:, None] * norm_gain + norm_shift
-    ).astype(jnp.bfloat16)
+    pieces = _gather(jnp.concatenate([act, norm_gain[None], norm_shift[None]]), "vocab", ways, _steps(ways)[::-1])
+    pieces = pieces.transpose(1, 0, 2).reshape(group_rows + 2, model)
+    act, gain, shift = pieces[:group_rows], pieces[group_rows], pieces[group_rows + 1]
+    mean = jnp.sum(act, axis=1) / model
+    var = jnp.sum(act * act, axis=1) / model - mean * mean
+    head_rows = ((act - mean[:, None]) * lax.rsqrt(var + EPS)[:, None] * gain + shift).astype(jnp.bfloat16)
+    head_all = lax.all_to_all(
+        jnp.broadcast_to(head_rows[None], (groups,) + head_rows.shape), "dp", 0, 0, tiled=True
+    ).reshape(total_rows, model)
     devices = groups * ways
-    every_head = lax.all_to_all(
-        jnp.broadcast_to(head_rows[None], (devices,) + head_rows.shape), ("dp", "vocab"), 0, 0, tiled=True
-    )
-    head_all = every_head.reshape(groups, ways, group_rows, -1).transpose(0, 2, 1, 3).reshape(total_rows, model)
     vocab_rows = embedding.shape[0]
     first_id = (lax.axis_index("dp") * ways + lax.axis_index("vocab")) * vocab_rows
     ids = first_id + jnp.arange(vocab_rows, dtype=jnp.int32)

time: 107 us -> 107 us (level)
  blocking collectives: 10 us -> 21.8 us
  waiting for transfers between devices: 38.4 us -> 28.7 us
  starting transfers between devices: 14.8 us -> 11.9 us
    all_to_all x0 -> x1, blocking collectives: none -> 11.7 us  [body(): lax.all_to_all(part.reshape(groups, group_rows, -1), 'dp', 0, 0, tiled=True)]
    all_to_all x2 -> x1, waiting for transfers between devices: 24.1 us -> 14.2 us  [body(): lax.all_to_all(jnp.broadcast_to(head_rows[None], (groups,) + head_rows.sh...]
    all_to_all x2 -> x1, starting transfers between devices: 6.4 us -> 3.57 us  [body(): lax.all_to_all(jnp.broadcast_to(head_rows[None], (groups,) + head_rows.sh...]
  transfers between devices with their start and end apart: 5 -> 4, of which waited for: 5 -> 4; matrix products, arithmetic and copies ran while one was open for 1% -> 1% of each run, Pallas kernels for 0% -> 0%
where the time goes in v6:
time: 107 us
  matrix products  32.1 us (30%)
  waiting for transfers between devices  28.7 us (27%)
  blocking collectives  21.8 us (20%)
  starting transfers between devices  11.9 us (11%)
  other arithmetic  6.41 us (6%)
  local copies, waits for them, and re-layouts  4.21 us (4%)
  between operations  1.5 us (1%)
    dot_general x1, matrix products, body(): jnp.einsum('rd,vd->rv', head_all, embedding, preferred_element_type=jnp.f...  15.7 us
    dot_general x1, matrix products, body(): jnp.einsum('rv,rd->vd', grad, head_all, preferred_element_type=jnp.float32)  14.5 us
    all_to_all x1, waiting for transfers between devices, body(): lax.all_to_all(jnp.broadcast_to(head_rows[None], (groups,) + head_rows.sh...  14.2 us
    all_to_all x1, blocking collectives, body(): lax.all_to_all(part.reshape(groups, group_rows, -1), 'dp', 0, 0, tiled=True)  11.7 us
    all_to_all x1, waiting for transfers between devices, body(): lax.all_to_all(jnp.repeat(blocks, ways, axis=0), ('dp', 'vocab'), 0, 0, t...  10.5 us
    all_to_all x1, blocking collectives, body(): lax.all_to_all(jnp.broadcast_to(local[None], (devices,) + local.shape), (...  10.1 us
    all_to_all x1, starting transfers between devices, body(): lax.all_to_all(jnp.repeat(blocks, ways, axis=0), ('dp', 'vocab'), 0, 0, t...  7.33 us
    ppermute x2, waiting for transfers between devices, _allgather(): theirs = lax.ppermute(buf, axis, [(a, a ^ step) for a in range(n)])  4.03 us
  transfers between devices with their start and end apart: 4, of which 4 were waited for; matrix products, arithmetic and copies ran while one was open for 1% of the time, Pallas kernels for 0%

profile of v6, /device:TPU:0, one launch (start us, length us, event | category | flops | bytes accessed | tf_op | source)
XLA Modules:
  0.0 106.7 jit_solution(10082497395589220454)
XLA Ops:
  0.6 0.0 copy-start
  0.6 0.7 shift-right-arithmetic_bitcast_fusion
  2.1 0.2 add_dynamic-update-slice_fusion
  2.2 1.5 %convolution_convert_fusion.1 = bf16[6,4096]{1,0:T(8,128)(2,1)S(1)} fusion(bf16[128,4096]{1,0:T(8,128)(2,1)} %param.13, s32[6]{0:T(128)} %bitcast.80), kind=kOutput, calls=%fused_computation.3 | convolution fusion | flops 6316800 | bytes 1097752 | tf_op jit(solution)/shard_map/dot_general | solution.py:123
  3.9 0.7 broadcast_in_dim.37
  4.6 7.3 %all-to-all-start = ((bf16[32,7,512]{2,1,0:T(8,128)(2,1)}), bf16[32,7,512]{2,1,0:T(8,128)(2,1)S(1)}, u32[]{:S(2)}, u32[]{:S(2)}) async-start(bf16[32,7,512]{2,1,0:T(8,128)(2,1)} %bitcast.5), calls=%async_computation | async-start | bytes 524288 | tf_op jit(solution)/shard_map/all_to_all | solution.py:133
  11.9 0.1 add.100
  12.0 10.5 %all-to-all-done = bf16[32,7,512]{2,1,0:T(8,128)(2,1)S(1)} async-done(((bf16[32,7,512]{2,1,0:T(8,128)(2,1)}), bf16[32,7,512]{2,1,0:T(8,128)(2,1)S(1)}, u32[]{:S(2)}, u32[]{:S(2)}) %all-to-all-start) | async-done | bytes 229408 | tf_op jit(solution)/shard_map/all_to_all | solution.py:133
  22.5 0.1 copy.55
  22.7 0.1 copy.57
  22.8 0.1 copy.56
  22.8 0.1 broadcast_in_dim.38
  22.9 0.1 reshape.232
  23.0 0.1 broadcast_in_dim.68
  23.1 0.1 reshape.233
  23.2 0.1 copy.58
  23.3 0.0 copy-done
  23.3 0.4 fusion
  23.7 11.7 %all_to_all.20 = f32[8,8,1024]{2,1,0:T(8,128)S(1)} all-to-all(f32[8,8,1024]{2,1,0:T(8,128)S(1)} %fusion), channel_id=1, replica_groups=mesh['dp'=8,'vocab'=4] {'dp'}, dimensions={0} | all-to-all | bytes 524288 | tf_op jit(solution)/shard_map/all_to_all | solution.py:154
  35.4 0.8 fusion.14
  36.2 0.7 maximum_bitcast_fusion
  36.9 1.0 collective-permute-start
  37.9 3.4 %collective-permute-done = f32[1,10,1024]{2,1,0:T(8,128)S(1)} collective-permute-done((f32[1,10,1024]{2,1,0:T(8,128)S(1)}, f32[1,10,1024]{2,1,0:T(8,128)S(1)}, u32[]{:S(2)}, u32[]{:S(2)}) %collective-permute-start) | collective-permute-done | bytes 40992 | tf_op jit(solution)/shard_map/ppermute | solution.py:35
  41.3 0.1 collective-permute-start.1
  41.3 0.7 pad_clamp_fusion
  42.0 0.7 collective-permute-done.1
  42.7 0.6 gather_fusion
  43.3 0.2 slice_reduce_fusion
  43.5 0.1 add_convert_fusion
  43.6 0.8 broadcast_in_dim.73
  44.4 3.6 %all-to-all-start.2 = ((bf16[8,8,4096]{2,1,0:T(8,128)(2,1)}), bf16[8,8,4096]{2,1,0:T(8,128)(2,1)S(1)}, u32[]{:S(2)}, u32[]{:S(2)}) async-start(bf16[8,8,4096]{2,1,0:T(8,128)(2,1)} %broadcast_in_dim.73), calls=%async_computation.2 | async-start | bytes 1048576 | tf_op jit(solution)/shard_map/all_to_all | solution.py:162
  48.0 0.1 slice.76
  48.1 0.1 copy.60
  48.2 0.1 copy.61
  48.3 0.1 add.114
  48.4 0.2 select_reduce_fusion
  48.6 0.1 eq.50
  48.7 14.2 %all-to-all-done.2 = bf16[8,8,4096]{2,1,0:T(8,128)(2,1)S(1)} async-done(((bf16[8,8,4096]{2,1,0:T(8,128)(2,1)}), bf16[8,8,4096]{2,1,0:T(8,128)(2,1)S(1)}, u32[]{:S(2)}, u32[]{:S(2)}) %all-to-all-start.2) | async-done | bytes 524320 | tf_op jit(solution)/shard_map/all_to_all | solution.py:162
  62.9 15.7 %fusion.36 = (f32[64]{0:T(128)S(1)}, f32[64,4096]{1,0:T(8,128)S(1)}) fusion(f32[4096]{0:T(1024)} %param.22, bf16[4096,4096]{1,0:T(8,128)(2,1)} %param.21, bf16[8,8,4096]{2,1,0:T(8,128)(2,1)S(1)} %all-to-all-done.2), kind=kOutput, calls=%fused_computation.79 | convolution fusion | flops 2148007936 | bytes 35143936 | tf_op jit(solution)/shard_map/rd,vd->rv/dot_general | solution.py:170
  78.6 0.4 exponential_reduce_fusion
  79.0 0.1 reshape.247
  79.1 10.1 %all_to_all.21 = f32[32,1,192]{2,1,0:T(1,128)S(1)} all-to-all(f32[32,1,192]{2,1,0:T(1,128)S(1)} %reshape.247), channel_id=1, replica_groups=mesh['dp'=8,'vocab'=4] {'dp','vocab'}, dimensions={0} | all-to-all | bytes 49152 | tf_op jit(solution)/shard_map/all_to_all | solution.py:182
  89.3 0.5 broadcast.157
  89.8 0.7 reduce.6
  90.5 0.1 reshape.248
  90.7 0.5 fusion.33
  91.2 0.3 fusion.4
  91.6 0.6 broadcast_multiply_fusion
  92.2 14.5 %convolution_convert_fusion = bf16[4096,4096]{1,0:T(8,128)(2,1)} fusion(f32[64,4096]{1,0:T(8,128)S(1)} %get-tuple-element.33, bf16[8,8,4096]{2,1,0:T(8,128)(2,1)S(1)} %all-to-all-done.2, f32[64]{0:T(128)S(1)} %get-tuple-element.20, s32[4096]{0:T(1024)S(1)} %iota_add_fusion, s32[64]{0:T(128)S(1)} %eq.50), kind=kOutput, calls=%fused_computation.1 | convolution fusion | flops 2165833728 | bytes 35144192 | tf_op jit(solution)/shard_map/rv,rd->vd/dot_general | solution.py:190
  (26 shorter events, 0.4 us)
Async XLA Ops:
  0.6 22.7 %copy-start = (bf16[512,1024]{1,0:T(8,128)(2,1)S(1)}, bf16[512,1024]{1,0:T(8,128)(2,1)}, u32[]{:S(2)}) copy-start(bf16[512,1024]{1,0:T(8,128)(2,1)} %param.17) | copy-start | bytes 3145732
  4.6 17.9 %all-to-all-start = ((bf16[32,7,512]{2,1,0:T(8,128)(2,1)}), bf16[32,7,512]{2,1,0:T(8,128)(2,1)S(1)}, u32[]{:S(2)}, u32[]{:S(2)}) async-start(bf16[32,7,512]{2,1,0:T(8,128)(2,1)} %bitcast.5), calls=%async_computation | async-start | bytes 524288 | tf_op jit(solution)/shard_map/all_to_all | solution.py:133
  36.9 4.3 %collective-permute-start = (f32[1,10,1024]{2,1,0:T(8,128)S(1)}, f32[1,10,1024]{2,1,0:T(8,128)S(1)}, u32[]{:S(2)}, u32[]{:S(2)}) collective-permute-start(f32[1,10,1024]{2,1,0:T(8,128)S(1)} %maximum_bitcast_fusion), channel_id=1, source_target_pairs={{0,2},{1,3},{2,0},{3,1},{4,6},{5,7},{6,4},{7,5},{8,10},{9,11},{10,... | collective-permute-start | bytes 122888 | tf_op jit(solution)/shard_map/ppermute | solution.py:35
  41.3 1.4 %collective-permute-start.1 = (f32[2,10,1024]{2,1,0:T(8,128)S(1)}, f32[2,10,1024]{2,1,0:T(8,128)S(1)}, u32[]{:S(2)}, u32[]{:S(2)}) collective-permute-start(f32[2,10,1024]{2,1,0:T(8,128)S(1)} %maximum_select_fusion.1), channel_id=1, source_target_pairs={{0,1},{1,0},{2,3},{3,2},{4,5},{5,4},{6,7},{7,6},{8,9},{9,8},{10,11... | collective-permute-start | bytes 245768 | tf_op jit(solution)/shard_map/ppermute | solution.py:35
  44.4 18.5 %all-to-all-start.2 = ((bf16[8,8,4096]{2,1,0:T(8,128)(2,1)}), bf16[8,8,4096]{2,1,0:T(8,128)(2,1)S(1)}, u32[]{:S(2)}, u32[]{:S(2)}) async-start(bf16[8,8,4096]{2,1,0:T(8,128)(2,1)} %broadcast_in_dim.73), calls=%async_computation.2 | async-start | bytes 1048576 | tf_op jit(solution)/shard_map/all_to_all | solution.py:162

commit v7 on v6

--- a/solution.py
+++ b/solution.py
@@ -130,8 +130,8 @@
         ],
         axis=1,
     )
-    got = lax.all_to_all(jnp.repeat(blocks, ways, axis=0), ("dp", "vocab"), 0, 0, tiled=True)
-    got = got.reshape(groups, ways, slots + 1, in_block)
+    got = lax.all_to_all(blocks, "dp", 0, 0, tiled=True)
+    got = _gather(got, "vocab", ways, _steps(ways)[::-1]).transpose(1, 0, 2, 3)
     slot_rows = got[:, :, :slots].reshape(groups, ways * slots, in_block)
     got_meta = got[:, :, slots, : 1 + 3 * slots].astype(jnp.int32)
     got_tgt = _unpieces(got_meta[:, :, 1:].reshape(groups, ways, 3, slots)).reshape(groups, ways * slots)

time: 107 us -> 109 us (1.019)
  blocking collectives: 21.8 us -> 36.6 us
  waiting for transfers between devices: 28.7 us -> 21.5 us
  starting transfers between devices: 11.9 us -> 6.88 us
    all_to_all x0 -> x1, blocking collectives: none -> 14 us  [body(): got = lax.all_to_all(blocks, 'dp', 0, 0, tiled=True)]
    all_to_all x1 -> x0, waiting for transfers between devices: 10.5 us -> none  [body(): lax.all_to_all(jnp.repeat(blocks, ways, axis=0), ('dp', 'vocab'), 0, 0, t...]
    all_to_all x1 -> x0, starting transfers between devices: 7.33 us -> none  [body(): lax.all_to_all(jnp.repeat(blocks, ways, axis=0), ('dp', 'vocab'), 0, 0, t...]
    ppermute x2 -> x4, waiting for transfers between devices: 4.03 us -> 7.29 us  [_allgather(): theirs = lax.ppermute(buf, axis, [(a, a ^ step) for a in range(n)])]
    ppermute x2 -> x4, starting transfers between devices: 1.05 us -> 3.31 us  [_allgather(): theirs = lax.ppermute(buf, axis, [(a, a ^ step) for a in range(n)])]
  transfers between devices with their start and end apart: 4 -> 5, of which waited for: 4 -> 5; matrix products, arithmetic and copies ran while one was open for 1% -> 1% of each run, Pallas kernels for 0% -> 0%
where the time goes in v7:
time: 109 us
  blocking collectives  36.6 us (34%)
  matrix products  32.1 us (29%)
  waiting for transfers between devices  21.5 us (20%)
  starting transfers between devices  6.88 us (6%)
  other arithmetic  6.47 us (6%)
  local copies, waits for them, and re-layouts  3.94 us (4%)
  between operations  1.51 us (1%)
    dot_general x1, matrix products, body(): jnp.einsum('rd,vd->rv', head_all, embedding, preferred_element_type=jnp.f...  15.7 us
    dot_general x1, matrix products, body(): jnp.einsum('rv,rd->vd', grad, head_all, preferred_element_type=jnp.float32)  14.5 us
    all_to_all x1, waiting for transfers between devices, body(): lax.all_to_all(jnp.broadcast_to(head_rows[None], (groups,) + head_rows.sh...  14.2 us
    all_to_all x1, blocking collectives, body(): got = lax.all_to_all(blocks, 'dp', 0, 0, tiled=True)  14 us
    all_to_all x1, blocking collectives, body(): lax.all_to_all(part.reshape(groups, group_rows, -1), 'dp', 0, 0, tiled=True)  11.9 us
    all_to_all x1, blocking collectives, body(): lax.all_to_all(jnp.broadcast_to(local[None], (devices,) + local.shape), (...  10.7 us
    ppermute x4, waiting for transfers between devices, _allgather(): theirs = lax.ppermute(buf, axis, [(a, a ^ step) for a in range(n)])  7.29 us
    all_to_all x1, starting transfers between devices, body(): lax.all_to_all(jnp.broadcast_to(head_rows[None], (groups,) + head_rows.sh...  3.57 us
  transfers between devices with their start and end apart: 5, of which 5 were waited for; matrix products, arithmetic and copies ran while one was open for 1% of the time, Pallas kernels for 0%

profile of v7, /device:TPU:0, one launch (start us, length us, event | category | flops | bytes accessed | tf_op | source)
XLA Modules:
  0.0 109.0 jit_solution(16669376117683239550)
XLA Ops:
  0.6 0.0 copy-start
  0.6 0.7 shift-right-arithmetic_bitcast_fusion
  2.1 0.2 add_dynamic-update-slice_fusion
  2.2 1.5 %convolution_convert_fusion.1 = bf16[6,4096]{1,0:T(8,128)(2,1)S(1)} fusion(bf16[128,4096]{1,0:T(8,128)(2,1)} %param.14, s32[6]{0:T(128)} %bitcast.72), kind=kOutput, calls=%fused_computation.4 | convolution fusion | flops 6316800 | bytes 1097752 | tf_op jit(solution)/shard_map/dot_general | solution.py:123
  3.8 14.0 %all_to_all.20 = bf16[8,7,512]{2,1,0:T(8,128)(2,1)S(1)} all-to-all(bf16[8,7,512]{2,1,0:T(8,128)(2,1)S(1)} %pad_maximum_fusion), channel_id=1, replica_groups=mesh['dp'=8,'vocab'=4] {'dp'}, dimensions={0} | all-to-all | bytes 114688 | tf_op jit(solution)/shard_map/all_to_all | solution.py:133
  17.8 1.6 %collective-permute-start = (bf16[1,8,7,512]{3,1,2,0:T(8,128)(2,1)S(1)}, bf16[1,8,7,512]{3,1,2,0:T(8,128)(2,1)S(1)}, u32[]{:S(2)}, u32[]{:S(2)}) collective-permute-start(bf16[1,8,7,512]{3,1,2,0:T(8,128)(2,1)S(1)} %bitcast.58), channel_id=1, source_target_pairs={{0,2},{1,3},{2,0},{3,1},{4,6},{5,7},{6,4},{7,5},{8,10},{9,11},{10,... | collective-permute-start | bytes 172040 | tf_op jit(solution)/shard_map/ppermute | solution.py:35
  19.4 2.7 %collective-permute-done = bf16[1,8,7,512]{3,1,2,0:T(8,128)(2,1)S(1)} collective-permute-done((bf16[1,8,7,512]{3,1,2,0:T(8,128)(2,1)S(1)}, bf16[1,8,7,512]{3,1,2,0:T(8,128)(2,1)S(1)}, u32[]{:S(2)}, u32[]{:S(2)}) %collective-permute-start) | collective-permute-done | bytes 57376 | tf_op jit(solution)/shard_map/ppermute | solution.py:35
  22.1 0.1 collective-permute-start.1
  22.2 0.1 add.104
  22.3 0.7 pad_clamp_fusion
  22.9 0.6 collective-permute-done.1
  23.5 0.6 gather_fusion
  24.1 0.1 slice_reduce_fusion
  24.3 0.1 copy.48
  24.4 0.1 copy.47
  24.5 0.1 broadcast_in_dim.71
  24.6 0.1 reshape.224
  24.6 0.1 broadcast_in_dim.72
  24.7 0.1 reshape.225
  24.8 0.0 copy-done
  24.8 0.4 fusion
  25.2 11.9 %all_to_all.21 = f32[8,8,1024]{2,1,0:T(8,128)S(1)} all-to-all(f32[8,8,1024]{2,1,0:T(8,128)S(1)} %fusion), channel_id=1, replica_groups=mesh['dp'=8,'vocab'=4] {'dp'}, dimensions={0} | all-to-all | bytes 524288 | tf_op jit(solution)/shard_map/all_to_all | solution.py:154
  37.2 0.8 fusion.14
  37.9 0.7 maximum_bitcast_fusion
  38.7 1.6 %collective-permute-start.2 = (f32[1,10,1024]{2,1,0:T(8,128)S(1)}, f32[1,10,1024]{2,1,0:T(8,128)S(1)}, u32[]{:S(2)}, u32[]{:S(2)}) collective-permute-start(f32[1,10,1024]{2,1,0:T(8,128)S(1)} %maximum_bitcast_fusion), channel_id=1, source_target_pairs={{0,2},{1,3},{2,0},{3,1},{4,6},{5,7},{6,4},{7,5},{8,10},{9,11},{10,... | collective-permute-start | bytes 122888 | tf_op jit(solution)/shard_map/ppermute | solution.py:35
  40.3 2.7 %collective-permute-done.2 = f32[1,10,1024]{2,1,0:T(8,128)S(1)} collective-permute-done((f32[1,10,1024]{2,1,0:T(8,128)S(1)}, f32[1,10,1024]{2,1,0:T(8,128)S(1)}, u32[]{:S(2)}, u32[]{:S(2)}) %collective-permute-start.2) | collective-permute-done | bytes 40992 | tf_op jit(solution)/shard_map/ppermute | solution.py:35
  43.0 0.1 collective-permute-start.3
  43.1 1.3 %collective-permute-done.3 = f32[2,10,1024]{2,1,0:T(8,128)S(1)} collective-permute-done((f32[2,10,1024]{2,1,0:T(8,128)S(1)}, f32[2,10,1024]{2,1,0:T(8,128)S(1)}, u32[]{:S(2)}, u32[]{:S(2)}) %collective-permute-start.3) | collective-permute-done | bytes 81952 | tf_op jit(solution)/shard_map/ppermute | solution.py:35
  44.5 0.6 gather_fusion.1
  45.0 0.2 slice_reduce_fusion.1
  45.3 0.1 add_convert_fusion
  45.4 0.8 broadcast_in_dim.77
  46.2 3.6 %all-to-all-start.2 = ((bf16[8,8,4096]{2,1,0:T(8,128)(2,1)}), bf16[8,8,4096]{2,1,0:T(8,128)(2,1)S(1)}, u32[]{:S(2)}, u32[]{:S(2)}) async-start(bf16[8,8,4096]{2,1,0:T(8,128)(2,1)} %broadcast_in_dim.77), calls=%async_computation.2 | async-start | bytes 1048576 | tf_op jit(solution)/shard_map/all_to_all | solution.py:162
  49.8 0.1 slice.78
  49.8 0.1 copy.50
  50.0 0.1 copy.51
  50.1 0.1 add.118
  50.1 0.2 select_reduce_fusion
  50.4 0.1 eq.50
  50.4 14.2 %all-to-all-done.2 = bf16[8,8,4096]{2,1,0:T(8,128)(2,1)S(1)} async-done(((bf16[8,8,4096]{2,1,0:T(8,128)(2,1)}), bf16[8,8,4096]{2,1,0:T(8,128)(2,1)S(1)}, u32[]{:S(2)}, u32[]{:S(2)}) %all-to-all-start.2) | async-done | bytes 524320 | tf_op jit(solution)/shard_map/all_to_all | solution.py:162
  64.7 15.7 %fusion.36 = (f32[64]{0:T(128)S(1)}, f32[64,4096]{1,0:T(8,128)S(1)}) fusion(f32[4096]{0:T(1024)} %param.23, bf16[4096,4096]{1,0:T(8,128)(2,1)} %param.22, bf16[8,8,4096]{2,1,0:T(8,128)(2,1)S(1)} %all-to-all-done.2), kind=kOutput, calls=%fused_computation.82 | convolution fusion | flops 2148007936 | bytes 35143936 | tf_op jit(solution)/shard_map/rd,vd->rv/dot_general | solution.py:170
  80.3 0.4 exponential_reduce_fusion
  80.8 0.1 reshape.248
  80.9 10.7 %all_to_all.22 = f32[32,1,192]{2,1,0:T(1,128)S(1)} all-to-all(f32[32,1,192]{2,1,0:T(1,128)S(1)} %reshape.248), channel_id=1, replica_groups=mesh['dp'=8,'vocab'=4] {'dp','vocab'}, dimensions={0} | all-to-all | bytes 49152 | tf_op jit(solution)/shard_map/all_to_all | solution.py:182
  91.6 0.5 broadcast.160
  92.1 0.7 reduce.8
  92.9 0.1 reshape.249
  93.1 0.5 fusion.33
  93.6 0.3 fusion.4
  94.0 0.6 broadcast_multiply_fusion
  94.6 14.5 %convolution_convert_fusion = bf16[4096,4096]{1,0:T(8,128)(2,1)} fusion(f32[64,4096]{1,0:T(8,128)S(1)} %get-tuple-element.33, bf16[8,8,4096]{2,1,0:T(8,128)(2,1)S(1)} %all-to-all-done.2, f32[64]{0:T(128)S(1)} %get-tuple-element.20, s32[4096]{0:T(1024)S(1)} %iota_add_fusion, s32[64]{0:T(128)S(1)} %eq.50), kind=kOutput, calls=%fused_computation.2 | convolution fusion | flops 2165833728 | bytes 35144192 | tf_op jit(solution)/shard_map/rv,rd->vd/dot_general | solution.py:190
  (27 shorter events, 0.5 us)
Async XLA Ops:
  0.6 24.2 %copy-start = (bf16[512,1024]{1,0:T(8,128)(2,1)S(1)}, bf16[512,1024]{1,0:T(8,128)(2,1)}, u32[]{:S(2)}) copy-start(bf16[512,1024]{1,0:T(8,128)(2,1)} %param.18) | copy-start | bytes 3145732
  17.8 4.2 %collective-permute-start = (bf16[1,8,7,512]{3,1,2,0:T(8,128)(2,1)S(1)}, bf16[1,8,7,512]{3,1,2,0:T(8,128)(2,1)S(1)}, u32[]{:S(2)}, u32[]{:S(2)}) collective-permute-start(bf16[1,8,7,512]{3,1,2,0:T(8,128)(2,1)S(1)} %bitcast.58), channel_id=1, source_target_pairs={{0,2},{1,3},{2,0},{3,1},{4,6},{5,7},{6,4},{7,5},{8,10},{9,11},{10,... | collective-permute-start | bytes 172040 | tf_op jit(solution)/shard_map/ppermute | solution.py:35
  22.1 1.4 %collective-permute-start.1 = (bf16[2,8,7,512]{3,1,2,0:T(8,128)(2,1)S(1)}, bf16[2,8,7,512]{3,1,2,0:T(8,128)(2,1)S(1)}, u32[]{:S(2)}, u32[]{:S(2)}) collective-permute-start(bf16[2,8,7,512]{3,1,2,0:T(8,128)(2,1)S(1)} %maximum_select_fusion.3), channel_id=1, source_target_pairs={{0,1},{1,0},{2,3},{3,2},{4,5},{5,4},{6,7},{7,6},{8,9},{9,8},{10,11... | collective-permute-start | bytes 344072 | tf_op jit(solution)/shard_map/ppermute | solution.py:35
  38.7 4.3 %collective-permute-start.2 = (f32[1,10,1024]{2,1,0:T(8,128)S(1)}, f32[1,10,1024]{2,1,0:T(8,128)S(1)}, u32[]{:S(2)}, u32[]{:S(2)}) collective-permute-start(f32[1,10,1024]{2,1,0:T(8,128)S(1)} %maximum_bitcast_fusion), channel_id=1, source_target_pairs={{0,2},{1,3},{2,0},{3,1},{4,6},{5,7},{6,4},{7,5},{8,10},{9,11},{10,... | collective-permute-start | bytes 122888 | tf_op jit(solution)/shard_map/ppermute | solution.py:35
  43.0 1.4 %collective-permute-start.3 = (f32[2,10,1024]{2,1,0:T(8,128)S(1)}, f32[2,10,1024]{2,1,0:T(8,128)S(1)}, u32[]{:S(2)}, u32[]{:S(2)}) collective-permute-start(f32[2,10,1024]{2,1,0:T(8,128)S(1)} %maximum_select_fusion.2), channel_id=1, source_target_pairs={{0,1},{1,0},{2,3},{3,2},{4,5},{5,4},{6,7},{7,6},{8,9},{9,8},{10,11... | collective-permute-start | bytes 245768 | tf_op jit(solution)/shard_map/ppermute | solution.py:35
  46.2 18.5 %all-to-all-start.2 = ((bf16[8,8,4096]{2,1,0:T(8,128)(2,1)}), bf16[8,8,4096]{2,1,0:T(8,128)(2,1)S(1)}, u32[]{:S(2)}, u32[]{:S(2)}) async-start(bf16[8,8,4096]{2,1,0:T(8,128)(2,1)} %broadcast_in_dim.77), calls=%async_computation.2 | async-start | bytes 1048576 | tf_op jit(solution)/shard_map/all_to_all | solution.py:162

commit v8 on v6

--- a/solution.py
+++ b/solution.py
@@ -153,7 +153,7 @@
     part = jnp.dot(rows_in, dense_weight, preferred_element_type=jnp.float32)
     act = jnp.sum(lax.all_to_all(part.reshape(groups, group_rows, -1), "dp", 0, 0, tiled=True), axis=0)
     act = jax.nn.gelu(act + dense_bias, approximate=False)
-    pieces = _gather(jnp.concatenate([act, norm_gain[None], norm_shift[None]]), "vocab", ways, _steps(ways)[::-1])
+    pieces = _gather(jnp.concatenate([act, norm_gain[None], norm_shift[None]]), "vocab", ways)
     pieces = pieces.transpose(1, 0, 2).reshape(group_rows + 2, model)
     act, gain, shift = pieces[:group_rows], pieces[group_rows], pieces[group_rows + 1]
     mean = jnp.sum(act, axis=1) / model

time: 107 us -> 107 us (level)
  waiting for transfers between devices: 28.7 us -> 29.8 us
    ppermute x2, waiting for transfers between devices: 4.03 us -> 5.88 us  [_allgather(): theirs = lax.ppermute(buf, axis, [(a, a ^ step) for a in range(n)])]
where the time goes in v8:
time: 107 us; the launch traced here: 106 us
  matrix products  32.1 us (30%)
  waiting for transfers between devices  29.8 us (28%)
  blocking collectives  21.8 us (20%)
  starting transfers between devices  11.9 us (11%)
  other arithmetic  5.75 us (5%)
  local copies, waits for them, and re-layouts  3.64 us (3%)
  between operations  1.5 us (1%)
    dot_general x1, matrix products, body(): jnp.einsum('rd,vd->rv', head_all, embedding, preferred_element_type=jnp.f...  15.7 us
    dot_general x1, matrix products, body(): jnp.einsum('rv,rd->vd', grad, head_all, preferred_element_type=jnp.float32)  14.5 us
    all_to_all x1, waiting for transfers between devices, body(): lax.all_to_all(jnp.broadcast_to(head_rows[None], (groups,) + head_rows.sh...  13.4 us
    all_to_all x1, blocking collectives, body(): lax.all_to_all(part.reshape(groups, group_rows, -1), 'dp', 0, 0, tiled=True)  11.7 us
    all_to_all x1, waiting for transfers between devices, body(): lax.all_to_all(jnp.repeat(blocks, ways, axis=0), ('dp', 'vocab'), 0, 0, t...  10.5 us
    all_to_all x1, blocking collectives, body(): lax.all_to_all(jnp.broadcast_to(local[None], (devices,) + local.shape), (...  10.1 us
    all_to_all x1, starting transfers between devices, body(): lax.all_to_all(jnp.repeat(blocks, ways, axis=0), ('dp', 'vocab'), 0, 0, t...  7.33 us
    ppermute x2, waiting for transfers between devices, _allgather(): theirs = lax.ppermute(buf, axis, [(a, a ^ step) for a in range(n)])  5.88 us
  transfers between devices with their start and end apart: 4, of which 4 were waited for; matrix products, arithmetic and copies ran while one was open for 1% of the time, Pallas kernels for 0%

profile of v8, /device:TPU:0, one launch (start us, length us, event | category | flops | bytes accessed | tf_op | source)
XLA Modules:
  0.0 106.5 jit_solution(9963183451818539943)
XLA Ops:
  0.6 0.0 copy-start
  0.6 0.7 shift-right-arithmetic_bitcast_fusion
  2.1 0.2 add_dynamic-update-slice_fusion
  2.2 1.5 %convolution_convert_fusion.1 = bf16[6,4096]{1,0:T(8,128)(2,1)S(1)} fusion(bf16[128,4096]{1,0:T(8,128)(2,1)} %param.12, s32[6]{0:T(128)} %bitcast.79), kind=kOutput, calls=%fused_computation.2 | convolution fusion | flops 6316800 | bytes 1097752 | tf_op jit(solution)/shard_map/dot_general | solution.py:123
  3.9 0.7 broadcast_in_dim.35
  4.6 7.3 %all-to-all-start = ((bf16[32,7,512]{2,1,0:T(8,128)(2,1)}), bf16[32,7,512]{2,1,0:T(8,128)(2,1)S(1)}, u32[]{:S(2)}, u32[]{:S(2)}) async-start(bf16[32,7,512]{2,1,0:T(8,128)(2,1)} %bitcast.5), calls=%async_computation | async-start | bytes 524288 | tf_op jit(solution)/shard_map/all_to_all | solution.py:133
  11.9 0.1 add.97
  12.0 10.5 %all-to-all-done = bf16[32,7,512]{2,1,0:T(8,128)(2,1)S(1)} async-done(((bf16[32,7,512]{2,1,0:T(8,128)(2,1)}), bf16[32,7,512]{2,1,0:T(8,128)(2,1)S(1)}, u32[]{:S(2)}, u32[]{:S(2)}) %all-to-all-start) | async-done | bytes 229408 | tf_op jit(solution)/shard_map/all_to_all | solution.py:133
  22.5 0.1 copy.54
  22.7 0.1 copy.56
  22.8 0.1 copy.55
  22.8 0.1 broadcast_in_dim.36
  22.9 0.1 reshape.232
  23.0 0.1 broadcast_in_dim.37
  23.1 0.1 reshape.233
  23.2 0.1 copy.57
  23.3 0.0 copy-done
  23.3 0.4 fusion
  23.7 11.7 %all_to_all.20 = f32[8,8,1024]{2,1,0:T(8,128)S(1)} all-to-all(f32[8,8,1024]{2,1,0:T(8,128)S(1)} %fusion), channel_id=1, replica_groups=mesh['dp'=8,'vocab'=4] {'dp'}, dimensions={0} | all-to-all | bytes 524288 | tf_op jit(solution)/shard_map/all_to_all | solution.py:154
  35.4 0.8 fusion.15
  36.2 0.7 maximum_bitcast_fusion
  36.9 0.1 collective-permute-start
  37.0 1.2 %collective-permute-done = f32[1,10,1024]{2,1,0:T(8,128)S(1)} collective-permute-done((f32[1,10,1024]{2,1,0:T(8,128)S(1)}, f32[1,10,1024]{2,1,0:T(8,128)S(1)}, u32[]{:S(2)}, u32[]{:S(2)}) %collective-permute-start) | collective-permute-done | bytes 40992 | tf_op jit(solution)/shard_map/ppermute | solution.py:35
  38.2 1.0 collective-permute-start.1
  39.2 4.6 %collective-permute-done.1 = f32[2,10,1024]{2,1,0:T(8,128)S(1)} collective-permute-done((f32[2,10,1024]{2,1,0:T(8,128)S(1)}, f32[2,10,1024]{2,1,0:T(8,128)S(1)}, u32[]{:S(2)}, u32[]{:S(2)}) %collective-permute-start.1) | collective-permute-done | bytes 81952 | tf_op jit(solution)/shard_map/ppermute | solution.py:35
  43.9 0.2 slice_reduce_fusion
  44.1 0.1 add_convert_fusion
  44.2 0.8 broadcast_in_dim.69
  45.0 3.6 %all-to-all-start.2 = ((bf16[8,8,4096]{2,1,0:T(8,128)(2,1)}), bf16[8,8,4096]{2,1,0:T(8,128)(2,1)S(1)}, u32[]{:S(2)}, u32[]{:S(2)}) async-start(bf16[8,8,4096]{2,1,0:T(8,128)(2,1)} %broadcast_in_dim.69), calls=%async_computation.2 | async-start | bytes 1048576 | tf_op jit(solution)/shard_map/all_to_all | solution.py:162
  48.6 0.1 slice.74
  48.7 0.1 copy.59
  48.8 0.1 copy.60
  48.9 0.1 add.110
  49.0 0.2 select_reduce_fusion
  49.2 0.1 eq.50
  49.3 13.4 %all-to-all-done.2 = bf16[8,8,4096]{2,1,0:T(8,128)(2,1)S(1)} async-done(((bf16[8,8,4096]{2,1,0:T(8,128)(2,1)}), bf16[8,8,4096]{2,1,0:T(8,128)(2,1)S(1)}, u32[]{:S(2)}, u32[]{:S(2)}) %all-to-all-start.2) | async-done | bytes 524320 | tf_op jit(solution)/shard_map/all_to_all | solution.py:162
  62.7 15.7 %fusion.37 = (f32[64]{0:T(128)S(1)}, f32[64,4096]{1,0:T(8,128)S(1)}) fusion(f32[4096]{0:T(1024)} %param.21, bf16[4096,4096]{1,0:T(8,128)(2,1)} %param.20, bf16[8,8,4096]{2,1,0:T(8,128)(2,1)S(1)} %all-to-all-done.2), kind=kOutput, calls=%fused_computation.78 | convolution fusion | flops 2148007936 | bytes 35143936 | tf_op jit(solution)/shard_map/rd,vd->rv/dot_general | solution.py:170
  78.4 0.4 exponential_reduce_fusion
  78.9 0.1 reshape.239
  79.0 10.1 %all_to_all.21 = f32[32,1,192]{2,1,0:T(1,128)S(1)} all-to-all(f32[32,1,192]{2,1,0:T(1,128)S(1)} %reshape.239), channel_id=1, replica_groups=mesh['dp'=8,'vocab'=4] {'dp','vocab'}, dimensions={0} | all-to-all | bytes 49152 | tf_op jit(solution)/shard_map/all_to_all | solution.py:182
  89.1 0.5 broadcast.145
  89.6 0.7 reduce.6
  90.3 0.1 reshape.240
  90.5 0.5 fusion.34
  91.1 0.3 fusion.4
  91.4 0.6 broadcast_multiply_fusion
  92.0 14.5 %convolution_convert_fusion = bf16[4096,4096]{1,0:T(8,128)(2,1)} fusion(f32[64,4096]{1,0:T(8,128)S(1)} %get-tuple-element.33, bf16[8,8,4096]{2,1,0:T(8,128)(2,1)S(1)} %all-to-all-done.2, f32[64]{0:T(128)S(1)} %get-tuple-element.20, s32[4096]{0:T(1024)S(1)} %iota_add_fusion, s32[64]{0:T(128)S(1)} %eq.50), kind=kOutput, calls=%fused_computation | convolution fusion | flops 2165833728 | bytes 35144192 | tf_op jit(solution)/shard_map/rv,rd->vd/dot_general | solution.py:190
  (26 shorter events, 0.4 us)
Async XLA Ops:
  0.6 22.7 %copy-start = (bf16[512,1024]{1,0:T(8,128)(2,1)S(1)}, bf16[512,1024]{1,0:T(8,128)(2,1)}, u32[]{:S(2)}) copy-start(bf16[512,1024]{1,0:T(8,128)(2,1)} %param.16) | copy-start | bytes 3145732
  4.6 17.9 %all-to-all-start = ((bf16[32,7,512]{2,1,0:T(8,128)(2,1)}), bf16[32,7,512]{2,1,0:T(8,128)(2,1)S(1)}, u32[]{:S(2)}, u32[]{:S(2)}) async-start(bf16[32,7,512]{2,1,0:T(8,128)(2,1)} %bitcast.5), calls=%async_computation | async-start | bytes 524288 | tf_op jit(solution)/shard_map/all_to_all | solution.py:133
  36.9 1.3 %collective-permute-start = (f32[1,10,1024]{2,1,0:T(8,128)S(1)}, f32[1,10,1024]{2,1,0:T(8,128)S(1)}, u32[]{:S(2)}, u32[]{:S(2)}) collective-permute-start(f32[1,10,1024]{2,1,0:T(8,128)S(1)} %maximum_bitcast_fusion), channel_id=1, source_target_pairs={{0,1},{1,0},{2,3},{3,2},{4,5},{5,4},{6,7},{7,6},{8,9},{9,8},{10,11... | collective-permute-start | bytes 122888 | tf_op jit(solution)/shard_map/ppermute | solution.py:35
  38.2 5.6 %collective-permute-start.1 = (f32[2,10,1024]{2,1,0:T(8,128)S(1)}, f32[2,10,1024]{2,1,0:T(8,128)S(1)}, u32[]{:S(2)}, u32[]{:S(2)}) collective-permute-start(f32[2,10,1024]{2,1,0:T(8,128)S(1)} %maximum_select_fusion.1), channel_id=1, source_target_pairs={{0,2},{1,3},{2,0},{3,1},{4,6},{5,7},{6,4},{7,5},{8,10},{9,11},{10,... | collective-permute-start | bytes 245768 | tf_op jit(solution)/shard_map/ppermute | solution.py:35
  45.0 17.7 %all-to-all-start.2 = ((bf16[8,8,4096]{2,1,0:T(8,128)(2,1)}), bf16[8,8,4096]{2,1,0:T(8,128)(2,1)S(1)}, u32[]{:S(2)}, u32[]{:S(2)}) async-start(bf16[8,8,4096]{2,1,0:T(8,128)(2,1)} %broadcast_in_dim.69), calls=%async_computation.2 | async-start | bytes 1048576 | tf_op jit(solution)/shard_map/all_to_all | solution.py:162

commit v9 on v8

--- a/solution.py
+++ b/solution.py
@@ -153,16 +153,15 @@
     part = jnp.dot(rows_in, dense_weight, preferred_element_type=jnp.float32)
     act = jnp.sum(lax.all_to_all(part.reshape(groups, group_rows, -1), "dp", 0, 0, tiled=True), axis=0)
     act = jax.nn.gelu(act + dense_bias, approximate=False)
-    pieces = _gather(jnp.concatenate([act, norm_gain[None], norm_shift[None]]), "vocab", ways)
-    pieces = pieces.transpose(1, 0, 2).reshape(group_rows + 2, model)
-    act, gain, shift = pieces[:group_rows], pieces[group_rows], pieces[group_rows + 1]
+    devices = groups * ways
+    every_act = lax.all_to_all(
+        jnp.broadcast_to(act[None], (devices,) + act.shape), ("dp", "vocab"), 0, 0, tiled=True
+    )
+    act = every_act.reshape(groups, ways, group_rows, -1).transpose(0, 2, 1, 3).reshape(total_rows, model)
+    affine = _gather(jnp.stack([norm_gain, norm_shift]), "vocab", ways).transpose(1, 0, 2).reshape(2, model)
     mean = jnp.sum(act, axis=1) / model
     var = jnp.sum(act * act, axis=1) / model - mean * mean
-    head_rows = ((act - mean[:, None]) * lax.rsqrt(var + EPS)[:, None] * gain + shift).astype(jnp.bfloat16)
-    head_all = lax.all_to_all(
-        jnp.broadcast_to(head_rows[None], (groups,) + head_rows.shape), "dp", 0, 0, tiled=True
-    ).reshape(total_rows, model)
-    devices = groups * ways
+    head_all = ((act - mean[:, None]) * lax.rsqrt(var + EPS)[:, None] * affine[0] + affine[1]).astype(jnp.bfloat16)
     vocab_rows = embedding.shape[0]
     first_id = (lax.axis_index("dp") * ways + lax.axis_index("vocab")) * vocab_rows
     ids = first_id + jnp.arange(vocab_rows, dtype=jnp.int32)

time: 107 us -> 112 us (1.047)
  waiting for transfers between devices: 29.8 us -> 33 us
    all_to_all x1, waiting for transfers between devices: 13.4 us -> 17 us  [body(): lax.all_to_all(jnp.broadcast_to(act[None], (devices,) + act.shape), ('dp'...]
where the time goes in v9:
time: 112 us; the launch traced here: 111 us
  waiting for transfers between devices  33 us (29%)
  matrix products  32.3 us (29%)
  blocking collectives  22.4 us (20%)
  starting transfers between devices  12.5 us (11%)
  other arithmetic  5.68 us (5%)
  local copies, waits for them, and re-layouts  4.07 us (4%)
  between operations  1.49 us (1%)
    all_to_all x1, waiting for transfers between devices, body(): lax.all_to_all(jnp.broadcast_to(act[None], (devices,) + act.shape), ('dp'...  17 us
    dot_general x1, matrix products, body(): jnp.einsum('rd,vd->rv', head_all, embedding, preferred_element_type=jnp.f...  15.8 us
    dot_general x1, matrix products, body(): jnp.einsum('rv,rd->vd', grad, head_all, preferred_element_type=jnp.float32)  14.5 us
    all_to_all x1, blocking collectives, body(): lax.all_to_all(part.reshape(groups, group_rows, -1), 'dp', 0, 0, tiled=True)  11.7 us
    all_to_all x1, blocking collectives, body(): lax.all_to_all(jnp.broadcast_to(local[None], (devices,) + local.shape), (...  10.7 us
    all_to_all x1, waiting for transfers between devices, body(): lax.all_to_all(jnp.repeat(blocks, ways, axis=0), ('dp', 'vocab'), 0, 0, t...  10.5 us
    all_to_all x1, starting transfers between devices, body(): lax.all_to_all(jnp.repeat(blocks, ways, axis=0), ('dp', 'vocab'), 0, 0, t...  7.33 us
    ppermute x2, waiting for transfers between devices, _allgather(): theirs = lax.ppermute(buf, axis, [(a, a ^ step) for a in range(n)])  5.52 us
  transfers between devices with their start and end apart: 4, of which 4 were waited for; matrix products, arithmetic and copies ran while one was open for 1% of the time, Pallas kernels for 0%

profile of v9, /device:TPU:0, one launch (start us, length us, event | category | flops | bytes accessed | tf_op | source)
XLA Modules:
  0.0 111.4 jit_solution(7527632523157260877)
XLA Ops:
  0.6 0.0 copy-start
  0.6 0.7 shift-right-arithmetic_bitcast_fusion
  2.1 0.2 add_dynamic-update-slice_fusion
  2.2 1.5 %convolution_convert_fusion.1 = bf16[6,4096]{1,0:T(8,128)(2,1)S(1)} fusion(bf16[128,4096]{1,0:T(8,128)(2,1)} %param.12, s32[6]{0:T(128)} %bitcast.80), kind=kOutput, calls=%fused_computation.2 | convolution fusion | flops 6316800 | bytes 1097752 | tf_op jit(solution)/shard_map/dot_general | solution.py:123
  3.9 0.7 broadcast_in_dim.31
  4.6 7.3 %all-to-all-start = ((bf16[32,7,512]{2,1,0:T(8,128)(2,1)}), bf16[32,7,512]{2,1,0:T(8,128)(2,1)S(1)}, u32[]{:S(2)}, u32[]{:S(2)}) async-start(bf16[32,7,512]{2,1,0:T(8,128)(2,1)} %bitcast.5), calls=%async_computation | async-start | bytes 524288 | tf_op jit(solution)/shard_map/all_to_all | solution.py:133
  11.9 0.1 add.100
  12.0 10.5 %all-to-all-done = bf16[32,7,512]{2,1,0:T(8,128)(2,1)S(1)} async-done(((bf16[32,7,512]{2,1,0:T(8,128)(2,1)}), bf16[32,7,512]{2,1,0:T(8,128)(2,1)S(1)}, u32[]{:S(2)}, u32[]{:S(2)}) %all-to-all-start) | async-done | bytes 229408 | tf_op jit(solution)/shard_map/all_to_all | solution.py:133
  22.5 0.1 copy.54
  22.7 0.1 copy.56
  22.8 0.1 copy.55
  22.8 0.1 broadcast_in_dim.32
  22.9 0.1 reshape.263
  23.0 0.1 broadcast_in_dim.33
  23.1 0.1 reshape.264
  23.2 0.1 copy.57
  23.3 0.0 copy-done
  23.3 0.4 fusion
  23.7 11.7 %all_to_all.20 = f32[8,8,1024]{2,1,0:T(8,128)S(1)} all-to-all(f32[8,8,1024]{2,1,0:T(8,128)S(1)} %fusion), channel_id=1, replica_groups=mesh['dp'=8,'vocab'=4] {'dp'}, dimensions={0} | all-to-all | bytes 524288 | tf_op jit(solution)/shard_map/all_to_all | solution.py:154
  35.4 0.8 fusion.12
  36.2 1.1 broadcast_in_dim.34
  37.3 3.0 %all-to-all-start.2 = ((f32[32,8,1024]{2,1,0:T(8,128)}), f32[32,8,1024]{2,1,0:T(8,128)S(1)}, u32[]{:S(2)}, u32[]{:S(2)}) async-start(f32[32,8,1024]{2,1,0:T(8,128)} %broadcast_in_dim.34), calls=%async_computation.2 | async-start | bytes 2097152 | tf_op jit(solution)/shard_map/all_to_all | solution.py:157
  40.3 0.7 maximum_bitcast_fusion
  41.0 0.3 collective-permute-start
  41.3 0.9 collective-permute-done
  42.3 1.8 %collective-permute-start.1 = (f32[2,2,1024]{2,1,0:T(2,128)S(1)}, f32[2,2,1024]{2,1,0:T(2,128)S(1)}, u32[]{:S(2)}, u32[]{:S(2)}) collective-permute-start(f32[2,2,1024]{2,1,0:T(2,128)S(1)} %maximum_select_fusion.1), channel_id=1, source_target_pairs={{0,2},{1,3},{2,0},{3,1},{4,6},{5,7},{6,4},{7,5},{8,10},{9,11},{10,... | collective-permute-start | bytes 49160 | tf_op jit(solution)/shard_map/ppermute | solution.py:35
  44.1 4.6 %collective-permute-done.1 = f32[2,2,1024]{2,1,0:T(2,128)S(1)} collective-permute-done((f32[2,2,1024]{2,1,0:T(2,128)S(1)}, f32[2,2,1024]{2,1,0:T(2,128)S(1)}, u32[]{:S(2)}, u32[]{:S(2)}) %collective-permute-start.1) | collective-permute-done | bytes 16416 | tf_op jit(solution)/shard_map/ppermute | solution.py:35
  48.8 0.1 slice.65
  48.8 0.1 copy.59
  49.0 0.1 copy.60
  49.1 0.1 add.114
  49.2 0.2 select_reduce_fusion
  49.4 0.1 eq.50
  49.4 17.0 %all-to-all-done.2 = f32[32,8,1024]{2,1,0:T(8,128)S(1)} async-done(((f32[32,8,1024]{2,1,0:T(8,128)}), f32[32,8,1024]{2,1,0:T(8,128)S(1)}, u32[]{:S(2)}, u32[]{:S(2)}) %all-to-all-start.2) | async-done | bytes 1048608 | tf_op jit(solution)/shard_map/all_to_all | solution.py:157
  66.5 0.2 fusion.32
  66.7 0.1 div.23
  66.8 0.1 div.25
  66.9 0.0 copy-start.1
  66.9 15.8 %fusion.36 = (f32[64]{0:T(128)S(1)}, f32[64,4096]{1,0:T(8,128)S(1)}) fusion(f32[4096]{0:T(1024)} %param.21, bf16[4096,4096]{1,0:T(8,128)(2,1)} %param.20, f32[64,4096]{1,0:T(8,128)S(1)} %bitcast.56, f32[4096]{0:T(1024)S(1)} %bitcast.63, f32[4096]{0:T(1024)S(1)} %bitcast.61, f32[64]{0:T(128)S(1)} %add_rsqrt_fusion, f32[64]{0:T(128)S(1)} %div.23), kind=kOutput, calls=%fused_computation.77 | convolution fusion | flops 2149318656 | bytes 35701504 | tf_op jit(solution)/shard_map/rd,vd->rv/dot_general | solution.py:169
  82.7 0.4 exponential_reduce_fusion
  83.2 0.1 reshape.271
  83.3 10.7 %all_to_all.21 = f32[32,1,192]{2,1,0:T(1,128)S(1)} all-to-all(f32[32,1,192]{2,1,0:T(1,128)S(1)} %reshape.271), channel_id=1, replica_groups=mesh['dp'=8,'vocab'=4] {'dp','vocab'}, dimensions={0} | all-to-all | bytes 49152 | tf_op jit(solution)/shard_map/all_to_all | solution.py:181
  94.0 0.5 broadcast.256
  94.5 0.7 reduce.6
  95.2 0.1 reshape.272
  95.4 0.5 fusion.33
  96.0 14.5 %convolution_convert_fusion = bf16[4096,4096]{1,0:T(8,128)(2,1)} fusion(f32[64,4096]{1,0:T(8,128)S(1)} %get-tuple-element.30, f32[64]{0:T(128)S(1)} %get-tuple-element.20, s32[4096]{0:T(1024)S(1)} %iota_add_fusion, s32[64]{0:T(128)S(1)} %eq.50, f32[64,4096]{1,0:T(8,128)S(1)} %bitcast.57, f32[4096]{0:T(1024)S(1)} %bitcast.64, f32[4096]{0:T(1024)S(1)} %bitcast.62, ...), kind=kOutput, calls=%fused_computation | convolution fusion | flops 2167144448 | bytes 35701760 | tf_op jit(solution)/shard_map/rv,rd->vd/dot_general | solution.py:189
  110.5 0.3 fusion.4
  110.8 0.6 broadcast_multiply_fusion
  111.4 0.0 copy-done.1
  (27 shorter events, 0.4 us)
Async XLA Ops:
  0.6 22.7 %copy-start = (bf16[512,1024]{1,0:T(8,128)(2,1)S(1)}, bf16[512,1024]{1,0:T(8,128)(2,1)}, u32[]{:S(2)}) copy-start(bf16[512,1024]{1,0:T(8,128)(2,1)} %param.16) | copy-start | bytes 3145732
  4.6 17.9 %all-to-all-start = ((bf16[32,7,512]{2,1,0:T(8,128)(2,1)}), bf16[32,7,512]{2,1,0:T(8,128)(2,1)S(1)}, u32[]{:S(2)}, u32[]{:S(2)}) async-start(bf16[32,7,512]{2,1,0:T(8,128)(2,1)} %bitcast.5), calls=%async_computation | async-start | bytes 524288 | tf_op jit(solution)/shard_map/all_to_all | solution.py:133
  37.3 29.2 %all-to-all-start.2 = ((f32[32,8,1024]{2,1,0:T(8,128)}), f32[32,8,1024]{2,1,0:T(8,128)S(1)}, u32[]{:S(2)}, u32[]{:S(2)}) async-start(f32[32,8,1024]{2,1,0:T(8,128)} %broadcast_in_dim.34), calls=%async_computation.2 | async-start | bytes 2097152 | tf_op jit(solution)/shard_map/all_to_all | solution.py:157
  41.0 1.2 %collective-permute-start = (f32[1,2,1024]{2,1,0:T(2,128)S(1)}, f32[1,2,1024]{2,1,0:T(2,128)S(1)}, u32[]{:S(2)}, u32[]{:S(2)}) collective-permute-start(f32[1,2,1024]{2,1,0:T(2,128)S(1)} %maximum_bitcast_fusion), channel_id=1, source_target_pairs={{0,1},{1,0},{2,3},{3,2},{4,5},{5,4},{6,7},{7,6},{8,9},{9,8},{10,11... | collective-permute-start | bytes 24584 | tf_op jit(solution)/shard_map/ppermute | solution.py:35
  42.3 6.4 %collective-permute-start.1 = (f32[2,2,1024]{2,1,0:T(2,128)S(1)}, f32[2,2,1024]{2,1,0:T(2,128)S(1)}, u32[]{:S(2)}, u32[]{:S(2)}) collective-permute-start(f32[2,2,1024]{2,1,0:T(2,128)S(1)} %maximum_select_fusion.1), channel_id=1, source_target_pairs={{0,2},{1,3},{2,0},{3,1},{4,6},{5,7},{6,4},{7,5},{8,10},{9,11},{10,... | collective-permute-start | bytes 49160 | tf_op jit(solution)/shard_map/ppermute | solution.py:35
  66.9 44.6 %copy-start.1 = (bf16[512,1024]{1,0:T(8,128)(2,1)S(1)}, bf16[512,1024]{1,0:T(8,128)(2,1)}, u32[]{:S(2)}) copy-start(bf16[512,1024]{1,0:T(8,128)(2,1)} %param.16) | copy-start | bytes 3145732

commit v10 on v8

--- a/solution.py
+++ b/solution.py
@@ -159,9 +159,12 @@
     mean = jnp.sum(act, axis=1) / model
     var = jnp.sum(act * act, axis=1) / model - mean * mean
     head_rows = ((act - mean[:, None]) * lax.rsqrt(var + EPS)[:, None] * gain + shift).astype(jnp.bfloat16)
-    head_all = lax.all_to_all(
-        jnp.broadcast_to(head_rows[None], (groups,) + head_rows.shape), "dp", 0, 0, tiled=True
-    ).reshape(total_rows, model)
+    feat = model // ways
+    head_blk = lax.dynamic_slice_in_dim(head_rows, lax.axis_index("vocab") * feat, feat, axis=1)
+    head_cols = lax.all_to_all(
+        jnp.broadcast_to(head_blk[None], (groups,) + head_blk.shape), "dp", 0, 0, tiled=True
+    ).reshape(total_rows, feat)
+    head_all = _gather(head_cols, "vocab", ways, _steps(ways)[::-1]).transpose(1, 0, 2).reshape(total_rows, model)
     devices = groups * ways
     vocab_rows = embedding.shape[0]
     first_id = (lax.axis_index("dp") * ways + lax.axis_index("vocab")) * vocab_rows

time: 107 us -> 105 us (0.981)
  blocking collectives: 21.8 us -> 31.3 us
  waiting for transfers between devices: 29.8 us -> 20.6 us
  starting transfers between devices: 11.9 us -> 9.35 us
    all_to_all x1 -> x0, waiting for transfers between devices: 13.4 us -> none  [body(): lax.all_to_all(jnp.broadcast_to(head_rows[None], (groups,) + head_rows.sh...]
    all_to_all x0 -> x1, blocking collectives: none -> 10.7 us  [body(): lax.all_to_all(jnp.broadcast_to(head_blk[None], (groups,) + head_blk.shap...]
    ppermute x2 -> x4, waiting for transfers between devices: 5.88 us -> 10.1 us  [_allgather(): theirs = lax.ppermute(buf, axis, [(a, a ^ step) for a in range(n)])]
    all_to_all x1 -> x0, starting transfers between devices: 3.57 us -> none  [body(): lax.all_to_all(jnp.broadcast_to(head_rows[None], (groups,) + head_rows.sh...]
    all_to_all x1, blocking collectives: 10.1 us -> 8.95 us  [body(): lax.all_to_all(jnp.broadcast_to(local[None], (devices,) + local.shape), (...]
  transfers between devices with their start and end apart: 4 -> 5, of which waited for: 4 -> 5; matrix products, arithmetic and copies ran while one was open for 1% -> 1% of each run, Pallas kernels for 0% -> 0%
where the time goes in v10:
time: 105 us
  matrix products  32.1 us (31%)
  blocking collectives  31.3 us (30%)
  waiting for transfers between devices  20.6 us (20%)
  starting transfers between devices  9.35 us (9%)
  other arithmetic  6.5 us (6%)
  local copies, waits for them, and re-layouts  3.47 us (3%)
  between operations  1.54 us (1%)
    dot_general x1, matrix products, body(): jnp.einsum('rd,vd->rv', head_all, embedding, preferred_element_type=jnp.f...  15.7 us
    dot_general x1, matrix products, body(): jnp.einsum('rv,rd->vd', grad, head_all, preferred_element_type=jnp.float32)  14.5 us
    all_to_all x1, blocking collectives, body(): lax.all_to_all(part.reshape(groups, group_rows, -1), 'dp', 0, 0, tiled=True)  11.7 us
    all_to_all x1, blocking collectives, body(): lax.all_to_all(jnp.broadcast_to(head_blk[None], (groups,) + head_blk.shap...  10.7 us
    all_to_all x1, waiting for transfers between devices, body(): lax.all_to_all(jnp.repeat(blocks, ways, axis=0), ('dp', 'vocab'), 0, 0, t...  10.5 us
    ppermute x4, waiting for transfers between devices, _allgather(): theirs = lax.ppermute(buf, axis, [(a, a ^ step) for a in range(n)])  10.1 us
    all_to_all x1, blocking collectives, body(): lax.all_to_all(jnp.broadcast_to(local[None], (devices,) + local.shape), (...  8.95 us
    all_to_all x1, starting transfers between devices, body(): lax.all_to_all(jnp.repeat(blocks, ways, axis=0), ('dp', 'vocab'), 0, 0, t...  7.33 us
  transfers between devices with their start and end apart: 5, of which 5 were waited for; matrix products, arithmetic and copies ran while one was open for 1% of the time, Pallas kernels for 0%

profile of v10, /device:TPU:0, one launch (start us, length us, event | category | flops | bytes accessed | tf_op | source)
XLA Modules:
  0.0 104.9 jit_solution(8812589202504714369)
XLA Ops:
  0.6 0.0 copy-start
  0.6 0.7 shift-right-arithmetic_bitcast_fusion
  2.1 0.2 add_dynamic-update-slice_fusion
  2.2 1.5 %convolution_convert_fusion.1 = bf16[6,4096]{1,0:T(8,128)(2,1)S(1)} fusion(bf16[128,4096]{1,0:T(8,128)(2,1)} %param.13, s32[6]{0:T(128)} %bitcast.83), kind=kOutput, calls=%fused_computation.3 | convolution fusion | flops 6316800 | bytes 1097752 | tf_op jit(solution)/shard_map/dot_general | solution.py:123
  3.9 0.7 broadcast_in_dim.37
  4.6 7.3 %all-to-all-start = ((bf16[32,7,512]{2,1,0:T(8,128)(2,1)}), bf16[32,7,512]{2,1,0:T(8,128)(2,1)S(1)}, u32[]{:S(2)}, u32[]{:S(2)}) async-start(bf16[32,7,512]{2,1,0:T(8,128)(2,1)} %bitcast.5), calls=%async_computation | async-start | bytes 524288 | tf_op jit(solution)/shard_map/all_to_all | solution.py:133
  11.9 0.1 add.99
  12.0 10.5 %all-to-all-done = bf16[32,7,512]{2,1,0:T(8,128)(2,1)S(1)} async-done(((bf16[32,7,512]{2,1,0:T(8,128)(2,1)}), bf16[32,7,512]{2,1,0:T(8,128)(2,1)S(1)}, u32[]{:S(2)}, u32[]{:S(2)}) %all-to-all-start) | async-done | bytes 229408 | tf_op jit(solution)/shard_map/all_to_all | solution.py:133
  22.5 0.1 copy.58
  22.7 0.1 copy.60
  22.8 0.1 copy.59
  22.8 0.1 broadcast_in_dim.38
  22.9 0.1 reshape.166
  23.0 0.1 broadcast_in_dim.68
  23.1 0.1 reshape.167
  23.2 0.1 copy.61
  23.3 0.0 copy-done
  23.3 0.4 fusion
  23.7 11.7 %all_to_all.20 = f32[8,8,1024]{2,1,0:T(8,128)S(1)} all-to-all(f32[8,8,1024]{2,1,0:T(8,128)S(1)} %fusion), channel_id=1, replica_groups=mesh['dp'=8,'vocab'=4] {'dp'}, dimensions={0} | all-to-all | bytes 524288 | tf_op jit(solution)/shard_map/all_to_all | solution.py:154
  35.4 0.8 fusion.13
  36.2 0.7 maximum_bitcast_fusion
  36.9 0.1 collective-permute-start
  37.0 1.2 %collective-permute-done = f32[1,10,1024]{2,1,0:T(8,128)S(1)} collective-permute-done((f32[1,10,1024]{2,1,0:T(8,128)S(1)}, f32[1,10,1024]{2,1,0:T(8,128)S(1)}, u32[]{:S(2)}, u32[]{:S(2)}) %collective-permute-start) | collective-permute-done | bytes 40992 | tf_op jit(solution)/shard_map/ppermute | solution.py:35
  38.2 1.0 collective-permute-start.1
  39.2 4.6 %collective-permute-done.1 = f32[2,10,1024]{2,1,0:T(8,128)S(1)} collective-permute-done((f32[2,10,1024]{2,1,0:T(8,128)S(1)}, f32[2,10,1024]{2,1,0:T(8,128)S(1)}, u32[]{:S(2)}, u32[]{:S(2)}) %collective-permute-start.1) | collective-permute-done | bytes 81952 | tf_op jit(solution)/shard_map/ppermute | solution.py:35
  43.9 0.2 slice_reduce_fusion
  44.2 0.1 fusion.17
  44.3 10.7 %all_to_all.21 = bf16[8,8,1024]{2,1,0:T(8,128)(2,1)S(1)} all-to-all(bf16[8,8,1024]{2,1,0:T(8,128)(2,1)S(1)} %broadcast_in_dim.72), channel_id=1, replica_groups=mesh['dp'=8,'vocab'=4] {'dp'}, dimensions={0} | all-to-all | bytes 262144 | tf_op jit(solution)/shard_map/all_to_all | solution.py:164
  55.0 0.9 collective-permute-start.2
  55.9 0.7 pad_clamp_fusion
  56.5 0.1 slice.76
  56.6 0.1 copy.64
  56.7 3.2 %collective-permute-done.2 = bf16[1,64,1024]{2,1,0:T(8,128)(2,1)S(1)} collective-permute-done((bf16[1,64,1024]{2,1,0:T(8,128)(2,1)S(1)}, bf16[1,64,1024]{2,1,0:T(8,128)(2,1)S(1)}, u32[]{:S(2)}, u32[]{:S(2)}) %collective-permute-start.2) | collective-permute-done | bytes 131104 | tf_op jit(solution)/shard_map/ppermute | solution.py:35
  60.0 0.1 collective-permute-start.3
  60.1 0.1 copy.65
  60.2 0.1 add.114
  60.2 0.2 select_reduce_fusion
  60.5 0.1 eq.50
  60.5 1.0 collective-permute-done.3
  61.6 0.1 maximum_select_fusion
  61.6 0.6 gather_fusion
  62.3 15.7 %fusion.39 = (f32[64]{0:T(128)S(1)}, f32[64,4096]{1,0:T(8,128)S(1)}) fusion(f32[4096]{0:T(1024)} %param.22, bf16[64,4096]{1,0:T(8,128)(2,1)S(1)} %bitcast.57, bf16[4096,4096]{1,0:T(8,128)(2,1)} %param.21), kind=kOutput, calls=%fused_computation.84 | convolution fusion | flops 2148007936 | bytes 35143936 | tf_op jit(solution)/shard_map/rd,vd->rv/dot_general | solution.py:173
  78.0 0.4 exponential_reduce_fusion
  78.4 0.1 reshape.181
  78.5 9.0 %all_to_all.22 = f32[32,1,192]{2,1,0:T(1,128)S(1)} all-to-all(f32[32,1,192]{2,1,0:T(1,128)S(1)} %reshape.181), channel_id=1, replica_groups=mesh['dp'=8,'vocab'=4] {'dp','vocab'}, dimensions={0} | all-to-all | bytes 49152 | tf_op jit(solution)/shard_map/all_to_all | solution.py:185
  87.5 0.5 broadcast.122
  88.0 0.7 reduce.6
  88.7 0.1 reshape.182
  88.9 0.5 fusion.36
  89.5 14.5 %convolution_convert_fusion = bf16[4096,4096]{1,0:T(8,128)(2,1)} fusion(bf16[64,4096]{1,0:T(8,128)(2,1)S(1)} %bitcast.58, f32[64,4096]{1,0:T(8,128)S(1)} %get-tuple-element.33, f32[64]{0:T(128)S(1)} %get-tuple-element.20, s32[4096]{0:T(1024)S(1)} %iota_add_fusion, s32[64]{0:T(128)S(1)} %eq.50), kind=kOutput, calls=%fused_computation.1 | convolution fusion | flops 2165833728 | bytes 35144192 | tf_op jit(solution)/shard_map/rv,rd->vd/dot_general | solution.py:193
  103.9 0.3 fusion.4
  104.3 0.6 broadcast_multiply_fusion
  (31 shorter events, 0.5 us)
Async XLA Ops:
  0.6 22.7 %copy-start = (bf16[512,1024]{1,0:T(8,128)(2,1)S(1)}, bf16[512,1024]{1,0:T(8,128)(2,1)}, u32[]{:S(2)}) copy-start(bf16[512,1024]{1,0:T(8,128)(2,1)} %param.17) | copy-start | bytes 3145732
  4.6 17.9 %all-to-all-start = ((bf16[32,7,512]{2,1,0:T(8,128)(2,1)}), bf16[32,7,512]{2,1,0:T(8,128)(2,1)S(1)}, u32[]{:S(2)}, u32[]{:S(2)}) async-start(bf16[32,7,512]{2,1,0:T(8,128)(2,1)} %bitcast.5), calls=%async_computation | async-start | bytes 524288 | tf_op jit(solution)/shard_map/all_to_all | solution.py:133
  36.9 1.3 %collective-permute-start = (f32[1,10,1024]{2,1,0:T(8,128)S(1)}, f32[1,10,1024]{2,1,0:T(8,128)S(1)}, u32[]{:S(2)}, u32[]{:S(2)}) collective-permute-start(f32[1,10,1024]{2,1,0:T(8,128)S(1)} %maximum_bitcast_fusion), channel_id=1, source_target_pairs={{0,1},{1,0},{2,3},{3,2},{4,5},{5,4},{6,7},{7,6},{8,9},{9,8},{10,11... | collective-permute-start | bytes 122888 | tf_op jit(solution)/shard_map/ppermute | solution.py:35
  38.2 5.6 %collective-permute-start.1 = (f32[2,10,1024]{2,1,0:T(8,128)S(1)}, f32[2,10,1024]{2,1,0:T(8,128)S(1)}, u32[]{:S(2)}, u32[]{:S(2)}) collective-permute-start(f32[2,10,1024]{2,1,0:T(8,128)S(1)} %maximum_select_fusion.3), channel_id=1, source_target_pairs={{0,2},{1,3},{2,0},{3,1},{4,6},{5,7},{6,4},{7,5},{8,10},{9,11},{10,... | collective-permute-start | bytes 245768 | tf_op jit(solution)/shard_map/ppermute | solution.py:35
  55.0 5.0 %collective-permute-start.2 = (bf16[1,64,1024]{2,1,0:T(8,128)(2,1)S(1)}, bf16[1,64,1024]{2,1,0:T(8,128)(2,1)S(1)}, u32[]{:S(2)}, u32[]{:S(2)}) collective-permute-start(bf16[1,64,1024]{2,1,0:T(8,128)(2,1)S(1)} %bitcast.63), channel_id=1, source_target_pairs={{0,2},{1,3},{2,0},{3,1},{4,6},{5,7},{6,4},{7,5},{8,10},{9,11},{10,... | collective-permute-start | bytes 393224 | tf_op jit(solution)/shard_map/ppermute | solution.py:35
  60.0 1.6 %collective-permute-start.3 = (bf16[2,64,1024]{2,1,0:T(8,128)(2,1)S(1)}, bf16[2,64,1024]{2,1,0:T(8,128)(2,1)S(1)}, u32[]{:S(2)}, u32[]{:S(2)}) collective-permute-start(bf16[2,64,1024]{2,1,0:T(8,128)(2,1)S(1)} %maximum_select_fusion.2), channel_id=1, source_target_pairs={{0,1},{1,0},{2,3},{3,2},{4,5},{5,4},{6,7},{7,6},{8,9},{9,8},{10,11... | collective-permute-start | bytes 786440 | tf_op jit(solution)/shard_map/ppermute | solution.py:35

commit v11 on v10

--- a/solution.py
+++ b/solution.py
@@ -120,12 +120,14 @@
     in_block = dense_weight.shape[0]
     tokens = hidden.shape[0]
     onehot = (positions[0][:, None] == jnp.arange(tokens, dtype=jnp.int32)[None, :]).astype(hidden.dtype)
-    picked = jnp.dot(onehot, hidden, preferred_element_type=jnp.float32).astype(hidden.dtype)
+    picked = jnp.einsum(
+        "sk,kbd->bsd", onehot, hidden.reshape(tokens, -1, dense_weight.shape[0]), preferred_element_type=jnp.float32
+    ).astype(hidden.dtype)
     meta = jnp.zeros((in_block,), jnp.int32).at[0].set(counts[0])
     meta = lax.dynamic_update_slice(meta, _pieces(targets[0]), (1,))
     blocks = jnp.concatenate(
         [
-            picked.reshape(slots, groups, in_block).transpose(1, 0, 2),
+            picked,
             jnp.broadcast_to(meta.astype(hidden.dtype), (groups, 1, in_block)),
         ],
         axis=1,

time: 105 us -> 105 us (level)
  no operation moved by 1% of the time
where the time goes in v11:
time: 105 us
  matrix products  32.1 us (31%)
  blocking collectives  31.3 us (30%)
  waiting for transfers between devices  20.6 us (20%)
  starting transfers between devices  9.35 us (9%)
  other arithmetic  6.52 us (6%)
  local copies, waits for them, and re-layouts  3.43 us (3%)
  between operations  1.53 us (1%)
    dot_general x1, matrix products, body(): jnp.einsum('rd,vd->rv', head_all, embedding, preferred_element_type=jnp.f...  15.7 us
    dot_general x1, matrix products, body(): jnp.einsum('rv,rd->vd', grad, head_all, preferred_element_type=jnp.float32)  14.5 us
    all_to_all x1, blocking collectives, body(): lax.all_to_all(part.reshape(groups, group_rows, -1), 'dp', 0, 0, tiled=True)  11.7 us
    all_to_all x1, blocking collectives, body(): lax.all_to_all(jnp.broadcast_to(head_blk[None], (groups,) + head_blk.shap...  10.7 us
    all_to_all x1, waiting for transfers between devices, body(): lax.all_to_all(jnp.repeat(blocks, ways, axis=0), ('dp', 'vocab'), 0, 0, t...  10.5 us
    ppermute x4, waiting for transfers between devices, _allgather(): theirs = lax.ppermute(buf, axis, [(a, a ^ step) for a in range(n)])  10.1 us
    all_to_all x1, blocking collectives, body(): lax.all_to_all(jnp.broadcast_to(local[None], (devices,) + local.shape), (...  8.95 us
    all_to_all x1, starting transfers between devices, body(): lax.all_to_all(jnp.repeat(blocks, ways, axis=0), ('dp', 'vocab'), 0, 0, t...  7.33 us
  transfers between devices with their start and end apart: 5, of which 5 were waited for; matrix products, arithmetic and copies ran while one was open for 1% of the time, Pallas kernels for 0%

profile of v11, /device:TPU:0, one launch (start us, length us, event | category | flops | bytes accessed | tf_op | source)
XLA Modules:
  0.0 104.9 jit_solution(2276959895616563100)
XLA Ops:
  0.6 0.0 copy-start
  0.6 0.7 shift-right-arithmetic_bitcast_fusion
  2.1 0.2 add_dynamic-update-slice_fusion
  2.2 1.5 %fusion.1 = bf16[8,6,512]{2,1,0:T(8,128)(2,1)S(1)} fusion(bf16[16,8,8,512]{3,2,1,0:T(8,128)(2,1)} %bitcast.63, s32[6]{0:T(128)} %bitcast.83), kind=kOutput, calls=%fused_computation.8 | convolution fusion | flops 6316800 | bytes 1097752 | tf_op jit(solution)/shard_map/sk,kbd->bsd/dot_general | solution.py:123
  3.8 0.7 broadcast_in_dim.37
  4.5 7.3 %all-to-all-start = ((bf16[32,7,512]{2,1,0:T(8,128)(2,1)}), bf16[32,7,512]{2,1,0:T(8,128)(2,1)S(1)}, u32[]{:S(2)}, u32[]{:S(2)}) async-start(bf16[32,7,512]{2,1,0:T(8,128)(2,1)} %bitcast.6), calls=%async_computation | async-start | bytes 524288 | tf_op jit(solution)/shard_map/all_to_all | solution.py:135
  11.9 0.1 add.99
  12.0 10.5 %all-to-all-done = bf16[32,7,512]{2,1,0:T(8,128)(2,1)S(1)} async-done(((bf16[32,7,512]{2,1,0:T(8,128)(2,1)}), bf16[32,7,512]{2,1,0:T(8,128)(2,1)S(1)}, u32[]{:S(2)}, u32[]{:S(2)}) %all-to-all-start) | async-done | bytes 229408 | tf_op jit(solution)/shard_map/all_to_all | solution.py:135
  22.5 0.1 copy.62
  22.6 0.1 copy.64
  22.7 0.1 copy.63
  22.8 0.1 broadcast_in_dim.38
  22.9 0.1 reshape.166
  23.0 0.1 broadcast_in_dim.68
  23.0 0.1 reshape.167
  23.1 0.1 copy.65
  23.3 0.0 copy-done
  23.3 0.4 fusion
  23.7 11.7 %all_to_all.20 = f32[8,8,1024]{2,1,0:T(8,128)S(1)} all-to-all(f32[8,8,1024]{2,1,0:T(8,128)S(1)} %fusion), channel_id=1, replica_groups=mesh['dp'=8,'vocab'=4] {'dp'}, dimensions={0} | all-to-all | bytes 524288 | tf_op jit(solution)/shard_map/all_to_all | solution.py:156
  35.4 0.8 fusion.16
  36.2 0.7 maximum_bitcast_fusion
  36.9 0.1 collective-permute-start
  37.0 1.2 %collective-permute-done = f32[1,10,1024]{2,1,0:T(8,128)S(1)} collective-permute-done((f32[1,10,1024]{2,1,0:T(8,128)S(1)}, f32[1,10,1024]{2,1,0:T(8,128)S(1)}, u32[]{:S(2)}, u32[]{:S(2)}) %collective-permute-start) | collective-permute-done | bytes 40992 | tf_op jit(solution)/shard_map/ppermute | solution.py:35
  38.2 1.0 collective-permute-start.1
  39.2 4.6 %collective-permute-done.1 = f32[2,10,1024]{2,1,0:T(8,128)S(1)} collective-permute-done((f32[2,10,1024]{2,1,0:T(8,128)S(1)}, f32[2,10,1024]{2,1,0:T(8,128)S(1)}, u32[]{:S(2)}, u32[]{:S(2)}) %collective-permute-start.1) | collective-permute-done | bytes 81952 | tf_op jit(solution)/shard_map/ppermute | solution.py:35
  43.9 0.2 slice_reduce_fusion
  44.1 0.1 fusion.20
  44.2 10.7 %all_to_all.21 = bf16[8,8,1024]{2,1,0:T(8,128)(2,1)S(1)} all-to-all(bf16[8,8,1024]{2,1,0:T(8,128)(2,1)S(1)} %broadcast_in_dim.72), channel_id=1, replica_groups=mesh['dp'=8,'vocab'=4] {'dp'}, dimensions={0} | all-to-all | bytes 262144 | tf_op jit(solution)/shard_map/all_to_all | solution.py:166
  54.9 0.9 collective-permute-start.2
  55.8 0.7 pad_clamp_fusion
  56.5 0.1 slice.76
  56.6 0.1 copy.68
  56.7 3.2 %collective-permute-done.2 = bf16[1,64,1024]{2,1,0:T(8,128)(2,1)S(1)} collective-permute-done((bf16[1,64,1024]{2,1,0:T(8,128)(2,1)S(1)}, bf16[1,64,1024]{2,1,0:T(8,128)(2,1)S(1)}, u32[]{:S(2)}, u32[]{:S(2)}) %collective-permute-start.2) | collective-permute-done | bytes 131104 | tf_op jit(solution)/shard_map/ppermute | solution.py:35
  59.9 0.1 collective-permute-start.3
  60.0 0.1 copy.69
  60.1 0.1 add.114
  60.2 0.2 select_reduce_fusion
  60.4 0.1 eq.50
  60.5 1.0 collective-permute-done.3
  61.5 0.1 maximum_select_fusion
  61.6 0.6 gather_fusion
  62.3 15.7 %fusion.44 = (f32[64]{0:T(128)S(1)}, f32[64,4096]{1,0:T(8,128)S(1)}) fusion(f32[4096]{0:T(1024)} %param.22, bf16[64,4096]{1,0:T(8,128)(2,1)S(1)} %bitcast.58, bf16[4096,4096]{1,0:T(8,128)(2,1)} %param.21), kind=kOutput, calls=%fused_computation.87 | convolution fusion | flops 2148007936 | bytes 35143936 | tf_op jit(solution)/shard_map/rd,vd->rv/dot_general | solution.py:175
  77.9 0.4 exponential_reduce_fusion
  78.4 0.1 reshape.182
  78.5 9.0 %all_to_all.22 = f32[32,1,192]{2,1,0:T(1,128)S(1)} all-to-all(f32[32,1,192]{2,1,0:T(1,128)S(1)} %reshape.182), channel_id=1, replica_groups=mesh['dp'=8,'vocab'=4] {'dp','vocab'}, dimensions={0} | all-to-all | bytes 49152 | tf_op jit(solution)/shard_map/all_to_all | solution.py:187
  87.5 0.5 broadcast.122
  88.0 0.7 reduce.6
  88.7 0.1 reshape.183
  88.9 0.5 fusion.41
  89.4 14.5 %convolution_convert_fusion = bf16[4096,4096]{1,0:T(8,128)(2,1)} fusion(bf16[64,4096]{1,0:T(8,128)(2,1)S(1)} %bitcast.59, f32[64,4096]{1,0:T(8,128)S(1)} %get-tuple-element.33, f32[64]{0:T(128)S(1)} %get-tuple-element.20, s32[4096]{0:T(1024)S(1)} %iota_add_fusion, s32[64]{0:T(128)S(1)} %eq.50), kind=kOutput, calls=%fused_computation.1 | convolution fusion | flops 2165833728 | bytes 35144192 | tf_op jit(solution)/shard_map/rv,rd->vd/dot_general | solution.py:195
  103.9 0.3 fusion.7
  104.3 0.6 broadcast_multiply_fusion
  (29 shorter events, 0.5 us)
Async XLA Ops:
  0.6 22.6 %copy-start = (bf16[512,1024]{1,0:T(8,128)(2,1)S(1)}, bf16[512,1024]{1,0:T(8,128)(2,1)}, u32[]{:S(2)}) copy-start(bf16[512,1024]{1,0:T(8,128)(2,1)} %param.17) | copy-start | bytes 3145732
  4.5 17.9 %all-to-all-start = ((bf16[32,7,512]{2,1,0:T(8,128)(2,1)}), bf16[32,7,512]{2,1,0:T(8,128)(2,1)S(1)}, u32[]{:S(2)}, u32[]{:S(2)}) async-start(bf16[32,7,512]{2,1,0:T(8,128)(2,1)} %bitcast.6), calls=%async_computation | async-start | bytes 524288 | tf_op jit(solution)/shard_map/all_to_all | solution.py:135
  36.9 1.3 %collective-permute-start = (f32[1,10,1024]{2,1,0:T(8,128)S(1)}, f32[1,10,1024]{2,1,0:T(8,128)S(1)}, u32[]{:S(2)}, u32[]{:S(2)}) collective-permute-start(f32[1,10,1024]{2,1,0:T(8,128)S(1)} %maximum_bitcast_fusion), channel_id=1, source_target_pairs={{0,1},{1,0},{2,3},{3,2},{4,5},{5,4},{6,7},{7,6},{8,9},{9,8},{10,11... | collective-permute-start | bytes 122888 | tf_op jit(solution)/shard_map/ppermute | solution.py:35
  38.2 5.6 %collective-permute-start.1 = (f32[2,10,1024]{2,1,0:T(8,128)S(1)}, f32[2,10,1024]{2,1,0:T(8,128)S(1)}, u32[]{:S(2)}, u32[]{:S(2)}) collective-permute-start(f32[2,10,1024]{2,1,0:T(8,128)S(1)} %maximum_select_fusion.3), channel_id=1, source_target_pairs={{0,2},{1,3},{2,0},{3,1},{4,6},{5,7},{6,4},{7,5},{8,10},{9,11},{10,... | collective-permute-start | bytes 245768 | tf_op jit(solution)/shard_map/ppermute | solution.py:35
  54.9 5.0 %collective-permute-start.2 = (bf16[1,64,1024]{2,1,0:T(8,128)(2,1)S(1)}, bf16[1,64,1024]{2,1,0:T(8,128)(2,1)S(1)}, u32[]{:S(2)}, u32[]{:S(2)}) collective-permute-start(bf16[1,64,1024]{2,1,0:T(8,128)(2,1)S(1)} %bitcast.65), channel_id=1, source_target_pairs={{0,2},{1,3},{2,0},{3,1},{4,6},{5,7},{6,4},{7,5},{8,10},{9,11},{10,... | collective-permute-start | bytes 393224 | tf_op jit(solution)/shard_map/ppermute | solution.py:35
  59.9 1.6 %collective-permute-start.3 = (bf16[2,64,1024]{2,1,0:T(8,128)(2,1)S(1)}, bf16[2,64,1024]{2,1,0:T(8,128)(2,1)S(1)}, u32[]{:S(2)}, u32[]{:S(2)}) collective-permute-start(bf16[2,64,1024]{2,1,0:T(8,128)(2,1)S(1)} %maximum_select_fusion.2), channel_id=1, source_target_pairs={{0,1},{1,0},{2,3},{3,2},{4,5},{5,4},{6,7},{7,6},{8,9},{9,8},{10,11... | collective-permute-start | bytes 786440 | tf_op jit(solution)/shard_map/ppermute | solution.py:35
